TPU v7x, 32 devices: a whole 2x2x4 slice. The times are simulated.
32 devices in a mesh: parts: 2 (over x), gy: 16 (over z, y, core).
Axes of the slice: x: 2, y: 2, z: 4, core: 2. Of those that a mesh axis runs over, the one named last changes fastest.
Arguments:
- measured: bfloat16 [8, 32, 256, 128], P(None, None, ('parts', 'gy')), parts along dimension 2, may hold values from 0.19921875 to 8
- start: float32 [32, 256, 128], P(None, ('parts', 'gy')), parts along dimension 1, may hold values from 0.5 to 4
- psf: float32 [8, 15, 7, 7], replicated, may hold values from 0.05 to 1
- background: float32 [8], replicated, may hold values from 0.2 to 2
Outputs:
- estimate: float32 [32, 256, 128], P(None, ('parts', 'gy')), parts along dimension 1
There are 2 independent parts, one for each index of `parts`. A program takes and returns all parts, laid end to end along the dimension named above; an argument that names none is the same for every part. Nothing has to cross between parts.
All inputs are finite; a program needn't handle non-finite values.
Results may differ from a plain program's by a relative error of at most 0.0003.
Values may be sent and summed in bfloat16 or wider, within the bound.
No kernel may reach another device: no remote copies, remote signals or barrier semaphores. Data moves between devices by JAX's collectives and lax.ppermute only.
A program may use at most 128 MiB of HBM per device.

v0:
```python
import jax
import jax.numpy as jnp
from jax import lax
from jax.experimental import pallas as pl
from jax.experimental.pallas import tpu as pltpu
from jax.sharding import PartitionSpec as P


def halos(x, axis, width):
    peers = lax.axis_size(axis)
    up = [(i, i + 1) for i in range(peers - 1)]
    down = [(j, i) for i, j in up]
    length = x.shape[-1]
    last = x[..., length - width:]
    first = x[..., :width]
    before = lax.ppermute(last, axis, up)
    after = lax.ppermute(first, axis, down)
    return before, after


def build_weights(psf, planes):
    kernel = psf / jnp.sum(psf, axis=(1, 2, 3), keepdims=True)
    rounded_kernel = lax.optimization_barrier(kernel.astype(jnp.bfloat16)).astype(jnp.float32)
    views, depth, reach_y, reach_x = psf.shape
    q = jnp.arange(planes, dtype=jnp.int32)
    tap = jnp.arange(depth, dtype=jnp.int32)
    onehot = (q[None, :, None] - q[None, None, :] + depth // 2 == tap[:, None, None]).astype(jnp.float32)
    blur_w = jnp.einsum("vabc,aqp->bvqcp", rounded_kernel, onehot, precision=lax.Precision.HIGHEST)
    blur_w = blur_w.reshape(reach_y, views * planes, reach_x * planes).astype(jnp.bfloat16)
    corr_w = jnp.einsum("vabc,apq->bcqvp", rounded_kernel, onehot, precision=lax.Precision.HIGHEST)
    corr_w = corr_w.reshape(reach_y, reach_x * planes, views * planes).astype(jnp.bfloat16)
    return blur_w, corr_w


def lane_shift(x, shift, cols):
    n = x.shape[-1]
    rolled = pltpu.roll(x, shift % n, x.ndim - 1) if shift % n else x
    col = lax.broadcasted_iota(jnp.int32, x.shape, x.ndim - 1) % cols
    keep = (col - shift >= 0) & (col - shift < cols)
    return jnp.where(keep, rolled, jnp.zeros_like(rolled))


def blur_kernel(start_ref, lo_ref, hi_ref, w_ref, meas_ref, bg_ref,
                ratio_ref, rlo_ref, rhi_ref, ext_ref, xs_ref, *, cols, reach_y, reach_x, half):
    planes = start_ref.shape[0]
    n_in = ext_ref.shape[1]
    n_out = start_ref.shape[1]
    hw = half * cols
    ext_ref[:, :hw] = lo_ref[...].astype(jnp.float32)
    ext_ref[:, hw:hw + n_out] = start_ref[...].astype(jnp.bfloat16).astype(jnp.float32)
    ext_ref[:, hw + n_out:] = hi_ref[...].astype(jnp.float32)
    ext = ext_ref[...]
    for c in range(reach_x):
        xs_ref[c * planes:(c + 1) * planes, :] = lane_shift(ext, c - reach_x // 2, cols).astype(jnp.bfloat16)
    acc = None
    for b in range(reach_y):
        off = (2 * half - b) * cols
        part = jnp.dot(w_ref[b], xs_ref[:, off:off + n_out], preferred_element_type=jnp.float32)
        acc = part if acc is None else acc + part
    ratio = (meas_ref[...].astype(jnp.float32) / (acc + bg_ref[...])).astype(jnp.bfloat16)
    ratio_ref[...] = ratio
    rlo_ref[...] = ratio[:, :hw]
    rhi_ref[...] = ratio[:, n_out - hw:]


def corr_kernel(ratio_ref, lo_ref, hi_ref, w_ref, est_ref, out_ref, ext_ref, *, cols, reach_y, reach_x, half, views):
    planes = est_ref.shape[0]
    n_out = est_ref.shape[1]
    hw = half * cols
    ext_ref[:, :hw] = lo_ref[...]
    ext_ref[:, hw:hw + n_out] = ratio_ref[...]
    ext_ref[:, hw + n_out:] = hi_ref[...]
    acc = None
    for b in range(reach_y):
        off = b * cols
        part = jnp.dot(w_ref[b], ext_ref[:, off:off + n_out], preferred_element_type=jnp.float32)
        acc = part if acc is None else acc + part
    total = None
    for c in range(reach_x):
        piece = lane_shift(acc[c * planes:(c + 1) * planes], reach_x // 2 - c, cols)
        total = piece if total is None else total + piece
    out_ref[...] = est_ref[...] * total / views


def local(measured, start, psf, background):
    planes, rows, cols = start.shape
    views = measured.shape[0]
    reach_y, reach_x = psf.shape[2], psf.shape[3]
    half = reach_y // 2
    blur_w, corr_w = build_weights(psf, planes)
    n_out = rows * cols
    hw = half * cols
    vmem = pl.BlockSpec(memory_space=pltpu.VMEM)

    start2 = start.reshape(planes, n_out)
    rounded = start2.astype(jnp.bfloat16)
    lo, hi = halos(rounded, "gy", hw)
    meas2 = measured.reshape(views * planes, n_out)
    bg = jnp.broadcast_to(jnp.repeat(background, planes)[:, None], (views * planes, cols))
    bg = jnp.tile(bg, (1, rows))

    ratio, rlo, rhi = pl.pallas_call(
        lambda *refs: blur_kernel(*refs, cols=cols, reach_y=reach_y, reach_x=reach_x, half=half),
        out_shape=(
            jax.ShapeDtypeStruct((views * planes, n_out), jnp.bfloat16),
            jax.ShapeDtypeStruct((views * planes, hw), jnp.bfloat16),
            jax.ShapeDtypeStruct((views * planes, hw), jnp.bfloat16),
        ),
        in_specs=[vmem] * 6,
        out_specs=(vmem, vmem, vmem),
        scratch_shapes=[
            pltpu.VMEM((planes, n_out + 2 * hw), jnp.float32),
            pltpu.VMEM((reach_x * planes, n_out + 2 * hw), jnp.bfloat16),
        ],
    )(start2, lo, hi, blur_w, meas2, bg)

    before = lax.ppermute(rhi, "gy", [(i, i + 1) for i in range(lax.axis_size("gy") - 1)])
    after = lax.ppermute(rlo, "gy", [(i + 1, i) for i in range(lax.axis_size("gy") - 1)])

    est = pl.pallas_call(
        lambda *refs: corr_kernel(*refs, cols=cols, reach_y=reach_y, reach_x=reach_x, half=half, views=views),
        out_shape=jax.ShapeDtypeStruct((planes, n_out), jnp.float32),
        in_specs=[vmem] * 5,
        out_specs=vmem,
        scratch_shapes=[pltpu.VMEM((views * planes, n_out + 2 * hw), jnp.bfloat16)],
    )(ratio, before, after, corr_w, start2)
    return est.reshape(planes, rows, cols)


def solution(mesh):
    in_specs = (P(None, None, ("parts", "gy"), None), P(None, ("parts", "gy"), None), P(), P())
    out_specs = P(None, ("parts", "gy"), None)
    return jax.shard_map(local, mesh=mesh, in_specs=in_specs, out_specs=out_specs, check_vma=False)
```

profile of v0, /device:TPU:10, one launch (start us, length us, event | category | flops | bytes accessed | tf_op | source)
XLA Modules:
  0.0 51.2 jit_solution(15538953433562824367)
XLA Ops:
  0.0 1.0 %copy.22 = bf16[4,8,8,128]{3,1,2,0:T(8,128)(2,1)S(1)} copy(f32[4,8,8,128]{3,2,1,0:T(8,128)} %bitcast.32) | data formatting | bytes 196608
  1.0 1.9 %collective-permute-start = (bf16[32,384]{1,0:T(8,128)(2,1)S(1)}, bf16[32,384]{1,0:T(8,128)(2,1)S(1)}, u32[]{:S(2)}, u32[]{:S(2)}) collective-permute-start(bf16[32,384]{1,0:T(8,128)(2,1)S(1)} %get-tuple-element.12), channel_id=1, source_target_pairs={{0,1},{1,2},{2,3},{3,4},{4,5},{5,6},{6,7},{7,8},{8,9},{9,10},{10,1... | collective-permute-start | bytes 73736 | tf_op jit(solution)/shard_map/ppermute | solution.py:16
  3.0 4.5 %collective-permute-start.1 = (bf16[32,384]{1,0:T(8,128)(2,1)S(1)}, bf16[32,384]{1,0:T(8,128)(2,1)S(1)}, u32[]{:S(2)}, u32[]{:S(2)}) collective-permute-start(bf16[32,384]{1,0:T(8,128)(2,1)S(1)} %get-tuple-element.11), channel_id=1, source_target_pairs={{1,0},{2,1},{3,2},{4,3},{5,4},{6,5},{7,6},{8,7},{9,8},{10,9},{11,1... | collective-permute-start | bytes 73736 | tf_op jit(solution)/shard_map/ppermute | solution.py:17
  7.5 1.1 %reduce_sum.9 = f32[8]{0:T(128)S(1)} reduce(f32[8,15,7,7]{1,0,3,2:T(8,128)} %param.6, f32[]{:T(128)} %constant.1.clone.1), dimensions={1,2,3}, to_apply=%region_0.0 | reduce | flops 5872 | bytes 23556 | tf_op jit(solution)/shard_map/reduce_sum | solution.py:22
  8.6 1.0 %divide_convert_fusion = bf16[8,15,7,7]{1,0,3,2:T(8,128)(2,1)S(1)} fusion(f32[8,15,7,7]{1,0,3,2:T(8,128)} %param.6, f32[8]{0:T(128)S(1)} %reduce_sum.9), kind=kLoop, calls=%fused_computation.4 | loop fusion | flops 11760 | bytes 35312 | tf_op jit(solution)/shard_map/convert_element_type | solution.py:23
  9.6 1.0 %convolution_convert_fusion = bf16[32,32,8,7,7]{1,2,4,3,0:T(8,128)(2,1)S(1)} fusion(s32[32,32]{1,0:T(8,128)S(1)} %subtract_add_fusion, bf16[8,15,7,7]{1,0,3,2:T(8,128)(2,1)S(1)} %divide_convert_fusion), kind=kOutput, calls=%fused_computation | convolution fusion | flops 12459008 | bytes 818672 | tf_op jit(solution)/shard_map/vabc,aqp->bvqcp/dot_general | solution.py:28
  10.6 0.0 copy-done
  10.6 0.7 %copy.21 = f32[4,8,8,128]{3,1,2,0:T(8,128)} copy(f32[4,8,8,128]{3,2,1,0:T(8,128)S(1)} %bitcast.33) | data formatting | bytes 262144
  11.3 2.8 %copy.11 = bf16[7,8,32,7,32]{4,3,2,1,0:T(8,128)(2,1)} copy(bf16[7,8,32,7,32]{4,1,3,0,2:T(8,128)(2,1)S(1)} %bitcast.26) | data formatting | bytes 1605632 | tf_op jit(solution)/shard_map/convert_element_type | solution.py:29
  14.1 0.0 copy-start.4
  14.1 5.5 %reshape.39.refs_3_ = bf16[7,256,224]{2,1,0:T(8,128)(2,1)} reshape(bf16[7,8,32,7,32]{4,3,2,1,0:T(8,128)(2,1)} %copy.11) | data formatting | bytes 1605632 | tf_op jit(solution)/shard_map/convert_element_type | solution.py:29
  19.6 0.0 copy-done.4
  19.6 0.1 broadcast_in_dim.4
  19.7 0.1 broadcast_in_dim.5
  19.8 2.0 %copy.20 = bf16[32,8,8,128]{3,1,2,0:T(8,128)(2,1)} copy(bf16[32,8,8,128]{3,2,1,0:T(8,128)(2,1)} %bitcast.31) | data formatting | bytes 1048576
  21.7 0.0 collective-permute-done.refs_1_
  21.7 0.0 copy-start.2
  21.7 0.0 collective-permute-done.1.refs_2_
  21.7 0.0 copy-start.3
  21.7 1.1 %tile.2.refs_5_ = f32[256,1024]{1,0:T(8,128)} broadcast(f32[256]{0:T(256)S(1)} %broadcast_in_dim.5), dimensions={0} | broadcast | bytes 1049600 | tf_op jit(solution)/shard_map/tile | solution.py:100
  22.8 0.0 copy-done.2
  22.8 0.0 copy-done.3
  22.8 4.0 %shard_map.46 = (bf16[256,1024]{1,0:T(8,128)(2,1)}, bf16[256,384]{1,0:T(8,128)(2,1)}, bf16[256,384]{1,0:T(8,128)(2,1)}) custom-call(f32[32,1024]{1,0:T(8,128)} %bitcast.29, bf16[32,384]{1,0:T(8,128)(2,1)} %copy-done.2, bf16[32,384]{1,0:T(8,128)(2,1)} %copy-done.3, bf16[7,256,224]{2,1,0:T(8,128)(2,1)} %reshape.39.refs_3_, bf16[256,1024]{1,0:T(8,128)(2,1)} %bitcast.28, ...), custom_call_target="tpu_custom_call" | custom-call | tf_op jit(solution)/shard_map/pallas_call | solution.py:102
  26.8 1.9 %collective-permute-start.2 = (bf16[256,384]{1,0:T(8,128)(2,1)}, bf16[256,384]{1,0:T(8,128)(2,1)S(1)}, u32[]{:S(2)}, u32[]{:S(2)}) collective-permute-start(bf16[256,384]{1,0:T(8,128)(2,1)} %get-tuple-element.9), channel_id=1, source_target_pairs={{0,1},{1,2},{2,3},{3,4},{4,5},{5,6},{6,7},{7,8},{8,9},{9,10},{10,1... | collective-permute-start | bytes 589832 | tf_op jit(solution)/shard_map/ppermute | solution.py:117
  28.7 4.5 %collective-permute-start.3 = (bf16[256,384]{1,0:T(8,128)(2,1)}, bf16[256,384]{1,0:T(8,128)(2,1)}, u32[]{:S(2)}, u32[]{:S(2)}) collective-permute-start(bf16[256,384]{1,0:T(8,128)(2,1)} %get-tuple-element.10), channel_id=1, source_target_pairs={{1,0},{2,1},{3,2},{4,3},{5,4},{6,5},{7,6},{8,7},{9,8},{10,9},{11,1... | collective-permute-start | bytes 589832 | tf_op jit(solution)/shard_map/ppermute | solution.py:118
  33.3 7.5 %copy.9 = bf16[7,7,32,8,32]{4,3,2,1,0:T(8,128)(2,1)} copy(bf16[7,7,32,8,32]{2,3,1,0,4:T(8,128)(2,1)S(1)} %bitcast.27) | data formatting | bytes 1605632 | tf_op jit(solution)/shard_map/convert_element_type | solution.py:31
  40.8 4.9 %convert_element_type.26.refs_3_ = bf16[7,224,256]{2,1,0:T(8,128)(2,1)} reshape(bf16[7,7,32,8,32]{4,3,2,1,0:T(8,128)(2,1)} %copy.9) | data formatting | bytes 1605632 | tf_op jit(solution)/shard_map/convert_element_type | solution.py:31
  45.6 0.0 collective-permute-done.2.refs_1_
  45.6 0.0 collective-permute-done.3.refs_2_
  45.6 0.7 %copy-done.1 = bf16[256,384]{1,0:T(8,128)(2,1)} copy-done((bf16[256,384]{1,0:T(8,128)(2,1)}, bf16[256,384]{1,0:T(8,128)(2,1)S(1)}, u32[]{:S(2)}) %copy-start.1) | copy-done | bytes 196632
  46.3 3.3 %shard_map.47 = f32[32,1024]{1,0:T(8,128)} custom-call(bf16[256,1024]{1,0:T(8,128)(2,1)} %get-tuple-element.8.refs_0_, bf16[256,384]{1,0:T(8,128)(2,1)} %copy-done.1, bf16[256,384]{1,0:T(8,128)(2,1)} %collective-permute-done.3.refs_2_, bf16[7,224,256]{2,1,0:T(8,128)(2,1)} %convert_element_type.26.refs_3_, f32[32,1024]{1,0:T(8,128)} %bitcast.30), custom_call_target="tpu_custom_call" | custom-call | tf_op jit(solution)/shard_map/pallas_call | solution.py:120
  49.6 1.6 %copy.15 = f32[4,8,8,128]{3,2,1,0:T(8,128)} copy(f32[4,8,8,128]{3,1,2,0:T(8,128)} %bitcast.34) | data formatting | bytes 262144
  (4 shorter events, 0.0 us)
Async XLA Ops:
  0.0 10.6 %copy-start = (f32[32,8,128]{2,1,0:T(8,128)S(1)}, f32[32,8,128]{2,1,0:T(8,128)}, u32[]{:S(2)}) copy-start(f32[32,8,128]{2,1,0:T(8,128)} %param.5) | copy-start | bytes 393220
  1.0 20.7 %collective-permute-start = (bf16[32,384]{1,0:T(8,128)(2,1)S(1)}, bf16[32,384]{1,0:T(8,128)(2,1)S(1)}, u32[]{:S(2)}, u32[]{:S(2)}) collective-permute-start(bf16[32,384]{1,0:T(8,128)(2,1)S(1)} %get-tuple-element.12), channel_id=1, source_target_pairs={{0,1},{1,2},{2,3},{3,4},{4,5},{5,6},{6,7},{7,8},{8,9},{9,10},{10,1... | collective-permute-start | bytes 73736 | tf_op jit(solution)/shard_map/ppermute | solution.py:16
  3.0 18.8 %collective-permute-start.1 = (bf16[32,384]{1,0:T(8,128)(2,1)S(1)}, bf16[32,384]{1,0:T(8,128)(2,1)S(1)}, u32[]{:S(2)}, u32[]{:S(2)}) collective-permute-start(bf16[32,384]{1,0:T(8,128)(2,1)S(1)} %get-tuple-element.11), channel_id=1, source_target_pairs={{1,0},{2,1},{3,2},{4,3},{5,4},{6,5},{7,6},{8,7},{9,8},{10,9},{11,1... | collective-permute-start | bytes 73736 | tf_op jit(solution)/shard_map/ppermute | solution.py:17
  14.1 5.5 %copy-start.4 = (f32[8]{0:T(128)S(1)}, f32[8]{0:T(128)}, u32[]{:S(2)}) copy-start(f32[8]{0:T(128)} %param.7) | copy-start | bytes 100
  21.7 1.1 %copy-start.2 = (bf16[32,384]{1,0:T(8,128)(2,1)}, bf16[32,384]{1,0:T(8,128)(2,1)S(1)}, u32[]{:S(2)}) copy-start(bf16[32,384]{1,0:T(8,128)(2,1)S(1)} %collective-permute-done.refs_1_) | copy-start | bytes 73732
  21.7 1.1 %copy-start.3 = (bf16[32,384]{1,0:T(8,128)(2,1)}, bf16[32,384]{1,0:T(8,128)(2,1)S(1)}, u32[]{:S(2)}) copy-start(bf16[32,384]{1,0:T(8,128)(2,1)S(1)} %collective-permute-done.1.refs_2_) | copy-start | bytes 73732
  26.8 18.8 %collective-permute-start.2 = (bf16[256,384]{1,0:T(8,128)(2,1)}, bf16[256,384]{1,0:T(8,128)(2,1)S(1)}, u32[]{:S(2)}, u32[]{:S(2)}) collective-permute-start(bf16[256,384]{1,0:T(8,128)(2,1)} %get-tuple-element.9), channel_id=1, source_target_pairs={{0,1},{1,2},{2,3},{3,4},{4,5},{5,6},{6,7},{7,8},{8,9},{9,10},{10,1... | collective-permute-start | bytes 589832 | tf_op jit(solution)/shard_map/ppermute | solution.py:117
  28.7 16.9 %collective-permute-start.3 = (bf16[256,384]{1,0:T(8,128)(2,1)}, bf16[256,384]{1,0:T(8,128)(2,1)}, u32[]{:S(2)}, u32[]{:S(2)}) collective-permute-start(bf16[256,384]{1,0:T(8,128)(2,1)} %get-tuple-element.10), channel_id=1, source_target_pairs={{1,0},{2,1},{3,2},{4,3},{5,4},{6,5},{7,6},{8,7},{9,8},{10,9},{11,1... | collective-permute-start | bytes 589832 | tf_op jit(solution)/shard_map/ppermute | solution.py:118
  45.6 0.7 %copy-start.1 = (bf16[256,384]{1,0:T(8,128)(2,1)}, bf16[256,384]{1,0:T(8,128)(2,1)S(1)}, u32[]{:S(2)}) copy-start(bf16[256,384]{1,0:T(8,128)(2,1)S(1)} %collective-permute-done.2.refs_1_) | copy-start | bytes 589828
where the time goes:
time: 51.8 us; the launch traced here: 51.2 us
  local copies, waits for them, and re-layouts  27.8 us (54%)
  starting transfers between devices  12.9 us (25%)
  Pallas kernels  7.26 us (14%)
  other arithmetic  2.12 us (4%)
  matrix products  0.98 us (2%)
    convert_element_type x2, local copies, waits for them, and re-layouts, build_weights(): corr_w.reshape(reach_y, reach_x * planes, views * planes)  12.4 us
    convert_element_type x2, local copies, waits for them, and re-layouts, build_weights(): blur_w.reshape(reach_y, views * planes, reach_x * planes)  8.29 us
    unnamed x14, local copies, waits for them, and re-layouts  5.91 us
    ppermute x1, starting transfers between devices, local(): lax.ppermute(rlo, 'gy', [(i + 1, i) for i in range(lax.axis_size('gy') -...  4.54 us
    ppermute x1, starting transfers between devices, halos(): after = lax.ppermute(first, axis, down)  4.54 us
    pallas_call x1, Pallas kernels, local(): pl.pallas_call(lambda *refs: blur_kernel(*refs, cols=cols, reach_y=reach_...  3.96 us
    pallas_call x1, Pallas kernels, local(): pl.pallas_call(lambda *refs: corr_kernel(*refs, cols=cols, reach_y=reach_...  3.3 us
    ppermute x1, starting transfers between devices, halos(): before = lax.ppermute(last, axis, up)  1.92 us
  transfers between devices with their start and end apart: 4, of which 0 were waited for; matrix products, arithmetic and copies ran while one was open for 52% of the time, Pallas kernels for 0%

commit v1 on v0

v1 whole, which is shorter than its diff:
```python
import jax
import jax.numpy as jnp
from jax import lax
from jax.experimental import pallas as pl
from jax.experimental.pallas import tpu as pltpu
from jax.sharding import PartitionSpec as P


def halos(x, axis, width):
    peers = lax.axis_size(axis)
    up = [(i, i + 1) for i in range(peers - 1)]
    down = [(j, i) for i, j in up]
    length = x.shape[-1]
    last = x[..., length - width:]
    first = x[..., :width]
    before = lax.ppermute(last, axis, up)
    after = lax.ppermute(first, axis, down)
    return before, after


def build_bases(psf, planes, lanes, corr_lanes):
    kernel = psf / jnp.sum(psf, axis=(1, 2, 3), keepdims=True)
    views, depth, reach_y, reach_x = psf.shape
    half_z = depth // 2
    lane = jnp.arange(lanes, dtype=jnp.int32)
    tap = jnp.arange(depth, dtype=jnp.int32)
    col = jnp.arange(reach_x, dtype=jnp.int32)
    at = (col[None, :, None] * planes + half_z - tap[:, None, None]) % lanes
    onehot = (lane[None, None, :] == at).astype(jnp.float32)
    blur = jnp.einsum("vabc,acl->bvl", kernel, onehot, precision=lax.Precision.HIGHEST)
    view = jnp.arange(views, dtype=jnp.int32)
    at = (view[:, None, None] * planes + tap[None, :, None] - half_z) % corr_lanes
    onehot = (jnp.arange(corr_lanes, dtype=jnp.int32)[None, None, :] == at).astype(jnp.float32)
    corr = jnp.einsum("vabc,val->bcl", kernel, onehot, precision=lax.Precision.HIGHEST)
    return blur.astype(jnp.bfloat16), corr.astype(jnp.bfloat16)


def toeplitz_block(row, planes, half_z, width):
    lanes = row.shape[-1]
    blk = jnp.broadcast_to(row, (planes, lanes))
    blk = pltpu.roll(blk, 0, 1, stride=1, stride_axis=0)
    q = lax.broadcasted_iota(jnp.int32, (planes, lanes), 0)
    l = lax.broadcasted_iota(jnp.int32, (planes, lanes), 1)
    d = l % planes - q
    keep = (d <= half_z) & (d >= -half_z) & (l < width)
    return jnp.where(keep, blk, 0.0).astype(jnp.bfloat16)


def lane_shift(x, shift, cols):
    n = x.shape[-1]
    rolled = pltpu.roll(x, shift % n, x.ndim - 1) if shift % n else x
    col = lax.broadcasted_iota(jnp.int32, x.shape, x.ndim - 1) % cols
    keep = (col - shift >= 0) & (col - shift < cols)
    return jnp.where(keep, rolled, jnp.zeros_like(rolled))


def blur_kernel(start_ref, lo_ref, hi_ref, base_ref, meas_ref, bg_ref,
                ratio_ref, rlo_ref, rhi_ref, ext_ref, xs_ref, w_ref, *, cols, reach_y, reach_x, half, half_z):
    planes = start_ref.shape[0]
    n_out = start_ref.shape[1]
    views = base_ref.shape[1]
    hw = half * cols
    width = reach_x * planes
    for b in range(reach_y):
        for v in range(views):
            row = base_ref[b, v:v + 1, :].astype(jnp.float32)
            w_ref[b, v * planes:(v + 1) * planes, :] = toeplitz_block(row, planes, half_z, width)
    xs_ref[width:, :] = jnp.zeros((xs_ref.shape[0] - width, xs_ref.shape[1]), jnp.bfloat16)
    ext_ref[:, :hw] = lo_ref[...].astype(jnp.float32)
    ext_ref[:, hw:hw + n_out] = start_ref[...].astype(jnp.bfloat16).astype(jnp.float32)
    ext_ref[:, hw + n_out:] = hi_ref[...].astype(jnp.float32)
    ext = ext_ref[...]
    for c in range(reach_x):
        xs_ref[c * planes:(c + 1) * planes, :] = lane_shift(ext, c - reach_x // 2, cols).astype(jnp.bfloat16)
    acc = None
    for b in range(reach_y):
        off = (2 * half - b) * cols
        part = jnp.dot(w_ref[b], xs_ref[:, off:off + n_out], preferred_element_type=jnp.float32)
        acc = part if acc is None else acc + part
    for v in range(views):
        rows = slice(v * planes, (v + 1) * planes)
        ratio = (meas_ref[rows, :].astype(jnp.float32) / (acc[rows] + bg_ref[v])).astype(jnp.bfloat16)
        ratio_ref[rows, :] = ratio
        rlo_ref[rows, :] = ratio[:, :hw]
        rhi_ref[rows, :] = ratio[:, n_out - hw:]


def corr_kernel(ratio_ref, lo_ref, hi_ref, base_ref, est_ref, out_ref, ext_ref, w_ref, *,
                cols, reach_y, reach_x, half, half_z, views):
    planes = est_ref.shape[0]
    n_out = est_ref.shape[1]
    hw = half * cols
    lanes = base_ref.shape[2]
    for b in range(reach_y):
        for c in range(reach_x):
            row = base_ref[b, c:c + 1, :].astype(jnp.float32)
            w_ref[b, c * planes:(c + 1) * planes, :] = toeplitz_block(row, planes, half_z, lanes)
    ext_ref[:, :hw] = lo_ref[...]
    ext_ref[:, hw:hw + n_out] = ratio_ref[...]
    ext_ref[:, hw + n_out:] = hi_ref[...]
    acc = None
    for b in range(reach_y):
        off = b * cols
        part = jnp.dot(w_ref[b], ext_ref[:, off:off + n_out], preferred_element_type=jnp.float32)
        acc = part if acc is None else acc + part
    total = None
    for c in range(reach_x):
        piece = lane_shift(acc[c * planes:(c + 1) * planes], reach_x // 2 - c, cols)
        total = piece if total is None else total + piece
    out_ref[...] = est_ref[...] * total / views


def local(measured, start, psf, background):
    planes, rows, cols = start.shape
    views = measured.shape[0]
    reach_y, reach_x = psf.shape[2], psf.shape[3]
    half = reach_y // 2
    half_z = psf.shape[1] // 2
    lanes = -(-(reach_x * planes + half_z) // 128) * 128
    blur_b, corr_b = build_bases(psf, planes, lanes, views * planes)
    n_out = rows * cols
    hw = half * cols
    vmem = pl.BlockSpec(memory_space=pltpu.VMEM)

    start2 = start.reshape(planes, n_out)
    rounded = start2.astype(jnp.bfloat16)
    lo, hi = halos(rounded, "gy", hw)
    meas2 = measured.reshape(views * planes, n_out)
    smem = pl.BlockSpec(memory_space=pltpu.SMEM)

    ratio, rlo, rhi = pl.pallas_call(
        lambda *refs: blur_kernel(*refs, cols=cols, reach_y=reach_y, reach_x=reach_x, half=half, half_z=half_z),
        out_shape=(
            jax.ShapeDtypeStruct((views * planes, n_out), jnp.bfloat16),
            jax.ShapeDtypeStruct((views * planes, hw), jnp.bfloat16),
            jax.ShapeDtypeStruct((views * planes, hw), jnp.bfloat16),
        ),
        in_specs=[vmem] * 5 + [smem],
        out_specs=(vmem, vmem, vmem),
        scratch_shapes=[
            pltpu.VMEM((planes, n_out + 2 * hw), jnp.float32),
            pltpu.VMEM((lanes, n_out + 2 * hw), jnp.bfloat16),
            pltpu.VMEM((reach_y, views * planes, lanes), jnp.bfloat16),
        ],
    )(start2, lo, hi, blur_b, meas2, background)

    before = lax.ppermute(rhi, "gy", [(i, i + 1) for i in range(lax.axis_size("gy") - 1)])
    after = lax.ppermute(rlo, "gy", [(i + 1, i) for i in range(lax.axis_size("gy") - 1)])

    est = pl.pallas_call(
        lambda *refs: corr_kernel(*refs, cols=cols, reach_y=reach_y, reach_x=reach_x, half=half, half_z=half_z,
                                  views=views),
        out_shape=jax.ShapeDtypeStruct((planes, n_out), jnp.float32),
        in_specs=[vmem] * 5,
        out_specs=vmem,
        scratch_shapes=[
            pltpu.VMEM((views * planes, n_out + 2 * hw), jnp.bfloat16),
            pltpu.VMEM((reach_y, reach_x * planes, views * planes), jnp.bfloat16),
        ],
    )(ratio, before, after, corr_b, start2)
    return est.reshape(planes, rows, cols)


def solution(mesh):
    in_specs = (P(None, None, ("parts", "gy"), None), P(None, ("parts", "gy"), None), P(), P())
    out_specs = P(None, ("parts", "gy"), None)
    return jax.shard_map(local, mesh=mesh, in_specs=in_specs, out_specs=out_specs, check_vma=False)
```

time: 51.8 us -> 31.2 us (0.60)
  the two profiles are of different devices: /device:TPU:10 before, /device:TPU:5 now
where the time goes in v1:
time: 31.2 us; the launch traced here: 31 us
  starting transfers between devices  11.4 us (37%)
  Pallas kernels  6.49 us (21%)
  local copies, waits for them, and re-layouts  5.42 us (17%)
  waiting for transfers between devices  5.08 us (16%)
  matrix products  2.04 us (7%)
  other arithmetic  0.42 us (1%)
    unnamed x18, local copies, waits for them, and re-layouts  5.41 us
    ppermute x1, waiting for transfers between devices, local(): lax.ppermute(rlo, 'gy', [(i + 1, i) for i in range(lax.axis_size('gy') -...  5.07 us
    ppermute x1, starting transfers between devices, halos(): before = lax.ppermute(last, axis, up)  3.88 us
    pallas_call x1, Pallas kernels, local(): pl.pallas_call(lambda *refs: blur_kernel(*refs, cols=cols, reach_y=reach_...  3.39 us
    pallas_call x1, Pallas kernels, local(): pl.pallas_call(lambda *refs: corr_kernel(*refs, cols=cols, reach_y=reach_...  3.1 us
    ppermute x1, starting transfers between devices, local(): lax.ppermute(rhi, 'gy', [(i, i + 1) for i in range(lax.axis_size('gy') -...  3.05 us
    ppermute x1, starting transfers between devices, halos(): after = lax.ppermute(first, axis, down)  2.58 us
    ppermute x1, starting transfers between devices, local(): lax.ppermute(rlo, 'gy', [(i + 1, i) for i in range(lax.axis_size('gy') -...  1.92 us
  transfers between devices with their start and end apart: 4, of which 1 were waited for; matrix products, arithmetic and copies ran while one was open for 13% of the time, Pallas kernels for 0%

profile of v1, /device:TPU:5, one launch (start us, length us, event | category | flops | bytes accessed | tf_op | source)
XLA Modules:
  0.0 31.0 jit_solution(10614837949844139988)
XLA Ops:
  0.0 0.0 copy-start
  0.0 1.0 %copy.19 = bf16[4,8,8,128]{3,1,2,0:T(8,128)(2,1)S(1)} copy(f32[4,8,8,128]{3,2,1,0:T(8,128)} %bitcast.40) | data formatting | bytes 196608
  1.0 2.6 %collective-permute-start.1 = (bf16[32,384]{1,0:T(8,128)(2,1)S(1)}, bf16[32,384]{1,0:T(8,128)(2,1)S(1)}, u32[]{:S(2)}, u32[]{:S(2)}) collective-permute-start(bf16[32,384]{1,0:T(8,128)(2,1)S(1)} %get-tuple-element.11), channel_id=1, source_target_pairs={{1,0},{2,1},{3,2},{4,3},{5,4},{6,5},{7,6},{8,7},{9,8},{10,9},{11,1... | collective-permute-start | bytes 73736 | tf_op jit(solution)/shard_map/ppermute | solution.py:17
  3.6 3.9 %collective-permute-start = (bf16[32,384]{1,0:T(8,128)(2,1)S(1)}, bf16[32,384]{1,0:T(8,128)(2,1)S(1)}, u32[]{:S(2)}, u32[]{:S(2)}) collective-permute-start(bf16[32,384]{1,0:T(8,128)(2,1)S(1)} %get-tuple-element.12), channel_id=1, source_target_pairs={{0,1},{1,2},{2,3},{3,4},{4,5},{5,6},{6,7},{7,8},{8,9},{9,10},{10,1... | collective-permute-start | bytes 73736 | tf_op jit(solution)/shard_map/ppermute | solution.py:16
  7.5 0.1 add_select_fusion.1
  7.6 0.0 copy-done
  7.6 0.0 copy-start.1
  7.6 0.2 reduce_sum.9
  7.7 0.1 broadcast_divide_fusion
  7.8 0.0 copy-start.2
  7.9 0.9 %fusion.2.refs_3_ = bf16[7,8,256]{2,1,0:T(8,128)(2,1)} fusion(f32[8,15,7,7]{1,0,3,2:T(8,128)S(1)} %broadcast_divide_fusion, s32[15,7]{0,1:T(8,128)S(1)} %add_select_fusion.1), kind=kOutput, calls=%fused_computation.4 | convolution fusion | flops 18104576 | bytes 52612 | tf_op jit(solution)/shard_map/vabc,acl->bvl/dot_general | solution.py:30
  8.8 0.1 add_select_fusion
  8.9 0.0 copy-done.2
  8.9 0.7 %copy.18 = f32[4,8,8,128]{3,1,2,0:T(8,128)} copy(f32[4,8,8,128]{3,2,1,0:T(8,128)S(1)} %bitcast.41) | data formatting | bytes 262144
  9.6 0.0 copy-done.1
  9.6 0.9 %copy.17 = bf16[32,8,8,128]{3,1,2,0:T(8,128)(2,1)} copy(bf16[32,8,8,128]{3,2,1,0:T(8,128)(2,1)S(1)} %bitcast.39) | data formatting | bytes 1048576
  10.4 0.0 collective-permute-done.1.refs_2_
  10.4 0.0 copy-start.5
  10.4 0.0 collective-permute-done.refs_1_
  10.4 0.0 copy-start.6
  10.5 0.6 %copy-done.5 = bf16[32,384]{1,0:T(8,128)(2,1)} copy-done((bf16[32,384]{1,0:T(8,128)(2,1)}, bf16[32,384]{1,0:T(8,128)(2,1)S(1)}, u32[]{:S(2)}) %copy-start.5) | copy-done | bytes 24600
  11.1 0.0 copy-done.6
  11.1 3.4 %shard_map.46 = (bf16[256,1024]{1,0:T(8,128)(2,1)}, bf16[256,384]{1,0:T(8,128)(2,1)}, bf16[256,384]{1,0:T(8,128)(2,1)}) custom-call(f32[32,1024]{1,0:T(8,128)} %bitcast.36, bf16[32,384]{1,0:T(8,128)(2,1)} %copy-done.6, bf16[32,384]{1,0:T(8,128)(2,1)} %copy-done.5, bf16[7,8,256]{2,1,0:T(8,128)(2,1)} %fusion.2.refs_3_, bf16[256,1024]{1,0:T(8,128)(2,1)} %bitcast.35, ...), custom_call_target="tpu_custom_call" | custom-call | tf_op jit(solution)/shard_map/pallas_call | solution.py:131
  14.4 3.1 %collective-permute-start.2 = (bf16[256,384]{1,0:T(8,128)(2,1)}, bf16[256,384]{1,0:T(8,128)(2,1)S(1)}, u32[]{:S(2)}, u32[]{:S(2)}) collective-permute-start(bf16[256,384]{1,0:T(8,128)(2,1)} %get-tuple-element.9), channel_id=1, source_target_pairs={{0,1},{1,2},{2,3},{3,4},{4,5},{5,6},{6,7},{7,8},{8,9},{9,10},{10,1... | collective-permute-start | bytes 589832 | tf_op jit(solution)/shard_map/ppermute | solution.py:147
  17.5 1.9 %collective-permute-start.3 = (bf16[256,384]{1,0:T(8,128)(2,1)}, bf16[256,384]{1,0:T(8,128)(2,1)S(1)}, u32[]{:S(2)}, u32[]{:S(2)}) collective-permute-start(bf16[256,384]{1,0:T(8,128)(2,1)} %get-tuple-element.10), channel_id=1, source_target_pairs={{1,0},{2,1},{3,2},{4,3},{5,4},{6,5},{7,6},{8,7},{9,8},{10,9},{11,1... | collective-permute-start | bytes 589832 | tf_op jit(solution)/shard_map/ppermute | solution.py:148
  19.4 1.1 %fusion.1.refs_3_ = bf16[7,7,256]{2,1,0:T(8,128)(2,1)} fusion(f32[8,15,7,7]{1,0,3,2:T(8,128)S(1)} %broadcast_divide_fusion, s32[8,15]{1,0:T(8,128)S(1)} %add_select_fusion), kind=kOutput, calls=%fused_computation.3 | convolution fusion | flops 18106624 | bytes 49088 | tf_op jit(solution)/shard_map/vabc,val->bcl/dot_general | solution.py:34
  20.5 0.0 collective-permute-done.2.refs_1_
  20.5 5.1 %collective-permute-done.3.refs_2_ = bf16[256,384]{1,0:T(8,128)(2,1)S(1)} collective-permute-done((bf16[256,384]{1,0:T(8,128)(2,1)}, bf16[256,384]{1,0:T(8,128)(2,1)S(1)}, u32[]{:S(2)}, u32[]{:S(2)}) %collective-permute-start.3) | collective-permute-done | bytes 196640 | tf_op jit(solution)/shard_map/ppermute | solution.py:148
  25.6 0.0 copy-done.3
  25.6 0.7 %copy-done.4 = bf16[256,384]{1,0:T(8,128)(2,1)} copy-done((bf16[256,384]{1,0:T(8,128)(2,1)}, bf16[256,384]{1,0:T(8,128)(2,1)S(1)}, u32[]{:S(2)}) %copy-start.4) | copy-done | bytes 196632
  26.3 3.1 %shard_map.47 = f32[32,1024]{1,0:T(8,128)} custom-call(bf16[256,1024]{1,0:T(8,128)(2,1)} %get-tuple-element.8.refs_0_, bf16[256,384]{1,0:T(8,128)(2,1)} %copy-done.3, bf16[256,384]{1,0:T(8,128)(2,1)} %copy-done.4, bf16[7,7,256]{2,1,0:T(8,128)(2,1)} %fusion.1.refs_3_, f32[32,1024]{1,0:T(8,128)} %bitcast.37), custom_call_target="tpu_custom_call" | custom-call | tf_op jit(solution)/shard_map/pallas_call | solution.py:150
  29.4 1.6 %copy.10 = f32[4,8,8,128]{3,2,1,0:T(8,128)} copy(f32[4,8,8,128]{3,1,2,0:T(8,128)} %bitcast.38) | data formatting | bytes 262144
  (5 shorter events, 0.0 us)
Async XLA Ops:
  0.0 7.6 %copy-start = (f32[8,15,7,7]{1,0,3,2:T(8,128)S(1)}, f32[8,15,7,7]{1,0,3,2:T(8,128)}, u32[]{:S(2)}) copy-start(f32[8,15,7,7]{1,0,3,2:T(8,128)} %param.6) | copy-start | bytes 70564
  1.0 9.4 %collective-permute-start.1 = (bf16[32,384]{1,0:T(8,128)(2,1)S(1)}, bf16[32,384]{1,0:T(8,128)(2,1)S(1)}, u32[]{:S(2)}, u32[]{:S(2)}) collective-permute-start(bf16[32,384]{1,0:T(8,128)(2,1)S(1)} %get-tuple-element.11), channel_id=1, source_target_pairs={{1,0},{2,1},{3,2},{4,3},{5,4},{6,5},{7,6},{8,7},{9,8},{10,9},{11,1... | collective-permute-start | bytes 73736 | tf_op jit(solution)/shard_map/ppermute | solution.py:17
  3.6 6.9 %collective-permute-start = (bf16[32,384]{1,0:T(8,128)(2,1)S(1)}, bf16[32,384]{1,0:T(8,128)(2,1)S(1)}, u32[]{:S(2)}, u32[]{:S(2)}) collective-permute-start(bf16[32,384]{1,0:T(8,128)(2,1)S(1)} %get-tuple-element.12), channel_id=1, source_target_pairs={{0,1},{1,2},{2,3},{3,4},{4,5},{5,6},{6,7},{7,8},{8,9},{9,10},{10,1... | collective-permute-start | bytes 73736 | tf_op jit(solution)/shard_map/ppermute | solution.py:16
  7.6 2.0 %copy-start.1 = (bf16[8,32,8,128]{3,2,1,0:T(8,128)(2,1)S(1)}, bf16[8,32,8,128]{3,2,1,0:T(8,128)(2,1)}, u32[]{:S(2)}) copy-start(bf16[8,32,8,128]{3,2,1,0:T(8,128)(2,1)} %param.4) | copy-start | bytes 1572868
  7.8 1.0 %copy-start.2 = (f32[32,8,128]{2,1,0:T(8,128)S(1)}, f32[32,8,128]{2,1,0:T(8,128)}, u32[]{:S(2)}) copy-start(f32[32,8,128]{2,1,0:T(8,128)} %param.5) | copy-start | bytes 393220
  10.4 0.6 %copy-start.5 = (bf16[32,384]{1,0:T(8,128)(2,1)}, bf16[32,384]{1,0:T(8,128)(2,1)S(1)}, u32[]{:S(2)}) copy-start(bf16[32,384]{1,0:T(8,128)(2,1)S(1)} %collective-permute-done.1.refs_2_) | copy-start | bytes 73732
  10.4 0.6 %copy-start.6 = (bf16[32,384]{1,0:T(8,128)(2,1)}, bf16[32,384]{1,0:T(8,128)(2,1)S(1)}, u32[]{:S(2)}) copy-start(bf16[32,384]{1,0:T(8,128)(2,1)S(1)} %collective-permute-done.refs_1_) | copy-start | bytes 73732
  14.4 6.1 %collective-permute-start.2 = (bf16[256,384]{1,0:T(8,128)(2,1)}, bf16[256,384]{1,0:T(8,128)(2,1)S(1)}, u32[]{:S(2)}, u32[]{:S(2)}) collective-permute-start(bf16[256,384]{1,0:T(8,128)(2,1)} %get-tuple-element.9), channel_id=1, source_target_pairs={{0,1},{1,2},{2,3},{3,4},{4,5},{5,6},{6,7},{7,8},{8,9},{9,10},{10,1... | collective-permute-start | bytes 589832 | tf_op jit(solution)/shard_map/ppermute | solution.py:147
  17.5 8.1 %collective-permute-start.3 = (bf16[256,384]{1,0:T(8,128)(2,1)}, bf16[256,384]{1,0:T(8,128)(2,1)S(1)}, u32[]{:S(2)}, u32[]{:S(2)}) collective-permute-start(bf16[256,384]{1,0:T(8,128)(2,1)} %get-tuple-element.10), channel_id=1, source_target_pairs={{1,0},{2,1},{3,2},{4,3},{5,4},{6,5},{7,6},{8,7},{9,8},{10,9},{11,1... | collective-permute-start | bytes 589832 | tf_op jit(solution)/shard_map/ppermute | solution.py:148
  20.5 5.1 %copy-start.3 = (bf16[256,384]{1,0:T(8,128)(2,1)}, bf16[256,384]{1,0:T(8,128)(2,1)S(1)}, u32[]{:S(2)}) copy-start(bf16[256,384]{1,0:T(8,128)(2,1)S(1)} %collective-permute-done.2.refs_1_) | copy-start | bytes 589828
  25.6 0.7 %copy-start.4 = (bf16[256,384]{1,0:T(8,128)(2,1)}, bf16[256,384]{1,0:T(8,128)(2,1)S(1)}, u32[]{:S(2)}) copy-start(bf16[256,384]{1,0:T(8,128)(2,1)S(1)} %collective-permute-done.3.refs_2_) | copy-start | bytes 589828

commit v2 on v1

v2 whole, which is shorter than its diff:
```python
import jax
import jax.numpy as jnp
from jax import lax
from jax.experimental import pallas as pl
from jax.experimental.pallas import tpu as pltpu
from jax.sharding import PartitionSpec as P


def build_bases(psf, planes, lanes, corr_lanes):
    kernel = psf / jnp.sum(psf, axis=(1, 2, 3), keepdims=True)
    views, depth, reach_y, reach_x = psf.shape
    half_z = depth // 2
    lane = jnp.arange(lanes, dtype=jnp.int32)
    tap = jnp.arange(depth, dtype=jnp.int32)
    col = jnp.arange(reach_x, dtype=jnp.int32)
    at = (col[None, :, None] * planes + half_z - tap[:, None, None]) % lanes
    onehot = (lane[None, None, :] == at).astype(jnp.float32)
    blur = jnp.einsum("vabc,acl->bvl", kernel, onehot, precision=lax.Precision.HIGHEST)
    view = jnp.arange(views, dtype=jnp.int32)
    at = (view[:, None, None] * planes + tap[None, :, None] - half_z) % corr_lanes
    onehot = (jnp.arange(corr_lanes, dtype=jnp.int32)[None, None, :] == at).astype(jnp.float32)
    corr = jnp.einsum("vabc,val->bcl", kernel, onehot, precision=lax.Precision.HIGHEST)
    return blur.astype(jnp.bfloat16), corr.astype(jnp.bfloat16)


def toeplitz_block(row, planes, half_z, width):
    lanes = row.shape[-1]
    blk = jnp.broadcast_to(row, (planes, lanes))
    blk = pltpu.roll(blk, 0, 1, stride=1, stride_axis=0)
    q = lax.broadcasted_iota(jnp.int32, (planes, lanes), 0)
    l = lax.broadcasted_iota(jnp.int32, (planes, lanes), 1)
    d = l % planes - q
    keep = (d <= half_z) & (d >= -half_z) & (l < width)
    return jnp.where(keep, blk, 0.0).astype(jnp.bfloat16)


def lane_shift(x, shift, cols):
    n = x.shape[-1]
    rolled = pltpu.roll(x, shift % n, x.ndim - 1) if shift % n else x
    col = lax.broadcasted_iota(jnp.int32, x.shape, x.ndim - 1) % cols
    keep = (col - shift >= 0) & (col - shift < cols)
    return jnp.where(keep, rolled, jnp.zeros_like(rolled))


def rl_kernel(start_ref, before_ref, after_ref, bbase_ref, cbase_ref, meas_ref, bg_ref, out_ref,
              ext_ref, xs_ref, wb_ref, wc_ref, mext_ref, rext_ref, *, cols, reach_y, reach_x, half, half_z):
    planes = start_ref.shape[0]
    n_out = start_ref.shape[1]
    views = bbase_ref.shape[1]
    hw = half * cols
    n_mid = n_out + 2 * hw
    width = reach_x * planes
    for b in range(reach_y):
        for v in range(views):
            row = bbase_ref[b, v:v + 1, :].astype(jnp.float32)
            wb_ref[b, v * planes:(v + 1) * planes, :] = toeplitz_block(row, planes, half_z, width)
        for c in range(reach_x):
            row = cbase_ref[b, c:c + 1, :].astype(jnp.float32)
            wc_ref[b, c * planes:(c + 1) * planes, :] = toeplitz_block(row, planes, half_z, views * planes)
    ext_ref[:, :hw] = before_ref[:planes, :].astype(jnp.float32)
    ext_ref[:, hw:2 * hw] = before_ref[planes:2 * planes, :].astype(jnp.float32)
    ext_ref[:, 2 * hw:2 * hw + n_out] = start_ref[...].astype(jnp.bfloat16).astype(jnp.float32)
    ext_ref[:, 2 * hw + n_out:3 * hw + n_out] = after_ref[:planes, :].astype(jnp.float32)
    ext_ref[:, 3 * hw + n_out:] = after_ref[planes:2 * planes, :].astype(jnp.float32)
    mext_ref[:, :hw] = before_ref[2 * planes:, :]
    mext_ref[:, hw:hw + n_out] = meas_ref[...]
    mext_ref[:, hw + n_out:] = after_ref[2 * planes:, :]
    xs_ref[width:, :] = jnp.zeros((xs_ref.shape[0] - width, xs_ref.shape[1]), jnp.bfloat16)
    ext = ext_ref[...]
    for c in range(reach_x):
        xs_ref[c * planes:(c + 1) * planes, :] = lane_shift(ext, c - reach_x // 2, cols).astype(jnp.bfloat16)
    acc = None
    for b in range(reach_y):
        off = (2 * half - b) * cols
        part = jnp.dot(wb_ref[b], xs_ref[:, off:off + n_mid], preferred_element_type=jnp.float32)
        acc = part if acc is None else acc + part
    for v in range(views):
        rows = slice(v * planes, (v + 1) * planes)
        rext_ref[rows, :] = (mext_ref[rows, :].astype(jnp.float32) / (acc[rows] + bg_ref[v])).astype(jnp.bfloat16)
    acc = None
    for b in range(reach_y):
        off = b * cols
        part = jnp.dot(wc_ref[b], rext_ref[:, off:off + n_out], preferred_element_type=jnp.float32)
        acc = part if acc is None else acc + part
    total = None
    for c in range(reach_x):
        piece = lane_shift(acc[c * planes:(c + 1) * planes], reach_x // 2 - c, cols)
        total = piece if total is None else total + piece
    out_ref[...] = start_ref[...] * total / views


def local(measured, start, psf, background):
    planes, rows, cols = start.shape
    views = measured.shape[0]
    reach_y, reach_x = psf.shape[2], psf.shape[3]
    half = reach_y // 2
    half_z = psf.shape[1] // 2
    assert rows >= 2 * half
    lanes = -(-(reach_x * planes + half_z) // 128) * 128
    blur_b, corr_b = build_bases(psf, planes, lanes, views * planes)
    n_out = rows * cols
    hw = half * cols
    vmem = pl.BlockSpec(memory_space=pltpu.VMEM)
    smem = pl.BlockSpec(memory_space=pltpu.SMEM)

    start2 = start.reshape(planes, n_out)
    rounded = start2.astype(jnp.bfloat16)
    meas2 = measured.reshape(views * planes, n_out)
    last = jnp.concatenate(
        [rounded[:, n_out - 2 * hw:n_out - hw], rounded[:, n_out - hw:], meas2[:, n_out - hw:]], axis=0)
    first = jnp.concatenate([rounded[:, :hw], rounded[:, hw:2 * hw], meas2[:, :hw]], axis=0)
    peers = lax.axis_size("gy")
    before = lax.ppermute(last, "gy", [(i, i + 1) for i in range(peers - 1)])
    after = lax.ppermute(first, "gy", [(i + 1, i) for i in range(peers - 1)])

    n_mid = n_out + 2 * hw
    est = pl.pallas_call(
        lambda *refs: rl_kernel(*refs, cols=cols, reach_y=reach_y, reach_x=reach_x, half=half, half_z=half_z),
        out_shape=jax.ShapeDtypeStruct((planes, n_out), jnp.float32),
        in_specs=[vmem] * 6 + [smem],
        out_specs=vmem,
        scratch_shapes=[
            pltpu.VMEM((planes, n_out + 4 * hw), jnp.float32),
            pltpu.VMEM((lanes, n_out + 4 * hw), jnp.bfloat16),
            pltpu.VMEM((reach_y, views * planes, lanes), jnp.bfloat16),
            pltpu.VMEM((reach_y, reach_x * planes, views * planes), jnp.bfloat16),
            pltpu.VMEM((views * planes, n_mid), jnp.bfloat16),
            pltpu.VMEM((views * planes, n_mid), jnp.bfloat16),
        ],
    )(start2, before, after, blur_b, corr_b, meas2, background)
    return est.reshape(planes, rows, cols)


def solution(mesh):
    in_specs = (P(None, None, ("parts", "gy"), None), P(None, ("parts", "gy"), None), P(), P())
    out_specs = P(None, ("parts", "gy"), None)
    return jax.shard_map(local, mesh=mesh, in_specs=in_specs, out_specs=out_specs, check_vma=False)
```

time: 31.2 us -> 23.3 us (0.75)
  the two profiles are of different devices: /device:TPU:5 before, /device:TPU:10 now
where the time goes in v2:
time: 23.3 us; the launch traced here: 23.1 us
  Pallas kernels  6.55 us (28%)
  local copies, waits for them, and re-layouts  5.78 us (25%)
  starting transfers between devices  4.79 us (21%)
  waiting for transfers between devices  3.28 us (14%)
  matrix products  2.05 us (9%)
  other arithmetic  0.48 us (2%)
    pallas_call x1, Pallas kernels, local(): pl.pallas_call(lambda *refs: rl_kernel(*refs, cols=cols, reach_y=reach_y,...  6.55 us
    unnamed x14, local copies, waits for them, and re-layouts  5.73 us
    ppermute x1, waiting for transfers between devices, local(): before = lax.ppermute(last, 'gy', [(i, i + 1) for i in range(peers - 1)])  3.28 us
    ppermute x1, starting transfers between devices, local(): after = lax.ppermute(first, 'gy', [(i + 1, i) for i in range(peers - 1)])  2.74 us
    ppermute x1, starting transfers between devices, local(): before = lax.ppermute(last, 'gy', [(i, i + 1) for i in range(peers - 1)])  2.05 us
    dot_general x1, matrix products, build_bases(): jnp.einsum('vabc,val->bcl', kernel, onehot, precision=lax.Precision.HIGHEST)  1.1 us
    dot_general x1, matrix products, build_bases(): jnp.einsum('vabc,acl->bvl', kernel, onehot, precision=lax.Precision.HIGHEST)  0.95 us
  transfers between devices with their start and end apart: 2, of which 1 were waited for; matrix products, arithmetic and copies ran while one was open for 14% of the time, Pallas kernels for 0%

profile of v2, /device:TPU:10, one launch (start us, length us, event | category | flops | bytes accessed | tf_op | source)
XLA Modules:
  0.0 23.1 jit_solution(4203027835896957158)
XLA Ops:
  0.0 0.9 %copy.19 = bf16[4,8,8,128]{3,1,2,0:T(8,128)(2,1)S(1)} copy(f32[4,8,8,128]{3,2,1,0:T(8,128)} %bitcast.40) | data formatting | bytes 196608
  1.0 1.1 %copy.17 = bf16[32,8,8,128]{3,1,2,0:T(8,128)(2,1)S(1)} copy(bf16[32,8,8,128]{3,2,1,0:T(8,128)(2,1)} %bitcast.39) | data formatting | bytes 1048576
  2.1 0.0 copy-start
  2.2 0.7 %copy-done = bf16[32,8,8,128]{3,1,2,0:T(8,128)(2,1)} copy-done((bf16[32,8,8,128]{3,1,2,0:T(8,128)(2,1)}, bf16[32,8,8,128]{3,1,2,0:T(8,128)(2,1)S(1)}, u32[]{:S(2)}) %copy-start) | copy-done | bytes 524312
  2.9 2.7 %collective-permute-start.1 = (bf16[320,384]{1,0:T(8,128)(2,1)S(1)}, bf16[320,384]{1,0:T(8,128)(2,1)S(1)}, u32[]{:S(2)}, u32[]{:S(2)}) collective-permute-start(bf16[320,384]{1,0:T(8,128)(2,1)S(1)} %pad_maximum_fusion.1), channel_id=1, source_target_pairs={{1,0},{2,1},{3,2},{4,3},{5,4},{6,5},{7,6},{8,7},{9,8},{10,9},{11,1... | collective-permute-start | bytes 737288 | tf_op jit(solution)/shard_map/ppermute | solution.py:114
  5.6 0.0 copy-start.1
  5.7 2.1 %collective-permute-start = (bf16[320,384]{1,0:T(8,128)(2,1)S(1)}, bf16[320,384]{1,0:T(8,128)(2,1)S(1)}, u32[]{:S(2)}, u32[]{:S(2)}) collective-permute-start(bf16[320,384]{1,0:T(8,128)(2,1)S(1)} %pad_maximum_fusion), channel_id=1, source_target_pairs={{0,1},{1,2},{2,3},{3,4},{4,5},{5,6},{6,7},{7,8},{8,9},{9,10},{10,1... | collective-permute-start | bytes 737288 | tf_op jit(solution)/shard_map/ppermute | solution.py:113
  7.8 0.0 copy-done.1
  7.8 0.2 reduce_sum.9
  7.9 0.1 broadcast_divide_fusion
  8.0 0.0 copy-start.2
  8.1 0.1 add_select_fusion.1
  8.1 1.0 %fusion.2.refs_3_ = bf16[7,8,256]{2,1,0:T(8,128)(2,1)} fusion(f32[8,15,7,7]{1,0,3,2:T(8,128)S(1)} %broadcast_divide_fusion, s32[15,7]{0,1:T(8,128)S(1)} %add_select_fusion.1), kind=kOutput, calls=%fused_computation.4 | convolution fusion | flops 18104576 | bytes 52612 | tf_op jit(solution)/shard_map/vabc,acl->bvl/dot_general | solution.py:18
  9.1 0.1 add_select_fusion
  9.2 0.0 copy-done.2
  9.2 0.7 %copy.18 = f32[4,8,8,128]{3,1,2,0:T(8,128)} copy(f32[4,8,8,128]{3,2,1,0:T(8,128)S(1)} %bitcast.41) | data formatting | bytes 262144
  9.9 1.1 %fusion.1.refs_4_ = bf16[7,7,256]{2,1,0:T(8,128)(2,1)} fusion(f32[8,15,7,7]{1,0,3,2:T(8,128)S(1)} %broadcast_divide_fusion, s32[8,15]{1,0:T(8,128)S(1)} %add_select_fusion), kind=kOutput, calls=%fused_computation.3 | convolution fusion | flops 18106624 | bytes 49088 | tf_op jit(solution)/shard_map/vabc,val->bcl/dot_general | solution.py:22
  10.9 0.0 collective-permute-done.1.refs_2_
  11.0 0.0 copy-start.3
  11.0 3.3 %collective-permute-done.refs_1_ = bf16[320,384]{1,0:T(8,128)(2,1)S(1)} collective-permute-done((bf16[320,384]{1,0:T(8,128)(2,1)S(1)}, bf16[320,384]{1,0:T(8,128)(2,1)S(1)}, u32[]{:S(2)}, u32[]{:S(2)}) %collective-permute-start) | collective-permute-done | bytes 245792 | tf_op jit(solution)/shard_map/ppermute | solution.py:113
  14.2 0.0 copy-start.4
  14.2 0.0 copy-done.3
  14.2 0.7 %copy-done.4 = bf16[320,384]{1,0:T(8,128)(2,1)} copy-done((bf16[320,384]{1,0:T(8,128)(2,1)}, bf16[320,384]{1,0:T(8,128)(2,1)S(1)}, u32[]{:S(2)}) %copy-start.4) | copy-done | bytes 245784
  14.9 6.6 %shard_map.46 = f32[32,1024]{1,0:T(8,128)} custom-call(f32[32,1024]{1,0:T(8,128)} %bitcast.37, bf16[320,384]{1,0:T(8,128)(2,1)} %copy-done.4, bf16[320,384]{1,0:T(8,128)(2,1)} %copy-done.3, bf16[7,8,256]{2,1,0:T(8,128)(2,1)} %fusion.2.refs_3_, bf16[7,7,256]{2,1,0:T(8,128)(2,1)} %fusion.1.refs_4_, bf16[256,1024]{1,0:T(8,128)(2,1)} %bitcast.36, f32[8]{0:T(128)} %refs_6_.1), custom_call_target="tpu_custom_call" | custom-call | tf_op jit(solution)/shard_map/pallas_call | solution.py:117
  21.5 1.6 %copy.10 = f32[4,8,8,128]{3,2,1,0:T(8,128)} copy(f32[4,8,8,128]{3,1,2,0:T(8,128)} %bitcast.38) | data formatting | bytes 262144
  (6 shorter events, 0.1 us)
Async XLA Ops:
  2.1 0.8 %copy-start = (bf16[32,8,8,128]{3,1,2,0:T(8,128)(2,1)}, bf16[32,8,8,128]{3,1,2,0:T(8,128)(2,1)S(1)}, u32[]{:S(2)}) copy-start(bf16[32,8,8,128]{3,1,2,0:T(8,128)(2,1)S(1)} %copy.17) | copy-start | bytes 1572868
  2.9 8.1 %collective-permute-start.1 = (bf16[320,384]{1,0:T(8,128)(2,1)S(1)}, bf16[320,384]{1,0:T(8,128)(2,1)S(1)}, u32[]{:S(2)}, u32[]{:S(2)}) collective-permute-start(bf16[320,384]{1,0:T(8,128)(2,1)S(1)} %pad_maximum_fusion.1), channel_id=1, source_target_pairs={{1,0},{2,1},{3,2},{4,3},{5,4},{6,5},{7,6},{8,7},{9,8},{10,9},{11,1... | collective-permute-start | bytes 737288 | tf_op jit(solution)/shard_map/ppermute | solution.py:114
  5.6 2.1 %copy-start.1 = (f32[8,15,7,7]{1,0,3,2:T(8,128)S(1)}, f32[8,15,7,7]{1,0,3,2:T(8,128)}, u32[]{:S(2)}) copy-start(f32[8,15,7,7]{1,0,3,2:T(8,128)} %param.6) | copy-start | bytes 70564
  5.7 8.5 %collective-permute-start = (bf16[320,384]{1,0:T(8,128)(2,1)S(1)}, bf16[320,384]{1,0:T(8,128)(2,1)S(1)}, u32[]{:S(2)}, u32[]{:S(2)}) collective-permute-start(bf16[320,384]{1,0:T(8,128)(2,1)S(1)} %pad_maximum_fusion), channel_id=1, source_target_pairs={{0,1},{1,2},{2,3},{3,4},{4,5},{5,6},{6,7},{7,8},{8,9},{9,10},{10,1... | collective-permute-start | bytes 737288 | tf_op jit(solution)/shard_map/ppermute | solution.py:113
  8.0 1.1 %copy-start.2 = (f32[32,8,128]{2,1,0:T(8,128)S(1)}, f32[32,8,128]{2,1,0:T(8,128)}, u32[]{:S(2)}) copy-start(f32[32,8,128]{2,1,0:T(8,128)} %param.5) | copy-start | bytes 393220
  11.0 3.3 %copy-start.3 = (bf16[320,384]{1,0:T(8,128)(2,1)}, bf16[320,384]{1,0:T(8,128)(2,1)S(1)}, u32[]{:S(2)}) copy-start(bf16[320,384]{1,0:T(8,128)(2,1)S(1)} %collective-permute-done.1.refs_2_) | copy-start | bytes 737284
  14.2 0.7 %copy-start.4 = (bf16[320,384]{1,0:T(8,128)(2,1)}, bf16[320,384]{1,0:T(8,128)(2,1)S(1)}, u32[]{:S(2)}) copy-start(bf16[320,384]{1,0:T(8,128)(2,1)S(1)} %collective-permute-done.refs_1_) | copy-start | bytes 737284

commit v3 on v2

--- a/solution.py
+++ b/solution.py
@@ -45,7 +45,7 @@
 def rl_kernel(start_ref, before_ref, after_ref, bbase_ref, cbase_ref, meas_ref, bg_ref, out_ref,
               ext_ref, xs_ref, wb_ref, wc_ref, mext_ref, rext_ref, *, cols, reach_y, reach_x, half, half_z):
     planes = start_ref.shape[0]
-    n_out = start_ref.shape[1]
+    n_out = start_ref.shape[1] * cols
     views = bbase_ref.shape[1]
     hw = half * cols
     n_mid = n_out + 2 * hw
@@ -57,14 +57,21 @@
         for c in range(reach_x):
             row = cbase_ref[b, c:c + 1, :].astype(jnp.float32)
             wc_ref[b, c * planes:(c + 1) * planes, :] = toeplitz_block(row, planes, half_z, views * planes)
-    ext_ref[:, :hw] = before_ref[:planes, :].astype(jnp.float32)
-    ext_ref[:, hw:2 * hw] = before_ref[planes:2 * planes, :].astype(jnp.float32)
-    ext_ref[:, 2 * hw:2 * hw + n_out] = start_ref[...].astype(jnp.bfloat16).astype(jnp.float32)
-    ext_ref[:, 2 * hw + n_out:3 * hw + n_out] = after_ref[:planes, :].astype(jnp.float32)
-    ext_ref[:, 3 * hw + n_out:] = after_ref[planes:2 * planes, :].astype(jnp.float32)
-    mext_ref[:, :hw] = before_ref[2 * planes:, :]
+    rows = start_ref.shape[1]
+    for j in range(2 * half):
+        ext_ref[:, j * cols:(j + 1) * cols] = before_ref[j * planes:(j + 1) * planes, :].astype(jnp.float32)
+        at = (2 * half + rows + j) * cols
+        ext_ref[:, at:at + cols] = after_ref[j * planes:(j + 1) * planes, :].astype(jnp.float32)
+    for r in range(rows):
+        at = (2 * half + r) * cols
+        ext_ref[:, at:at + cols] = start_ref[:, r, :].astype(jnp.bfloat16).astype(jnp.float32)
+    m0 = 2 * half * planes
+    vp = views * planes
+    for j in range(half):
+        mext_ref[:, j * cols:(j + 1) * cols] = before_ref[m0 + j * vp:m0 + (j + 1) * vp, :]
+        at = (half + rows + j) * cols
+        mext_ref[:, at:at + cols] = after_ref[m0 + j * vp:m0 + (j + 1) * vp, :]
     mext_ref[:, hw:hw + n_out] = meas_ref[...]
-    mext_ref[:, hw + n_out:] = after_ref[2 * planes:, :]
     xs_ref[width:, :] = jnp.zeros((xs_ref.shape[0] - width, xs_ref.shape[1]), jnp.bfloat16)
     ext = ext_ref[...]
     for c in range(reach_x):
@@ -86,7 +93,8 @@
     for c in range(reach_x):
         piece = lane_shift(acc[c * planes:(c + 1) * planes], reach_x // 2 - c, cols)
         total = piece if total is None else total + piece
-    out_ref[...] = start_ref[...] * total / views
+    for r in range(start_ref.shape[1]):
+        out_ref[:, r, :] = start_ref[:, r, :] * total[:, r * cols:(r + 1) * cols] / views
 
 
 def local(measured, start, psf, background):
@@ -103,12 +111,19 @@
     vmem = pl.BlockSpec(memory_space=pltpu.VMEM)
     smem = pl.BlockSpec(memory_space=pltpu.SMEM)
 
-    start2 = start.reshape(planes, n_out)
-    rounded = start2.astype(jnp.bfloat16)
+    rounded = start.astype(jnp.bfloat16)
     meas2 = measured.reshape(views * planes, n_out)
-    last = jnp.concatenate(
-        [rounded[:, n_out - 2 * hw:n_out - hw], rounded[:, n_out - hw:], meas2[:, n_out - hw:]], axis=0)
-    first = jnp.concatenate([rounded[:, :hw], rounded[:, hw:2 * hw], meas2[:, :hw]], axis=0)
+
+    def slab(lo, hi):
+        r = jnp.transpose(rounded[:, lo:hi, :], (1, 0, 2)).reshape(-1, cols)
+        return r
+
+    def meas_rows(lo, hi):
+        m = jnp.transpose(measured[:, :, lo:hi, :], (2, 0, 1, 3)).reshape(-1, cols)
+        return m
+
+    last = jnp.concatenate([slab(rows - 2 * half, rows), meas_rows(rows - half, rows)], axis=0)
+    first = jnp.concatenate([slab(0, 2 * half), meas_rows(0, half)], axis=0)
     peers = lax.axis_size("gy")
     before = lax.ppermute(last, "gy", [(i, i + 1) for i in range(peers - 1)])
     after = lax.ppermute(first, "gy", [(i + 1, i) for i in range(peers - 1)])
@@ -116,7 +131,7 @@
     n_mid = n_out + 2 * hw
     est = pl.pallas_call(
         lambda *refs: rl_kernel(*refs, cols=cols, reach_y=reach_y, reach_x=reach_x, half=half, half_z=half_z),
-        out_shape=jax.ShapeDtypeStruct((planes, n_out), jnp.float32),
+        out_shape=jax.ShapeDtypeStruct((planes, rows, cols), jnp.float32),
         in_specs=[vmem] * 6 + [smem],
         out_specs=vmem,
         scratch_shapes=[
@@ -127,8 +142,8 @@
             pltpu.VMEM((views * planes, n_mid), jnp.bfloat16),
             pltpu.VMEM((views * planes, n_mid), jnp.bfloat16),
         ],
-    )(start2, before, after, blur_b, corr_b, meas2, background)
-    return est.reshape(planes, rows, cols)
+    )(start, before, after, blur_b, corr_b, meas2, background)
+    return est
 
 
 def solution(mesh):

time: 23.3 us -> 22.5 us (0.966)
  the two profiles are of different devices: /device:TPU:10 before, /device:TPU:5 now
where the time goes in v3:
time: 22.5 us; the launch traced here: 22.3 us
  Pallas kernels  6.72 us (30%)
  starting transfers between devices  5.76 us (26%)
  local copies, waits for them, and re-layouts  4.09 us (18%)
  waiting for transfers between devices  3.08 us (14%)
  matrix products  2.06 us (9%)
  other arithmetic  0.47 us (2%)
    pallas_call x1, Pallas kernels, local(): pl.pallas_call(lambda *refs: rl_kernel(*refs, cols=cols, reach_y=reach_y,...  6.72 us
    ppermute x1, starting transfers between devices, local(): before = lax.ppermute(last, 'gy', [(i, i + 1) for i in range(peers - 1)])  3.71 us
    ppermute x1, waiting for transfers between devices, local(): after = lax.ppermute(first, 'gy', [(i + 1, i) for i in range(peers - 1)])  3.07 us
    unnamed x11, local copies, waits for them, and re-layouts  2.46 us
    ppermute x1, starting transfers between devices, local(): after = lax.ppermute(first, 'gy', [(i + 1, i) for i in range(peers - 1)])  2.05 us
    transpose x3, local copies, waits for them, and re-layouts, meas_rows(): m = jnp.transpose(measured[:, :, lo:hi, :], (2, 0, 1, 3)).reshape(-1, cols)  1.58 us
    dot_general x1, matrix products, build_bases(): jnp.einsum('vabc,val->bcl', kernel, onehot, precision=lax.Precision.HIGHEST)  1.12 us
    dot_general x1, matrix products, build_bases(): jnp.einsum('vabc,acl->bvl', kernel, onehot, precision=lax.Precision.HIGHEST)  0.94 us
  transfers between devices with their start and end apart: 2, of which 1 were waited for; matrix products, arithmetic and copies ran while one was open for 15% of the time, Pallas kernels for 0%

profile of v3, /device:TPU:5, one launch (start us, length us, event | category | flops | bytes accessed | tf_op | source)
XLA Modules:
  0.0 22.3 jit_solution(2841445023891701803)
XLA Ops:
  0.0 1.5 %slice_bitcast_fusion = (bf16[3,8,32,128]{3,0,2,1:T(4,128)(2,1)S(1)}, bf16[3,8,32,128]{3,0,2,1:T(4,128)(2,1)S(1)}) fusion(bf16[8,32,8,128]{3,2,1,0:T(8,128)(2,1)} %param.4), kind=kLoop, calls=%fused_computation.6 | loop fusion | bytes 786432 | tf_op jit(solution)/shard_map/transpose | solution.py:122
  1.5 0.0 copy-start.2
  1.6 0.9 %copy-done.2 = f32[32,8,128]{2,1,0:T(8,128)S(1)} copy-done((f32[32,8,128]{2,1,0:T(8,128)S(1)}, f32[32,8,128]{2,1,0:T(8,128)}, u32[]{:S(2)}) %copy-start.2) | copy-done | bytes 131096
  2.5 3.7 %collective-permute-start = (bf16[960,128]{1,0:T(8,128)(2,1)S(1)}, bf16[960,128]{1,0:T(8,128)(2,1)S(1)}, u32[]{:S(2)}, u32[]{:S(2)}) collective-permute-start(bf16[960,128]{1,0:T(8,128)(2,1)S(1)} %pad_maximum_fusion), channel_id=1, source_target_pairs={{0,1},{1,2},{2,3},{3,4},{4,5},{5,6},{6,7},{7,8},{8,9},{9,10},{10,1... | collective-permute-start | bytes 737288 | tf_op jit(solution)/shard_map/ppermute | solution.py:128
  6.3 0.0 copy-start.1
  6.3 0.0 copy-start
  6.3 2.1 %collective-permute-start.1 = (bf16[960,128]{1,0:T(8,128)(2,1)S(1)}, bf16[960,128]{1,0:T(8,128)(2,1)S(1)}, u32[]{:S(2)}, u32[]{:S(2)}) collective-permute-start(bf16[960,128]{1,0:T(8,128)(2,1)S(1)} %pad_maximum_fusion.1), channel_id=1, source_target_pairs={{1,0},{2,1},{3,2},{4,3},{5,4},{6,5},{7,6},{8,7},{9,8},{10,9},{11,1... | collective-permute-start | bytes 737288 | tf_op jit(solution)/shard_map/ppermute | solution.py:129
  8.4 0.0 copy-done.1
  8.4 0.2 reduce_sum.9
  8.6 0.1 broadcast_divide_fusion
  8.7 0.1 add_select_fusion.1
  8.8 0.9 %fusion.2.refs_3_ = bf16[7,8,256]{2,1,0:T(8,128)(2,1)} fusion(f32[8,15,7,7]{1,0,3,2:T(8,128)S(1)} %broadcast_divide_fusion, s32[15,7]{0,1:T(8,128)S(1)} %add_select_fusion.1), kind=kOutput, calls=%fused_computation.4 | convolution fusion | flops 18104576 | bytes 52612 | tf_op jit(solution)/shard_map/vabc,acl->bvl/dot_general | solution.py:18
  9.7 0.1 add_select_fusion
  9.8 0.0 copy-done
  9.8 0.9 %copy.16 = bf16[32,8,8,128]{3,1,2,0:T(8,128)(2,1)} copy(bf16[32,8,8,128]{3,2,1,0:T(8,128)(2,1)S(1)} %bitcast.39) | data formatting | bytes 1048576
  10.7 1.1 %fusion.1.refs_4_ = bf16[7,7,256]{2,1,0:T(8,128)(2,1)} fusion(f32[8,15,7,7]{1,0,3,2:T(8,128)S(1)} %broadcast_divide_fusion, s32[8,15]{1,0:T(8,128)S(1)} %add_select_fusion), kind=kOutput, calls=%fused_computation.3 | convolution fusion | flops 18106624 | bytes 49088 | tf_op jit(solution)/shard_map/vabc,val->bcl/dot_general | solution.py:22
  11.8 0.0 collective-permute-done.refs_1_
  11.8 0.0 copy-start.3
  11.8 3.1 %collective-permute-done.1.refs_2_ = bf16[960,128]{1,0:T(8,128)(2,1)S(1)} collective-permute-done((bf16[960,128]{1,0:T(8,128)(2,1)S(1)}, bf16[960,128]{1,0:T(8,128)(2,1)S(1)}, u32[]{:S(2)}, u32[]{:S(2)}) %collective-permute-start.1) | collective-permute-done | bytes 245792 | tf_op jit(solution)/shard_map/ppermute | solution.py:129
  14.9 0.0 copy-start.4
  14.9 0.0 copy-done.3
  14.9 0.7 %copy-done.4 = bf16[960,128]{1,0:T(8,128)(2,1)} copy-done((bf16[960,128]{1,0:T(8,128)(2,1)}, bf16[960,128]{1,0:T(8,128)(2,1)S(1)}, u32[]{:S(2)}) %copy-start.4) | copy-done | bytes 245784
  15.6 6.7 %shard_map.46 = f32[32,8,128]{2,1,0:T(8,128)} custom-call(f32[32,8,128]{2,1,0:T(8,128)} %refs_0_.1, bf16[960,128]{1,0:T(8,128)(2,1)} %copy-done.3, bf16[960,128]{1,0:T(8,128)(2,1)} %copy-done.4, bf16[7,8,256]{2,1,0:T(8,128)(2,1)} %fusion.2.refs_3_, bf16[7,7,256]{2,1,0:T(8,128)(2,1)} %fusion.1.refs_4_, bf16[256,1024]{1,0:T(8,128)(2,1)} %bitcast.38, f32[8]{0:T(128)} %refs_6_.1), custom_call_target="tpu_custom_call" | custom-call | tf_op jit(solution)/shard_map/pallas_call | solution.py:132
  (10 shorter events, 0.2 us)
Async XLA Ops:
  1.5 0.9 %copy-start.2 = (f32[32,8,128]{2,1,0:T(8,128)S(1)}, f32[32,8,128]{2,1,0:T(8,128)}, u32[]{:S(2)}) copy-start(f32[32,8,128]{2,1,0:T(8,128)} %refs_0_.1) | copy-start | bytes 393220
  2.5 9.3 %collective-permute-start = (bf16[960,128]{1,0:T(8,128)(2,1)S(1)}, bf16[960,128]{1,0:T(8,128)(2,1)S(1)}, u32[]{:S(2)}, u32[]{:S(2)}) collective-permute-start(bf16[960,128]{1,0:T(8,128)(2,1)S(1)} %pad_maximum_fusion), channel_id=1, source_target_pairs={{0,1},{1,2},{2,3},{3,4},{4,5},{5,6},{6,7},{7,8},{8,9},{9,10},{10,1... | collective-permute-start | bytes 737288 | tf_op jit(solution)/shard_map/ppermute | solution.py:128
  6.3 2.1 %copy-start.1 = (f32[8,15,7,7]{1,0,3,2:T(8,128)S(1)}, f32[8,15,7,7]{1,0,3,2:T(8,128)}, u32[]{:S(2)}) copy-start(f32[8,15,7,7]{1,0,3,2:T(8,128)} %param.6) | copy-start | bytes 70564
  6.3 3.5 %copy-start = (bf16[8,32,8,128]{3,2,1,0:T(8,128)(2,1)S(1)}, bf16[8,32,8,128]{3,2,1,0:T(8,128)(2,1)}, u32[]{:S(2)}) copy-start(bf16[8,32,8,128]{3,2,1,0:T(8,128)(2,1)} %param.4) | copy-start | bytes 1572868
  6.3 8.5 %collective-permute-start.1 = (bf16[960,128]{1,0:T(8,128)(2,1)S(1)}, bf16[960,128]{1,0:T(8,128)(2,1)S(1)}, u32[]{:S(2)}, u32[]{:S(2)}) collective-permute-start(bf16[960,128]{1,0:T(8,128)(2,1)S(1)} %pad_maximum_fusion.1), channel_id=1, source_target_pairs={{1,0},{2,1},{3,2},{4,3},{5,4},{6,5},{7,6},{8,7},{9,8},{10,9},{11,1... | collective-permute-start | bytes 737288 | tf_op jit(solution)/shard_map/ppermute | solution.py:129
  11.8 3.1 %copy-start.3 = (bf16[960,128]{1,0:T(8,128)(2,1)}, bf16[960,128]{1,0:T(8,128)(2,1)S(1)}, u32[]{:S(2)}) copy-start(bf16[960,128]{1,0:T(8,128)(2,1)S(1)} %collective-permute-done.refs_1_) | copy-start | bytes 737284
  14.9 0.7 %copy-start.4 = (bf16[960,128]{1,0:T(8,128)(2,1)}, bf16[960,128]{1,0:T(8,128)(2,1)S(1)}, u32[]{:S(2)}) copy-start(bf16[960,128]{1,0:T(8,128)(2,1)S(1)} %collective-permute-done.1.refs_2_) | copy-start | bytes 737284

commit v4 on v3

--- a/solution.py
+++ b/solution.py
@@ -42,14 +42,9 @@
     return jnp.where(keep, rolled, jnp.zeros_like(rolled))
 
 
-def rl_kernel(start_ref, before_ref, after_ref, bbase_ref, cbase_ref, meas_ref, bg_ref, out_ref,
-              ext_ref, xs_ref, wb_ref, wc_ref, mext_ref, rext_ref, *, cols, reach_y, reach_x, half, half_z):
-    planes = start_ref.shape[0]
-    n_out = start_ref.shape[1] * cols
-    views = bbase_ref.shape[1]
-    hw = half * cols
-    n_mid = n_out + 2 * hw
-    width = reach_x * planes
+def weights_kernel(bbase_ref, cbase_ref, wb_ref, wc_ref, *, planes, half_z, width):
+    reach_y, views = bbase_ref.shape[0], bbase_ref.shape[1]
+    reach_x = cbase_ref.shape[1]
     for b in range(reach_y):
         for v in range(views):
             row = bbase_ref[b, v:v + 1, :].astype(jnp.float32)
@@ -57,6 +52,20 @@
         for c in range(reach_x):
             row = cbase_ref[b, c:c + 1, :].astype(jnp.float32)
             wc_ref[b, c * planes:(c + 1) * planes, :] = toeplitz_block(row, planes, half_z, views * planes)
+
+
+def rl_kernel(start_ref, before_ref, after_ref, wb_hbm, wc_hbm, meas_ref, bg_ref, out_ref,
+              ext_ref, xs_ref, wb_ref, wc_ref, mext_ref, rext_ref, sems, *, cols, reach_y, reach_x, half, half_z):
+    planes = start_ref.shape[0]
+    n_out = start_ref.shape[1] * cols
+    views = meas_ref.shape[0] // planes
+    hw = half * cols
+    n_mid = n_out + 2 * hw
+    width = reach_x * planes
+    copy_b = pltpu.make_async_copy(wb_hbm, wb_ref, sems.at[0])
+    copy_c = pltpu.make_async_copy(wc_hbm, wc_ref, sems.at[1])
+    copy_b.start()
+    copy_c.start()
     rows = start_ref.shape[1]
     for j in range(2 * half):
         ext_ref[:, j * cols:(j + 1) * cols] = before_ref[j * planes:(j + 1) * planes, :].astype(jnp.float32)
@@ -76,6 +85,7 @@
     ext = ext_ref[...]
     for c in range(reach_x):
         xs_ref[c * planes:(c + 1) * planes, :] = lane_shift(ext, c - reach_x // 2, cols).astype(jnp.bfloat16)
+    copy_b.wait()
     acc = None
     for b in range(reach_y):
         off = (2 * half - b) * cols
@@ -84,6 +94,7 @@
     for v in range(views):
         rows = slice(v * planes, (v + 1) * planes)
         rext_ref[rows, :] = (mext_ref[rows, :].astype(jnp.float32) / (acc[rows] + bg_ref[v])).astype(jnp.bfloat16)
+    copy_c.wait()
     acc = None
     for b in range(reach_y):
         off = b * cols
@@ -129,10 +140,20 @@
     after = lax.ppermute(first, "gy", [(i + 1, i) for i in range(peers - 1)])
 
     n_mid = n_out + 2 * hw
+    wb, wc = pl.pallas_call(
+        lambda *refs: weights_kernel(*refs, planes=planes, half_z=half_z, width=reach_x * planes),
+        out_shape=(
+            jax.ShapeDtypeStruct((reach_y, views * planes, lanes), jnp.bfloat16),
+            jax.ShapeDtypeStruct((reach_y, reach_x * planes, views * planes), jnp.bfloat16),
+        ),
+        in_specs=[vmem] * 2,
+        out_specs=(vmem, vmem),
+    )(blur_b, corr_b)
+    anyspace = pl.BlockSpec(memory_space=pl.ANY)
     est = pl.pallas_call(
         lambda *refs: rl_kernel(*refs, cols=cols, reach_y=reach_y, reach_x=reach_x, half=half, half_z=half_z),
         out_shape=jax.ShapeDtypeStruct((planes, rows, cols), jnp.float32),
-        in_specs=[vmem] * 6 + [smem],
+        in_specs=[vmem] * 3 + [anyspace] * 2 + [vmem, smem],
         out_specs=vmem,
         scratch_shapes=[
             pltpu.VMEM((planes, n_out + 4 * hw), jnp.float32),
@@ -141,8 +162,9 @@
             pltpu.VMEM((reach_y, reach_x * planes, views * planes), jnp.bfloat16),
             pltpu.VMEM((views * planes, n_mid), jnp.bfloat16),
             pltpu.VMEM((views * planes, n_mid), jnp.bfloat16),
+            pltpu.SemaphoreType.DMA((2,)),
         ],
-    )(start, before, after, blur_b, corr_b, meas2, background)
+    )(start, before, after, wb, wc, meas2, background)
     return est
 
 

time: 22.5 us -> 22.8 us (1.013)
  the two profiles are of different devices: /device:TPU:5 before, /device:TPU:10 now
where the time goes in v4:
time: 22.8 us; the launch traced here: 22.6 us
  Pallas kernels  10.2 us (45%)
  starting transfers between devices  6.59 us (29%)
  local copies, waits for them, and re-layouts  2.12 us (9%)
  matrix products  2.05 us (9%)
  other arithmetic  1.43 us (6%)
    pallas_call x1, Pallas kernels, local(): pl.pallas_call(lambda *refs: rl_kernel(*refs, cols=cols, reach_y=reach_y,...  7.76 us
    ppermute x1, starting transfers between devices, local(): after = lax.ppermute(first, 'gy', [(i + 1, i) for i in range(peers - 1)])  4.67 us
    pallas_call x1, Pallas kernels, local(): pl.pallas_call(lambda *refs: weights_kernel(*refs, planes=planes, half_z=...  2.48 us
    ppermute x1, starting transfers between devices, local(): before = lax.ppermute(last, 'gy', [(i, i + 1) for i in range(peers - 1)])  1.92 us
    unnamed x9, local copies, waits for them, and re-layouts  1.78 us
    dot_general x1, matrix products, build_bases(): jnp.einsum('vabc,val->bcl', kernel, onehot, precision=lax.Precision.HIGHEST)  1.1 us
    convert_element_type x1, other arithmetic, local(): rounded = start.astype(jnp.bfloat16)  0.97 us
    dot_general x1, matrix products, build_bases(): jnp.einsum('vabc,acl->bvl', kernel, onehot, precision=lax.Precision.HIGHEST)  0.95 us
  transfers between devices with their start and end apart: 2, of which 0 were waited for; matrix products, arithmetic and copies ran while one was open for 15% of the time, Pallas kernels for 11%

profile of v4, /device:TPU:10, one launch (start us, length us, event | category | flops | bytes accessed | tf_op | source)
XLA Modules:
  0.0 22.6 jit_solution(7494140971942823490)
XLA Ops:
  0.0 0.0 copy-start
  0.0 1.0 %convert_element_type.13 = bf16[32,8,128]{2,1,0:T(8,128)(2,1)S(1)} convert(f32[32,8,128]{2,1,0:T(8,128)} %refs_0_.1) | non-fusion elementwise | flops 32768 | bytes 196608 | tf_op jit(solution)/shard_map/convert_element_type | solution.py:125
  1.0 0.1 copy-done
  1.1 0.2 %slice_bitcast_fusion = (bf16[3,8,32,128]{3,0,2,1:T(4,128)(2,1)S(1)}, bf16[3,8,32,128]{3,0,2,1:T(4,128)(2,1)S(1)}) fusion(bf16[8,32,8,128]{3,2,1,0:T(8,128)(2,1)S(1)} %copy-done), kind=kLoop, calls=%fused_computation.6 | loop fusion | bytes 786432 | tf_op jit(solution)/shard_map/transpose | solution.py:133
  1.4 1.9 %collective-permute-start = (bf16[960,128]{1,0:T(8,128)(2,1)S(1)}, bf16[960,128]{1,0:T(8,128)(2,1)S(1)}, u32[]{:S(2)}, u32[]{:S(2)}) collective-permute-start(bf16[960,128]{1,0:T(8,128)(2,1)S(1)} %pad_maximum_fusion), channel_id=1, source_target_pairs={{0,1},{1,2},{2,3},{3,4},{4,5},{5,6},{6,7},{7,8},{8,9},{9,10},{10,1... | collective-permute-start | bytes 737288 | tf_op jit(solution)/shard_map/ppermute | solution.py:139
  3.4 0.0 copy-start.1
  3.4 4.7 %collective-permute-start.1 = (bf16[960,128]{1,0:T(8,128)(2,1)S(1)}, bf16[960,128]{1,0:T(8,128)(2,1)S(1)}, u32[]{:S(2)}, u32[]{:S(2)}) collective-permute-start(bf16[960,128]{1,0:T(8,128)(2,1)S(1)} %pad_maximum_fusion.1), channel_id=1, source_target_pairs={{1,0},{2,1},{3,2},{4,3},{5,4},{6,5},{7,6},{8,7},{9,8},{10,9},{11,1... | collective-permute-start | bytes 737288 | tf_op jit(solution)/shard_map/ppermute | solution.py:140
  8.1 0.1 add_select_fusion.1
  8.2 0.0 copy-done.1
  8.2 0.2 reduce_sum.9
  8.4 0.1 broadcast_divide_fusion
  8.5 0.9 %fusion.2.refs_0_ = bf16[7,8,256]{2,1,0:T(8,128)(2,1)} fusion(f32[8,15,7,7]{1,0,3,2:T(8,128)S(1)} %broadcast_divide_fusion, s32[15,7]{0,1:T(8,128)S(1)} %add_select_fusion.1), kind=kOutput, calls=%fused_computation.4 | convolution fusion | flops 18104576 | bytes 52612 | tf_op jit(solution)/shard_map/vabc,acl->bvl/dot_general | solution.py:18
  9.4 0.1 add_select_fusion
  9.5 0.9 %copy.16 = bf16[32,8,8,128]{3,1,2,0:T(8,128)(2,1)} copy(bf16[32,8,8,128]{3,2,1,0:T(8,128)(2,1)S(1)} %bitcast.39) | data formatting | bytes 1048576
  10.4 1.1 %fusion.1.refs_1_ = bf16[7,7,256]{2,1,0:T(8,128)(2,1)} fusion(f32[8,15,7,7]{1,0,3,2:T(8,128)S(1)} %broadcast_divide_fusion, s32[8,15]{1,0:T(8,128)S(1)} %add_select_fusion), kind=kOutput, calls=%fused_computation.3 | convolution fusion | flops 18106624 | bytes 49088 | tf_op jit(solution)/shard_map/vabc,val->bcl/dot_general | solution.py:22
  11.5 2.5 %shard_map.46 = (bf16[7,256,256]{2,1,0:T(8,128)(2,1)}, bf16[7,224,256]{2,1,0:T(8,128)(2,1)}) custom-call(bf16[7,8,256]{2,1,0:T(8,128)(2,1)} %fusion.2.refs_0_, bf16[7,7,256]{2,1,0:T(8,128)(2,1)} %fusion.1.refs_1_), custom_call_target="tpu_custom_call" | custom-call | tf_op jit(solution)/shard_map/pallas_call | solution.py:143
  14.0 0.0 collective-permute-done.refs_1_
  14.0 0.0 copy-start.2
  14.0 0.0 collective-permute-done.1.refs_2_
  14.0 0.0 copy-start.3
  14.0 0.7 %copy-done.2 = bf16[960,128]{1,0:T(8,128)(2,1)} copy-done((bf16[960,128]{1,0:T(8,128)(2,1)}, bf16[960,128]{1,0:T(8,128)(2,1)S(1)}, u32[]{:S(2)}) %copy-start.2) | copy-done | bytes 245784
  14.7 0.1 copy-done.3
  14.8 7.8 %shard_map.47 = f32[32,8,128]{2,1,0:T(8,128)} custom-call(f32[32,8,128]{2,1,0:T(8,128)} %refs_0_.1, bf16[960,128]{1,0:T(8,128)(2,1)} %copy-done.2, bf16[960,128]{1,0:T(8,128)(2,1)} %copy-done.3, bf16[7,256,256]{2,1,0:T(8,128)(2,1)} %get-tuple-element.7.refs_3_, bf16[7,224,256]{2,1,0:T(8,128)(2,1)} %get-tuple-element.8.refs_4_, bf16[256,1024]{1,0:T(8,128)(2,1)} %bitcast.38, ...), custom_call_target="tpu_custom_call" | custom-call | tf_op jit(solution)/shard_map/pallas_call | solution.py:153
  (9 shorter events, 0.2 us)
Async XLA Ops:
  0.0 1.1 %copy-start = (bf16[8,32,8,128]{3,2,1,0:T(8,128)(2,1)S(1)}, bf16[8,32,8,128]{3,2,1,0:T(8,128)(2,1)}, u32[]{:S(2)}) copy-start(bf16[8,32,8,128]{3,2,1,0:T(8,128)(2,1)} %param.4) | copy-start | bytes 1572868
  1.4 12.6 %collective-permute-start = (bf16[960,128]{1,0:T(8,128)(2,1)S(1)}, bf16[960,128]{1,0:T(8,128)(2,1)S(1)}, u32[]{:S(2)}, u32[]{:S(2)}) collective-permute-start(bf16[960,128]{1,0:T(8,128)(2,1)S(1)} %pad_maximum_fusion), channel_id=1, source_target_pairs={{0,1},{1,2},{2,3},{3,4},{4,5},{5,6},{6,7},{7,8},{8,9},{9,10},{10,1... | collective-permute-start | bytes 737288 | tf_op jit(solution)/shard_map/ppermute | solution.py:139
  3.4 4.8 %copy-start.1 = (f32[8,15,7,7]{1,0,3,2:T(8,128)S(1)}, f32[8,15,7,7]{1,0,3,2:T(8,128)}, u32[]{:S(2)}) copy-start(f32[8,15,7,7]{1,0,3,2:T(8,128)} %param.6) | copy-start | bytes 70564
  3.4 10.6 %collective-permute-start.1 = (bf16[960,128]{1,0:T(8,128)(2,1)S(1)}, bf16[960,128]{1,0:T(8,128)(2,1)S(1)}, u32[]{:S(2)}, u32[]{:S(2)}) collective-permute-start(bf16[960,128]{1,0:T(8,128)(2,1)S(1)} %pad_maximum_fusion.1), channel_id=1, source_target_pairs={{1,0},{2,1},{3,2},{4,3},{5,4},{6,5},{7,6},{8,7},{9,8},{10,9},{11,1... | collective-permute-start | bytes 737288 | tf_op jit(solution)/shard_map/ppermute | solution.py:140
  14.0 0.7 %copy-start.2 = (bf16[960,128]{1,0:T(8,128)(2,1)}, bf16[960,128]{1,0:T(8,128)(2,1)S(1)}, u32[]{:S(2)}) copy-start(bf16[960,128]{1,0:T(8,128)(2,1)S(1)} %collective-permute-done.refs_1_) | copy-start | bytes 737284
  14.0 0.8 %copy-start.3 = (bf16[960,128]{1,0:T(8,128)(2,1)}, bf16[960,128]{1,0:T(8,128)(2,1)S(1)}, u32[]{:S(2)}) copy-start(bf16[960,128]{1,0:T(8,128)(2,1)S(1)} %collective-permute-done.1.refs_2_) | copy-start | bytes 737284

commit v5 on v3

--- a/solution.py
+++ b/solution.py
@@ -43,7 +43,7 @@
 
 
 def rl_kernel(start_ref, before_ref, after_ref, bbase_ref, cbase_ref, meas_ref, bg_ref, out_ref,
-              ext_ref, xs_ref, wb_ref, wc_ref, mext_ref, rext_ref, *, cols, reach_y, reach_x, half, half_z):
+              xs_ref, wb_ref, wc_ref, rext_ref, *, cols, reach_y, reach_x, half, half_z):
     planes = start_ref.shape[0]
     n_out = start_ref.shape[1] * cols
     views = bbase_ref.shape[1]
@@ -58,43 +58,58 @@
             row = cbase_ref[b, c:c + 1, :].astype(jnp.float32)
             wc_ref[b, c * planes:(c + 1) * planes, :] = toeplitz_block(row, planes, half_z, views * planes)
     rows = start_ref.shape[1]
-    for j in range(2 * half):
-        ext_ref[:, j * cols:(j + 1) * cols] = before_ref[j * planes:(j + 1) * planes, :].astype(jnp.float32)
-        at = (2 * half + rows + j) * cols
-        ext_ref[:, at:at + cols] = after_ref[j * planes:(j + 1) * planes, :].astype(jnp.float32)
-    for r in range(rows):
-        at = (2 * half + r) * cols
-        ext_ref[:, at:at + cols] = start_ref[:, r, :].astype(jnp.bfloat16).astype(jnp.float32)
+    vp = views * planes
     m0 = 2 * half * planes
-    vp = views * planes
-    for j in range(half):
-        mext_ref[:, j * cols:(j + 1) * cols] = before_ref[m0 + j * vp:m0 + (j + 1) * vp, :]
-        at = (half + rows + j) * cols
-        mext_ref[:, at:at + cols] = after_ref[m0 + j * vp:m0 + (j + 1) * vp, :]
-    mext_ref[:, hw:hw + n_out] = meas_ref[...]
+
+    def rounded_slab(e):
+        if e < 2 * half:
+            return before_ref[e * planes:(e + 1) * planes, :].astype(jnp.float32)
+        if e >= 2 * half + rows:
+            j = e - 2 * half - rows
+            return after_ref[j * planes:(j + 1) * planes, :].astype(jnp.float32)
+        return start_ref[:, e - 2 * half, :].astype(jnp.bfloat16).astype(jnp.float32)
+
+    def measured_slab(m):
+        if m < half:
+            return before_ref[m0 + m * vp:m0 + (m + 1) * vp, :]
+        if m >= half + rows:
+            j = m - half - rows
+            return after_ref[m0 + j * vp:m0 + (j + 1) * vp, :]
+        return meas_ref[:, (m - half) * cols:(m - half + 1) * cols]
+
     xs_ref[width:, :] = jnp.zeros((xs_ref.shape[0] - width, xs_ref.shape[1]), jnp.bfloat16)
-    ext = ext_ref[...]
-    for c in range(reach_x):
-        xs_ref[c * planes:(c + 1) * planes, :] = lane_shift(ext, c - reach_x // 2, cols).astype(jnp.bfloat16)
-    acc = None
-    for b in range(reach_y):
-        off = (2 * half - b) * cols
-        part = jnp.dot(wb_ref[b], xs_ref[:, off:off + n_mid], preferred_element_type=jnp.float32)
-        acc = part if acc is None else acc + part
-    for v in range(views):
-        rows = slice(v * planes, (v + 1) * planes)
-        rext_ref[rows, :] = (mext_ref[rows, :].astype(jnp.float32) / (acc[rows] + bg_ref[v])).astype(jnp.bfloat16)
-    acc = None
-    for b in range(reach_y):
-        off = b * cols
-        part = jnp.dot(wc_ref[b], rext_ref[:, off:off + n_out], preferred_element_type=jnp.float32)
-        acc = part if acc is None else acc + part
-    total = None
-    for c in range(reach_x):
-        piece = lane_shift(acc[c * planes:(c + 1) * planes], reach_x // 2 - c, cols)
-        total = piece if total is None else total + piece
-    for r in range(start_ref.shape[1]):
-        out_ref[:, r, :] = start_ref[:, r, :] * total[:, r * cols:(r + 1) * cols] / views
+    for e in range(rows + 4 * half):
+        slab = rounded_slab(e)
+        for c in range(reach_x):
+            xs_ref[c * planes:(c + 1) * planes, e * cols:(e + 1) * cols] = (
+                lane_shift(slab, c - reach_x // 2, cols).astype(jnp.bfloat16))
+    step = 2 * cols
+    for k in range(n_mid // step):
+        acc = None
+        for b in range(reach_y):
+            off = (2 * half - b) * cols + k * step
+            part = jnp.dot(wb_ref[b], xs_ref[:, off:off + step], preferred_element_type=jnp.float32)
+            acc = part if acc is None else acc + part
+        for i in range(step // cols):
+            m = k * (step // cols) + i
+            meas = measured_slab(m)
+            for v in range(views):
+                rs = slice(v * planes, (v + 1) * planes)
+                ratio = meas[rs].astype(jnp.float32) / (acc[rs, i * cols:(i + 1) * cols] + bg_ref[v])
+                rext_ref[rs, m * cols:(m + 1) * cols] = ratio.astype(jnp.bfloat16)
+    for k in range(n_out // step):
+        acc = None
+        for b in range(reach_y):
+            off = b * cols + k * step
+            part = jnp.dot(wc_ref[b], rext_ref[:, off:off + step], preferred_element_type=jnp.float32)
+            acc = part if acc is None else acc + part
+        total = None
+        for c in range(reach_x):
+            piece = lane_shift(acc[c * planes:(c + 1) * planes], reach_x // 2 - c, cols)
+            total = piece if total is None else total + piece
+        for i in range(step // cols):
+            r = k * (step // cols) + i
+            out_ref[:, r, :] = start_ref[:, r, :] * total[:, i * cols:(i + 1) * cols] / views
 
 
 def local(measured, start, psf, background):
@@ -103,7 +118,7 @@
     reach_y, reach_x = psf.shape[2], psf.shape[3]
     half = reach_y // 2
     half_z = psf.shape[1] // 2
-    assert rows >= 2 * half
+    assert rows >= 2 * half and rows % 2 == 0
     lanes = -(-(reach_x * planes + half_z) // 128) * 128
     blur_b, corr_b = build_bases(psf, planes, lanes, views * planes)
     n_out = rows * cols
@@ -135,11 +150,9 @@
         in_specs=[vmem] * 6 + [smem],
         out_specs=vmem,
         scratch_shapes=[
-            pltpu.VMEM((planes, n_out + 4 * hw), jnp.float32),
             pltpu.VMEM((lanes, n_out + 4 * hw), jnp.bfloat16),
             pltpu.VMEM((reach_y, views * planes, lanes), jnp.bfloat16),
             pltpu.VMEM((reach_y, reach_x * planes, views * planes), jnp.bfloat16),
-            pltpu.VMEM((views * planes, n_mid), jnp.bfloat16),
             pltpu.VMEM((views * planes, n_mid), jnp.bfloat16),
         ],
     )(start, before, after, blur_b, corr_b, meas2, background)

time: 22.5 us -> 20.9 us (0.929)
  Pallas kernels: 6.72 us -> 5.06 us
    pallas_call x1, Pallas kernels: 6.72 us -> 5.06 us  [local(): pl.pallas_call(lambda *refs: rl_kernel(*refs, cols=cols, reach_y=reach_y,...]
  transfers between devices with their start and end apart: 2 -> 2, of which waited for: 1 -> 1; matrix products, arithmetic and copies ran while one was open for 15% -> 17% of each run, Pallas kernels for 0% -> 0%
where the time goes in v5:
time: 20.9 us; the launch traced here: 20.7 us
  starting transfers between devices  5.76 us (28%)
  Pallas kernels  5.06 us (24%)
  local copies, waits for them, and re-layouts  4.09 us (20%)
  waiting for transfers between devices  3.08 us (15%)
  matrix products  2.06 us (10%)
  other arithmetic  0.47 us (2%)
    pallas_call x1, Pallas kernels, local(): pl.pallas_call(lambda *refs: rl_kernel(*refs, cols=cols, reach_y=reach_y,...  5.06 us
    ppermute x1, starting transfers between devices, local(): before = lax.ppermute(last, 'gy', [(i, i + 1) for i in range(peers - 1)])  3.71 us
    ppermute x1, waiting for transfers between devices, local(): after = lax.ppermute(first, 'gy', [(i + 1, i) for i in range(peers - 1)])  3.07 us
    unnamed x11, local copies, waits for them, and re-layouts  2.46 us
    ppermute x1, starting transfers between devices, local(): after = lax.ppermute(first, 'gy', [(i + 1, i) for i in range(peers - 1)])  2.05 us
    transpose x3, local copies, waits for them, and re-layouts, meas_rows(): m = jnp.transpose(measured[:, :, lo:hi, :], (2, 0, 1, 3)).reshape(-1, cols)  1.58 us
    dot_general x1, matrix products, build_bases(): jnp.einsum('vabc,val->bcl', kernel, onehot, precision=lax.Precision.HIGHEST)  1.12 us
    dot_general x1, matrix products, build_bases(): jnp.einsum('vabc,acl->bvl', kernel, onehot, precision=lax.Precision.HIGHEST)  0.94 us
  transfers between devices with their start and end apart: 2, of which 1 were waited for; matrix products, arithmetic and copies ran while one was open for 17% of the time, Pallas kernels for 0%

profile of v5, /device:TPU:5, one launch (start us, length us, event | category | flops | bytes accessed | tf_op | source)
XLA Modules:
  0.0 20.7 jit_solution(15532002333542716094)
XLA Ops:
  0.0 1.5 %slice_bitcast_fusion = (bf16[3,8,32,128]{3,0,2,1:T(4,128)(2,1)S(1)}, bf16[3,8,32,128]{3,0,2,1:T(4,128)(2,1)S(1)}) fusion(bf16[8,32,8,128]{3,2,1,0:T(8,128)(2,1)} %param.4), kind=kLoop, calls=%fused_computation.6 | loop fusion | bytes 786432 | tf_op jit(solution)/shard_map/transpose | solution.py:137
  1.5 0.0 copy-start.2
  1.6 0.9 %copy-done.2 = f32[32,8,128]{2,1,0:T(8,128)S(1)} copy-done((f32[32,8,128]{2,1,0:T(8,128)S(1)}, f32[32,8,128]{2,1,0:T(8,128)}, u32[]{:S(2)}) %copy-start.2) | copy-done | bytes 131096
  2.5 3.7 %collective-permute-start = (bf16[960,128]{1,0:T(8,128)(2,1)S(1)}, bf16[960,128]{1,0:T(8,128)(2,1)S(1)}, u32[]{:S(2)}, u32[]{:S(2)}) collective-permute-start(bf16[960,128]{1,0:T(8,128)(2,1)S(1)} %pad_maximum_fusion), channel_id=1, source_target_pairs={{0,1},{1,2},{2,3},{3,4},{4,5},{5,6},{6,7},{7,8},{8,9},{9,10},{10,1... | collective-permute-start | bytes 737288 | tf_op jit(solution)/shard_map/ppermute | solution.py:143
  6.3 0.0 copy-start.1
  6.3 0.0 copy-start
  6.3 2.1 %collective-permute-start.1 = (bf16[960,128]{1,0:T(8,128)(2,1)S(1)}, bf16[960,128]{1,0:T(8,128)(2,1)S(1)}, u32[]{:S(2)}, u32[]{:S(2)}) collective-permute-start(bf16[960,128]{1,0:T(8,128)(2,1)S(1)} %pad_maximum_fusion.1), channel_id=1, source_target_pairs={{1,0},{2,1},{3,2},{4,3},{5,4},{6,5},{7,6},{8,7},{9,8},{10,9},{11,1... | collective-permute-start | bytes 737288 | tf_op jit(solution)/shard_map/ppermute | solution.py:144
  8.4 0.0 copy-done.1
  8.4 0.2 reduce_sum.9
  8.6 0.1 broadcast_divide_fusion
  8.7 0.1 add_select_fusion.1
  8.8 0.9 %fusion.2.refs_3_ = bf16[7,8,256]{2,1,0:T(8,128)(2,1)} fusion(f32[8,15,7,7]{1,0,3,2:T(8,128)S(1)} %broadcast_divide_fusion, s32[15,7]{0,1:T(8,128)S(1)} %add_select_fusion.1), kind=kOutput, calls=%fused_computation.4 | convolution fusion | flops 18104576 | bytes 52612 | tf_op jit(solution)/shard_map/vabc,acl->bvl/dot_general | solution.py:18
  9.7 0.1 add_select_fusion
  9.8 0.0 copy-done
  9.8 0.9 %copy.16 = bf16[32,8,8,128]{3,1,2,0:T(8,128)(2,1)} copy(bf16[32,8,8,128]{3,2,1,0:T(8,128)(2,1)S(1)} %bitcast.39) | data formatting | bytes 1048576
  10.7 1.1 %fusion.1.refs_4_ = bf16[7,7,256]{2,1,0:T(8,128)(2,1)} fusion(f32[8,15,7,7]{1,0,3,2:T(8,128)S(1)} %broadcast_divide_fusion, s32[8,15]{1,0:T(8,128)S(1)} %add_select_fusion), kind=kOutput, calls=%fused_computation.3 | convolution fusion | flops 18106624 | bytes 49088 | tf_op jit(solution)/shard_map/vabc,val->bcl/dot_general | solution.py:22
  11.8 0.0 collective-permute-done.refs_1_
  11.8 0.0 copy-start.3
  11.8 3.1 %collective-permute-done.1.refs_2_ = bf16[960,128]{1,0:T(8,128)(2,1)S(1)} collective-permute-done((bf16[960,128]{1,0:T(8,128)(2,1)S(1)}, bf16[960,128]{1,0:T(8,128)(2,1)S(1)}, u32[]{:S(2)}, u32[]{:S(2)}) %collective-permute-start.1) | collective-permute-done | bytes 245792 | tf_op jit(solution)/shard_map/ppermute | solution.py:144
  14.9 0.0 copy-start.4
  14.9 0.0 copy-done.3
  14.9 0.7 %copy-done.4 = bf16[960,128]{1,0:T(8,128)(2,1)} copy-done((bf16[960,128]{1,0:T(8,128)(2,1)}, bf16[960,128]{1,0:T(8,128)(2,1)S(1)}, u32[]{:S(2)}) %copy-start.4) | copy-done | bytes 245784
  15.6 5.1 %shard_map.46 = f32[32,8,128]{2,1,0:T(8,128)} custom-call(f32[32,8,128]{2,1,0:T(8,128)} %refs_0_.1, bf16[960,128]{1,0:T(8,128)(2,1)} %copy-done.3, bf16[960,128]{1,0:T(8,128)(2,1)} %copy-done.4, bf16[7,8,256]{2,1,0:T(8,128)(2,1)} %fusion.2.refs_3_, bf16[7,7,256]{2,1,0:T(8,128)(2,1)} %fusion.1.refs_4_, bf16[256,1024]{1,0:T(8,128)(2,1)} %bitcast.38, f32[8]{0:T(128)} %refs_6_.1), custom_call_target="tpu_custom_call" | custom-call | tf_op jit(solution)/shard_map/pallas_call | solution.py:147
  (10 shorter events, 0.2 us)
Async XLA Ops:
  1.5 0.9 %copy-start.2 = (f32[32,8,128]{2,1,0:T(8,128)S(1)}, f32[32,8,128]{2,1,0:T(8,128)}, u32[]{:S(2)}) copy-start(f32[32,8,128]{2,1,0:T(8,128)} %refs_0_.1) | copy-start | bytes 393220
  2.5 9.3 %collective-permute-start = (bf16[960,128]{1,0:T(8,128)(2,1)S(1)}, bf16[960,128]{1,0:T(8,128)(2,1)S(1)}, u32[]{:S(2)}, u32[]{:S(2)}) collective-permute-start(bf16[960,128]{1,0:T(8,128)(2,1)S(1)} %pad_maximum_fusion), channel_id=1, source_target_pairs={{0,1},{1,2},{2,3},{3,4},{4,5},{5,6},{6,7},{7,8},{8,9},{9,10},{10,1... | collective-permute-start | bytes 737288 | tf_op jit(solution)/shard_map/ppermute | solution.py:143
  6.3 2.1 %copy-start.1 = (f32[8,15,7,7]{1,0,3,2:T(8,128)S(1)}, f32[8,15,7,7]{1,0,3,2:T(8,128)}, u32[]{:S(2)}) copy-start(f32[8,15,7,7]{1,0,3,2:T(8,128)} %param.6) | copy-start | bytes 70564
  6.3 3.5 %copy-start = (bf16[8,32,8,128]{3,2,1,0:T(8,128)(2,1)S(1)}, bf16[8,32,8,128]{3,2,1,0:T(8,128)(2,1)}, u32[]{:S(2)}) copy-start(bf16[8,32,8,128]{3,2,1,0:T(8,128)(2,1)} %param.4) | copy-start | bytes 1572868
  6.3 8.5 %collective-permute-start.1 = (bf16[960,128]{1,0:T(8,128)(2,1)S(1)}, bf16[960,128]{1,0:T(8,128)(2,1)S(1)}, u32[]{:S(2)}, u32[]{:S(2)}) collective-permute-start(bf16[960,128]{1,0:T(8,128)(2,1)S(1)} %pad_maximum_fusion.1), channel_id=1, source_target_pairs={{1,0},{2,1},{3,2},{4,3},{5,4},{6,5},{7,6},{8,7},{9,8},{10,9},{11,1... | collective-permute-start | bytes 737288 | tf_op jit(solution)/shard_map/ppermute | solution.py:144
  11.8 3.1 %copy-start.3 = (bf16[960,128]{1,0:T(8,128)(2,1)}, bf16[960,128]{1,0:T(8,128)(2,1)S(1)}, u32[]{:S(2)}) copy-start(bf16[960,128]{1,0:T(8,128)(2,1)S(1)} %collective-permute-done.refs_1_) | copy-start | bytes 737284
  14.9 0.7 %copy-start.4 = (bf16[960,128]{1,0:T(8,128)(2,1)}, bf16[960,128]{1,0:T(8,128)(2,1)S(1)}, u32[]{:S(2)}) copy-start(bf16[960,128]{1,0:T(8,128)(2,1)S(1)} %collective-permute-done.1.refs_2_) | copy-start | bytes 737284

commit v6 on v5

--- a/solution.py
+++ b/solution.py
@@ -40,6 +40,26 @@
     col = lax.broadcasted_iota(jnp.int32, x.shape, x.ndim - 1) % cols
     keep = (col - shift >= 0) & (col - shift < cols)
     return jnp.where(keep, rolled, jnp.zeros_like(rolled))
+
+
+def prep_kernel(start_ref, meas_ref, last_ref, first_ref, meas2_ref, *, half):
+    planes, rows, cols = start_ref.shape
+    vp = meas_ref.shape[0]
+    m0 = 2 * half * planes
+    for r in range(rows):
+        slab = meas_ref[:, r, :]
+        meas2_ref[:, r * cols:(r + 1) * cols] = slab
+        rounded = start_ref[:, r, :].astype(jnp.bfloat16)
+        if r < half:
+            first_ref[m0 + r * vp:m0 + (r + 1) * vp, :] = slab
+        if r >= rows - half:
+            j = r - (rows - half)
+            last_ref[m0 + j * vp:m0 + (j + 1) * vp, :] = slab
+        if r < 2 * half:
+            first_ref[r * planes:(r + 1) * planes, :] = rounded
+        if r >= rows - 2 * half:
+            j = r - (rows - 2 * half)
+            last_ref[j * planes:(j + 1) * planes, :] = rounded
 
 
 def rl_kernel(start_ref, before_ref, after_ref, bbase_ref, cbase_ref, meas_ref, bg_ref, out_ref,
@@ -126,19 +146,17 @@
     vmem = pl.BlockSpec(memory_space=pltpu.VMEM)
     smem = pl.BlockSpec(memory_space=pltpu.SMEM)
 
-    rounded = start.astype(jnp.bfloat16)
-    meas2 = measured.reshape(views * planes, n_out)
-
-    def slab(lo, hi):
-        r = jnp.transpose(rounded[:, lo:hi, :], (1, 0, 2)).reshape(-1, cols)
-        return r
-
-    def meas_rows(lo, hi):
-        m = jnp.transpose(measured[:, :, lo:hi, :], (2, 0, 1, 3)).reshape(-1, cols)
-        return m
-
-    last = jnp.concatenate([slab(rows - 2 * half, rows), meas_rows(rows - half, rows)], axis=0)
-    first = jnp.concatenate([slab(0, 2 * half), meas_rows(0, half)], axis=0)
+    n_slab = 2 * half * planes + half * views * planes
+    last, first, meas2 = pl.pallas_call(
+        lambda *refs: prep_kernel(*refs, half=half),
+        out_shape=(
+            jax.ShapeDtypeStruct((n_slab, cols), jnp.bfloat16),
+            jax.ShapeDtypeStruct((n_slab, cols), jnp.bfloat16),
+            jax.ShapeDtypeStruct((views * planes, n_out), jnp.bfloat16),
+        ),
+        in_specs=[vmem] * 2,
+        out_specs=(vmem, vmem, vmem),
+    )(start, measured.reshape(views * planes, rows, cols))
     peers = lax.axis_size("gy")
     before = lax.ppermute(last, "gy", [(i, i + 1) for i in range(peers - 1)])
     after = lax.ppermute(first, "gy", [(i + 1, i) for i in range(peers - 1)])

time: 20.9 us -> 21.2 us (1.014)
  local copies, waits for them, and re-layouts: 4.09 us -> 0.69 us
  Pallas kernels: 5.06 us -> 7.99 us
  waiting for transfers between devices: 3.08 us -> 4.18 us
    pallas_call x0 -> x1, Pallas kernels: none -> 2.94 us  [local(): pl.pallas_call(lambda *refs: prep_kernel(*refs, half=half), out_shape=(ja...]
    unnamed x11 -> x6, local copies, waits for them, and re-layouts: 2.46 us -> 0.69 us
    transpose x6 -> x0, local copies, waits for them, and re-layouts: 1.62 us -> none  [the longest x3 1.58 us: meas_rows(): m = jnp.transpose(measured[:, :, lo:hi, :], (2, 0, 1, 3)).reshape(-1, cols)]
    ppermute x1, waiting for transfers between devices: 3.07 us -> 4.18 us  [local(): after = lax.ppermute(first, 'gy', [(i + 1, i) for i in range(peers - 1)])]
  transfers between devices with their start and end apart: 2 -> 2, of which waited for: 1 -> 1; matrix products, arithmetic and copies ran while one was open for 17% -> 12% of each run, Pallas kernels for 0% -> 0%
where the time goes in v6:
time: 21.2 us; the launch traced here: 21 us
  Pallas kernels  7.99 us (38%)
  starting transfers between devices  5.62 us (27%)
  waiting for transfers between devices  4.18 us (20%)
  matrix products  2.06 us (10%)
  local copies, waits for them, and re-layouts  0.69 us (3%)
  other arithmetic  0.42 us (2%)
    pallas_call x1, Pallas kernels, local(): pl.pallas_call(lambda *refs: rl_kernel(*refs, cols=cols, reach_y=reach_y,...  5.06 us
    ppermute x1, waiting for transfers between devices, local(): after = lax.ppermute(first, 'gy', [(i + 1, i) for i in range(peers - 1)])  4.18 us
    ppermute x1, starting transfers between devices, local(): before = lax.ppermute(last, 'gy', [(i, i + 1) for i in range(peers - 1)])  3.7 us
    pallas_call x1, Pallas kernels, local(): pl.pallas_call(lambda *refs: prep_kernel(*refs, half=half), out_shape=(ja...  2.94 us
    ppermute x1, starting transfers between devices, local(): after = lax.ppermute(first, 'gy', [(i + 1, i) for i in range(peers - 1)])  1.92 us
    dot_general x1, matrix products, build_bases(): jnp.einsum('vabc,val->bcl', kernel, onehot, precision=lax.Precision.HIGHEST)  1.11 us
    dot_general x1, matrix products, build_bases(): jnp.einsum('vabc,acl->bvl', kernel, onehot, precision=lax.Precision.HIGHEST)  0.95 us
    unnamed x6, local copies, waits for them, and re-layouts  0.69 us
  transfers between devices with their start and end apart: 2, of which 1 were waited for; matrix products, arithmetic and copies ran while one was open for 12% of the time, Pallas kernels for 0%

profile of v6, /device:TPU:5, one launch (start us, length us, event | category | flops | bytes accessed | tf_op | source)
XLA Modules:
  0.0 21.0 jit_solution(9156519410915482507)
XLA Ops:
  0.0 0.0 copy-start
  0.0 2.9 %shard_map.46 = (bf16[960,128]{1,0:T(8,128)(2,1)}, bf16[960,128]{1,0:T(8,128)(2,1)}, bf16[256,1024]{1,0:T(8,128)(2,1)}) custom-call(f32[32,8,128]{2,1,0:T(8,128)} %refs_0_.3, bf16[256,8,128]{2,1,0:T(8,128)(2,1)} %bitcast.22), custom_call_target="tpu_custom_call" | custom-call | tf_op jit(solution)/shard_map/pallas_call | solution.py:150
  2.9 3.7 %collective-permute-start = (bf16[960,128]{1,0:T(8,128)(2,1)}, bf16[960,128]{1,0:T(8,128)(2,1)S(1)}, u32[]{:S(2)}, u32[]{:S(2)}) collective-permute-start(bf16[960,128]{1,0:T(8,128)(2,1)} %get-tuple-element.8), channel_id=1, source_target_pairs={{0,1},{1,2},{2,3},{3,4},{4,5},{5,6},{6,7},{7,8},{8,9},{9,10},{10,1... | collective-permute-start | bytes 737288 | tf_op jit(solution)/shard_map/ppermute | solution.py:161
  6.6 1.9 %collective-permute-start.1 = (bf16[960,128]{1,0:T(8,128)(2,1)}, bf16[960,128]{1,0:T(8,128)(2,1)S(1)}, u32[]{:S(2)}, u32[]{:S(2)}) collective-permute-start(bf16[960,128]{1,0:T(8,128)(2,1)} %get-tuple-element.9), channel_id=1, source_target_pairs={{1,0},{2,1},{3,2},{4,3},{5,4},{6,5},{7,6},{8,7},{9,8},{10,9},{11,1... | collective-permute-start | bytes 737288 | tf_op jit(solution)/shard_map/ppermute | solution.py:162
  8.6 0.0 copy-done
  8.6 0.2 reduce_sum.9
  8.8 0.1 broadcast_divide_fusion
  8.9 0.1 add_select_fusion.1
  8.9 0.9 %fusion.2.refs_3_ = bf16[7,8,256]{2,1,0:T(8,128)(2,1)} fusion(f32[8,15,7,7]{1,0,3,2:T(8,128)S(1)} %broadcast_divide_fusion, s32[15,7]{0,1:T(8,128)S(1)} %add_select_fusion.1), kind=kOutput, calls=%fused_computation.4 | convolution fusion | flops 18104576 | bytes 52612 | tf_op jit(solution)/shard_map/vabc,acl->bvl/dot_general | solution.py:18
  9.9 0.1 add_select_fusion
  10.0 1.1 %fusion.1.refs_4_ = bf16[7,7,256]{2,1,0:T(8,128)(2,1)} fusion(f32[8,15,7,7]{1,0,3,2:T(8,128)S(1)} %broadcast_divide_fusion, s32[8,15]{1,0:T(8,128)S(1)} %add_select_fusion), kind=kOutput, calls=%fused_computation.3 | convolution fusion | flops 18106624 | bytes 49088 | tf_op jit(solution)/shard_map/vabc,val->bcl/dot_general | solution.py:22
  11.1 0.0 collective-permute-done.refs_1_
  11.1 0.0 copy-start.1
  11.1 4.2 %collective-permute-done.1.refs_2_ = bf16[960,128]{1,0:T(8,128)(2,1)S(1)} collective-permute-done((bf16[960,128]{1,0:T(8,128)(2,1)}, bf16[960,128]{1,0:T(8,128)(2,1)S(1)}, u32[]{:S(2)}, u32[]{:S(2)}) %collective-permute-start.1) | collective-permute-done | bytes 245792 | tf_op jit(solution)/shard_map/ppermute | solution.py:162
  15.3 0.0 copy-start.2
  15.3 0.0 copy-done.1
  15.3 0.7 %copy-done.2 = bf16[960,128]{1,0:T(8,128)(2,1)} copy-done((bf16[960,128]{1,0:T(8,128)(2,1)}, bf16[960,128]{1,0:T(8,128)(2,1)S(1)}, u32[]{:S(2)}) %copy-start.2) | copy-done | bytes 245784
  16.0 5.1 %shard_map.47 = f32[32,8,128]{2,1,0:T(8,128)} custom-call(f32[32,8,128]{2,1,0:T(8,128)} %refs_0_.3, bf16[960,128]{1,0:T(8,128)(2,1)} %copy-done.1, bf16[960,128]{1,0:T(8,128)(2,1)} %copy-done.2, bf16[7,8,256]{2,1,0:T(8,128)(2,1)} %fusion.2.refs_3_, bf16[7,7,256]{2,1,0:T(8,128)(2,1)} %fusion.1.refs_4_, bf16[256,1024]{1,0:T(8,128)(2,1)} %get-tuple-element.10.refs_5_, ...), custom_call_target="tpu_custom_call" | custom-call | tf_op jit(solution)/shard_map/pallas_call | solution.py:165
  (2 shorter events, 0.0 us)
Async XLA Ops:
  0.0 8.6 %copy-start = (f32[8,15,7,7]{1,0,3,2:T(8,128)S(1)}, f32[8,15,7,7]{1,0,3,2:T(8,128)}, u32[]{:S(2)}) copy-start(f32[8,15,7,7]{1,0,3,2:T(8,128)} %param.6) | copy-start | bytes 70564
  2.9 8.1 %collective-permute-start = (bf16[960,128]{1,0:T(8,128)(2,1)}, bf16[960,128]{1,0:T(8,128)(2,1)S(1)}, u32[]{:S(2)}, u32[]{:S(2)}) collective-permute-start(bf16[960,128]{1,0:T(8,128)(2,1)} %get-tuple-element.8), channel_id=1, source_target_pairs={{0,1},{1,2},{2,3},{3,4},{4,5},{5,6},{6,7},{7,8},{8,9},{9,10},{10,1... | collective-permute-start | bytes 737288 | tf_op jit(solution)/shard_map/ppermute | solution.py:161
  6.6 8.6 %collective-permute-start.1 = (bf16[960,128]{1,0:T(8,128)(2,1)}, bf16[960,128]{1,0:T(8,128)(2,1)S(1)}, u32[]{:S(2)}, u32[]{:S(2)}) collective-permute-start(bf16[960,128]{1,0:T(8,128)(2,1)} %get-tuple-element.9), channel_id=1, source_target_pairs={{1,0},{2,1},{3,2},{4,3},{5,4},{6,5},{7,6},{8,7},{9,8},{10,9},{11,1... | collective-permute-start | bytes 737288 | tf_op jit(solution)/shard_map/ppermute | solution.py:162
  11.1 4.2 %copy-start.1 = (bf16[960,128]{1,0:T(8,128)(2,1)}, bf16[960,128]{1,0:T(8,128)(2,1)S(1)}, u32[]{:S(2)}) copy-start(bf16[960,128]{1,0:T(8,128)(2,1)S(1)} %collective-permute-done.refs_1_) | copy-start | bytes 737284
  15.3 0.7 %copy-start.2 = (bf16[960,128]{1,0:T(8,128)(2,1)}, bf16[960,128]{1,0:T(8,128)(2,1)S(1)}, u32[]{:S(2)}) copy-start(bf16[960,128]{1,0:T(8,128)(2,1)S(1)} %collective-permute-done.1.refs_2_) | copy-start | bytes 737284

commit v7 on v5

v7 whole, which is shorter than its diff:
```python
import jax
import jax.numpy as jnp
from jax import lax
from jax.experimental import pallas as pl
from jax.experimental.pallas import tpu as pltpu
from jax.sharding import PartitionSpec as P


def build_bases(psf, planes, lanes, corr_lanes):
    kernel = psf / jnp.sum(psf, axis=(1, 2, 3), keepdims=True)
    views, depth, reach_y, reach_x = psf.shape
    half_z = depth // 2
    lane = jnp.arange(lanes, dtype=jnp.int32)
    tap = jnp.arange(depth, dtype=jnp.int32)
    col = jnp.arange(reach_x, dtype=jnp.int32)
    at = (col[None, :, None] * planes + half_z - tap[:, None, None]) % lanes
    onehot = (lane[None, None, :] == at).astype(jnp.float32)
    blur = jnp.einsum("vabc,acl->bvl", kernel, onehot, precision=lax.Precision.HIGHEST)
    view = jnp.arange(views, dtype=jnp.int32)
    at = (view[:, None, None] * planes + tap[None, :, None] - half_z) % corr_lanes
    onehot = (jnp.arange(corr_lanes, dtype=jnp.int32)[None, None, :] == at).astype(jnp.float32)
    corr = jnp.einsum("vabc,val->bcl", kernel, onehot, precision=lax.Precision.HIGHEST)
    return blur.astype(jnp.bfloat16), corr.astype(jnp.bfloat16)


def toeplitz_block(row, planes, half_z, width):
    lanes = row.shape[-1]
    blk = jnp.broadcast_to(row, (planes, lanes))
    blk = pltpu.roll(blk, 0, 1, stride=1, stride_axis=0)
    q = lax.broadcasted_iota(jnp.int32, (planes, lanes), 0)
    l = lax.broadcasted_iota(jnp.int32, (planes, lanes), 1)
    d = l % planes - q
    keep = (d <= half_z) & (d >= -half_z) & (l < width)
    return jnp.where(keep, blk, 0.0).astype(jnp.bfloat16)


def lane_shift(x, shift, cols):
    n = x.shape[-1]
    rolled = pltpu.roll(x, shift % n, x.ndim - 1) if shift % n else x
    col = lax.broadcasted_iota(jnp.int32, x.shape, x.ndim - 1) % cols
    keep = (col - shift >= 0) & (col - shift < cols)
    return jnp.where(keep, rolled, jnp.zeros_like(rolled))


def rl_kernel(start_ref, before_ref, after_ref, bbase_ref, cbase_ref, meas_ref, bg_ref,
              tot_ref, up_ref, down_ref, xs_ref, wb_ref, wc_ref, rext_ref, *, cols, reach_y, reach_x, half, half_z):
    planes, rows = start_ref.shape[0], start_ref.shape[1]
    views = bbase_ref.shape[1]
    width = reach_x * planes
    for b in range(reach_y):
        for v in range(views):
            row = bbase_ref[b, v:v + 1, :].astype(jnp.float32)
            wb_ref[b, v * planes:(v + 1) * planes, :] = toeplitz_block(row, planes, half_z, width)
        for c in range(reach_x):
            row = cbase_ref[b, c:c + 1, :].astype(jnp.float32)
            wc_ref[b, c * planes:(c + 1) * planes, :] = toeplitz_block(row, planes, half_z, views * planes)

    def rounded_slab(e):
        if e < half:
            return before_ref[e * planes:(e + 1) * planes, :].astype(jnp.float32)
        if e >= half + rows:
            j = e - half - rows
            return after_ref[j * planes:(j + 1) * planes, :].astype(jnp.float32)
        return start_ref[:, e - half, :].astype(jnp.bfloat16).astype(jnp.float32)

    xs_ref[width:, :] = jnp.zeros((xs_ref.shape[0] - width, xs_ref.shape[1]), jnp.bfloat16)
    for e in range(rows + 2 * half):
        slab = rounded_slab(e)
        for c in range(reach_x):
            xs_ref[c * planes:(c + 1) * planes, e * cols:(e + 1) * cols] = (
                lane_shift(slab, c - reach_x // 2, cols).astype(jnp.bfloat16))
    pad = 2 * half * cols
    zeros = jnp.zeros((rext_ref.shape[0], pad), jnp.bfloat16)
    rext_ref[:, :pad] = zeros
    rext_ref[:, pad + rows * cols:] = zeros
    step = 2 * cols
    for k in range(rows * cols // step):
        acc = None
        for b in range(reach_y):
            off = (2 * half - b) * cols + k * step
            part = jnp.dot(wb_ref[b], xs_ref[:, off:off + step], preferred_element_type=jnp.float32)
            acc = part if acc is None else acc + part
        for v in range(views):
            rs = slice(v * planes, (v + 1) * planes)
            ratio = meas_ref[rs, k * step:(k + 1) * step].astype(jnp.float32) / (acc[rs] + bg_ref[v])
            rext_ref[rs, pad + k * step:pad + (k + 1) * step] = ratio.astype(jnp.bfloat16)
    for k in range((rows + 2 * half) * cols // step):
        acc = None
        for b in range(reach_y):
            off = b * cols + k * step
            part = jnp.dot(wc_ref[b], rext_ref[:, off:off + step], preferred_element_type=jnp.float32)
            acc = part if acc is None else acc + part
        total = None
        for c in range(reach_x):
            piece = lane_shift(acc[c * planes:(c + 1) * planes], reach_x // 2 - c, cols)
            total = piece if total is None else total + piece
        for i in range(step // cols):
            o = k * (step // cols) + i - half
            t = total[:, i * cols:(i + 1) * cols]
            if o < 0:
                up_ref[(o + half) * planes:(o + half + 1) * planes, :] = t
            elif o >= rows:
                down_ref[(o - rows) * planes:(o - rows + 1) * planes, :] = t
            else:
                tot_ref[:, o, :] = t


def local(measured, start, psf, background):
    planes, rows, cols = start.shape
    views = measured.shape[0]
    reach_y, reach_x = psf.shape[2], psf.shape[3]
    half = reach_y // 2
    half_z = psf.shape[1] // 2
    assert rows >= half and rows % 2 == 0
    lanes = -(-(reach_x * planes + half_z) // 128) * 128
    blur_b, corr_b = build_bases(psf, planes, lanes, views * planes)
    n_out = rows * cols
    vmem = pl.BlockSpec(memory_space=pltpu.VMEM)
    smem = pl.BlockSpec(memory_space=pltpu.SMEM)
    meas2 = measured.reshape(views * planes, n_out)
    peers = lax.axis_size("gy")
    up = [(i, i + 1) for i in range(peers - 1)]
    down = [(i + 1, i) for i in range(peers - 1)]

    def slab(x, lo, hi):
        return jnp.transpose(x[:, lo:hi, :], (1, 0, 2)).reshape(-1, cols)

    rounded = start.astype(jnp.bfloat16)
    before = lax.ppermute(slab(rounded, rows - half, rows), "gy", up)
    after = lax.ppermute(slab(rounded, 0, half), "gy", down)

    tot, to_up, to_down = pl.pallas_call(
        lambda *refs: rl_kernel(*refs, cols=cols, reach_y=reach_y, reach_x=reach_x, half=half, half_z=half_z),
        out_shape=(
            jax.ShapeDtypeStruct((planes, rows, cols), jnp.float32),
            jax.ShapeDtypeStruct((half * planes, cols), jnp.float32),
            jax.ShapeDtypeStruct((half * planes, cols), jnp.float32),
        ),
        in_specs=[vmem] * 6 + [smem],
        out_specs=(vmem, vmem, vmem),
        scratch_shapes=[
            pltpu.VMEM((lanes, n_out + 2 * half * cols), jnp.bfloat16),
            pltpu.VMEM((reach_y, views * planes, lanes), jnp.bfloat16),
            pltpu.VMEM((reach_y, reach_x * planes, views * planes), jnp.bfloat16),
            pltpu.VMEM((views * planes, n_out + 4 * half * cols), jnp.bfloat16),
        ],
    )(start, before, after, blur_b, corr_b, meas2, background)
    top = lax.ppermute(to_down, "gy", up)
    bottom = lax.ppermute(to_up, "gy", down)
    top = jnp.transpose(top.reshape(half, planes, cols), (1, 0, 2))
    bottom = jnp.transpose(bottom.reshape(half, planes, cols), (1, 0, 2))
    total = tot.at[:, :half].add(top).at[:, rows - half:].add(bottom)
    return start * total / views


def solution(mesh):
    in_specs = (P(None, None, ("parts", "gy"), None), P(None, ("parts", "gy"), None), P(), P())
    out_specs = P(None, ("parts", "gy"), None)
    return jax.shard_map(local, mesh=mesh, in_specs=in_specs, out_specs=out_specs, check_vma=False)
```

time: 20.9 us -> 28.6 us (1.37)
  starting transfers between devices: 5.76 us -> 11.5 us
  other arithmetic: 0.47 us -> 3.03 us
  local copies, waits for them, and re-layouts: 4.09 us -> 2.61 us
  waiting for transfers between devices: 3.08 us -> 4.13 us
    ppermute x2 -> x4, starting transfers between devices: 5.76 us -> 11.5 us  [the longest x1 3.95 us: local(): top = lax.ppermute(to_down, 'gy', up)]
    transpose x6 -> x3, local copies, waits for them, and re-layouts: 1.62 us -> 0.04 us  [slab(): return jnp.transpose(x[:, lo:hi, :], (1, 0, 2)).reshape(-1, cols)]
    ppermute x2 -> x4, waiting for transfers between devices: 3.08 us -> 4.13 us  [the longest x1 3.4 us: local(): bottom = lax.ppermute(to_up, 'gy', down)]
    add x0 -> x2, other arithmetic: none -> 0.99 us  [local(): total = tot.at[:, :half].add(top).at[:, rows - half:].add(bottom)]
    convert_element_type x1, other arithmetic: 0.01 us -> 0.95 us  [local(): rounded = start.astype(jnp.bfloat16)]
    div x0 -> x1, other arithmetic: none -> 0.67 us  [local(): return start * total / views]
    scatter-add x0 -> x2, local copies, waits for them, and re-layouts: none -> 0.43 us  [local(): total = tot.at[:, :half].add(top).at[:, rows - half:].add(bottom)]
    unnamed x11 -> x13, local copies, waits for them, and re-layouts: 2.46 us -> 2.14 us
  transfers between devices with their start and end apart: 2 -> 4, of which waited for: 1 -> 2; matrix products, arithmetic and copies ran while one was open for 17% -> 16% of each run, Pallas kernels for 0% -> 0%
where the time goes in v7:
time: 28.6 us; the launch traced here: 28.3 us
  starting transfers between devices  11.5 us (40%)
  Pallas kernels  4.89 us (17%)
  waiting for transfers between devices  4.13 us (14%)
  other arithmetic  3.03 us (11%)
  local copies, waits for them, and re-layouts  2.61 us (9%)
  matrix products  2.04 us (7%)
    pallas_call x1, Pallas kernels, local(): pl.pallas_call(lambda *refs: rl_kernel(*refs, cols=cols, reach_y=reach_y,...  4.89 us
    ppermute x1, starting transfers between devices, local(): top = lax.ppermute(to_down, 'gy', up)  3.95 us
    ppermute x1, starting transfers between devices, local(): before = lax.ppermute(slab(rounded, rows - half, rows), 'gy', up)  3.71 us
    ppermute x1, waiting for transfers between devices, local(): bottom = lax.ppermute(to_up, 'gy', down)  3.4 us
    unnamed x13, local copies, waits for them, and re-layouts  2.14 us
    ppermute x1, starting transfers between devices, local(): after = lax.ppermute(slab(rounded, 0, half), 'gy', down)  1.92 us
    ppermute x1, starting transfers between devices, local(): bottom = lax.ppermute(to_up, 'gy', down)  1.92 us
    dot_general x1, matrix products, build_bases(): jnp.einsum('vabc,val->bcl', kernel, onehot, precision=lax.Precision.HIGHEST)  1.1 us
  transfers between devices with their start and end apart: 4, of which 2 were waited for; matrix products, arithmetic and copies ran while one was open for 16% of the time, Pallas kernels for 0%

profile of v7, /device:TPU:5, one launch (start us, length us, event | category | flops | bytes accessed | tf_op | source)
XLA Modules:
  0.0 28.3 jit_solution(5208599777718206261)
XLA Ops:
  0.0 0.0 copy-start.1
  0.0 1.0 %convert_element_type.13 = bf16[32,8,128]{2,1,0:T(8,128)(2,1)S(1)} convert(f32[32,8,128]{2,1,0:T(8,128)} %refs_0_.1) | non-fusion elementwise | flops 32768 | bytes 196608 | tf_op jit(solution)/shard_map/convert_element_type | solution.py:128
  1.0 3.7 %collective-permute-start = (bf16[96,128]{1,0:T(8,128)(2,1)S(1)}, bf16[96,128]{1,0:T(8,128)(2,1)S(1)}, u32[]{:S(2)}, u32[]{:S(2)}) collective-permute-start(bf16[96,128]{1,0:T(8,128)(2,1)S(1)} %bitcast.42), channel_id=1, source_target_pairs={{0,1},{1,2},{2,3},{3,4},{4,5},{5,6},{6,7},{7,8},{8,9},{9,10},{10,1... | collective-permute-start | bytes 73736 | tf_op jit(solution)/shard_map/ppermute | solution.py:129
  4.7 1.9 %collective-permute-start.1 = (bf16[96,128]{1,0:T(8,128)(2,1)S(1)}, bf16[96,128]{1,0:T(8,128)(2,1)S(1)}, u32[]{:S(2)}, u32[]{:S(2)}) collective-permute-start(bf16[96,128]{1,0:T(8,128)(2,1)S(1)} %bitcast.43), channel_id=1, source_target_pairs={{1,0},{2,1},{3,2},{4,3},{5,4},{6,5},{7,6},{8,7},{9,8},{10,9},{11,1... | collective-permute-start | bytes 73736 | tf_op jit(solution)/shard_map/ppermute | solution.py:130
  6.7 0.1 add_select_fusion
  6.8 0.1 add_select_fusion.1
  6.8 0.0 copy-done.1
  6.8 0.0 copy-start.2
  6.8 0.2 reduce_sum.9
  7.0 0.1 broadcast_divide_fusion
  7.1 1.1 %fusion.1.refs_4_ = bf16[7,7,256]{2,1,0:T(8,128)(2,1)} fusion(f32[8,15,7,7]{1,0,3,2:T(8,128)S(1)} %broadcast_divide_fusion, s32[8,15]{1,0:T(8,128)S(1)} %add_select_fusion), kind=kOutput, calls=%fused_computation.3 | convolution fusion | flops 18106624 | bytes 49088 | tf_op jit(solution)/shard_map/vabc,val->bcl/dot_general | solution.py:22
  8.2 0.9 %fusion.2.refs_3_ = bf16[7,8,256]{2,1,0:T(8,128)(2,1)} fusion(f32[8,15,7,7]{1,0,3,2:T(8,128)S(1)} %broadcast_divide_fusion, s32[15,7]{0,1:T(8,128)S(1)} %add_select_fusion.1), kind=kOutput, calls=%fused_computation.4 | convolution fusion | flops 18104576 | bytes 52612 | tf_op jit(solution)/shard_map/vabc,acl->bvl/dot_general | solution.py:18
  9.1 0.0 copy-done.2
  9.1 0.9 %copy.18 = bf16[32,8,8,128]{3,1,2,0:T(8,128)(2,1)} copy(bf16[32,8,8,128]{3,2,1,0:T(8,128)(2,1)S(1)} %bitcast.39) | data formatting | bytes 1048576
  10.0 0.0 collective-permute-done.refs_1_
  10.0 0.0 copy-start.4
  10.0 0.7 %collective-permute-done.1.refs_2_ = bf16[96,128]{1,0:T(8,128)(2,1)S(1)} collective-permute-done((bf16[96,128]{1,0:T(8,128)(2,1)S(1)}, bf16[96,128]{1,0:T(8,128)(2,1)S(1)}, u32[]{:S(2)}, u32[]{:S(2)}) %collective-permute-start.1) | collective-permute-done | bytes 24608 | tf_op jit(solution)/shard_map/ppermute | solution.py:130
  10.8 0.0 copy-start.5
  10.8 0.0 copy-done.4
  10.8 0.6 %copy-done.5 = bf16[96,128]{1,0:T(8,128)(2,1)} copy-done((bf16[96,128]{1,0:T(8,128)(2,1)}, bf16[96,128]{1,0:T(8,128)(2,1)S(1)}, u32[]{:S(2)}) %copy-start.5) | copy-done | bytes 24600
  11.4 4.9 %shard_map.46 = (f32[32,8,128]{2,1,0:T(8,128)}, f32[96,128]{1,0:T(8,128)}, f32[96,128]{1,0:T(8,128)}) custom-call(f32[32,8,128]{2,1,0:T(8,128)} %refs_0_.1, bf16[96,128]{1,0:T(8,128)(2,1)} %copy-done.4, bf16[96,128]{1,0:T(8,128)(2,1)} %copy-done.5, bf16[7,8,256]{2,1,0:T(8,128)(2,1)} %fusion.2.refs_3_, bf16[7,7,256]{2,1,0:T(8,128)(2,1)} %fusion.1.refs_4_, ...), custom_call_target="tpu_custom_call" | custom-call | tf_op jit(solution)/shard_map/pallas_call | solution.py:132
  16.3 0.0 copy-start.3
  16.3 4.0 %collective-permute-start.2 = (f32[96,128]{1,0:T(8,128)}, f32[96,128]{1,0:T(8,128)S(1)}, u32[]{:S(2)}, u32[]{:S(2)}) collective-permute-start(f32[96,128]{1,0:T(8,128)} %get-tuple-element.33), channel_id=1, source_target_pairs={{0,1},{1,2},{2,3},{3,4},{4,5},{5,6},{6,7},{7,8},{8,9},{9,10},{10,1... | collective-permute-start | bytes 147464 | tf_op jit(solution)/shard_map/ppermute | solution.py:148
  20.2 1.9 %collective-permute-start.3 = (f32[96,128]{1,0:T(8,128)}, f32[96,128]{1,0:T(8,128)S(1)}, u32[]{:S(2)}, u32[]{:S(2)}) collective-permute-start(f32[96,128]{1,0:T(8,128)} %get-tuple-element.34), channel_id=1, source_target_pairs={{1,0},{2,1},{3,2},{4,3},{5,4},{6,5},{7,6},{8,7},{9,8},{10,9},{11,1... | collective-permute-start | bytes 147464 | tf_op jit(solution)/shard_map/ppermute | solution.py:149
  22.1 0.0 collective-permute-done.2
  22.2 0.9 %bitcast_add_fusion = f32[32,3,128]{2,1,0:T(4,128)S(1)} fusion(f32[3,32,128]{2,1,0:T(8,128)S(1)} %bitcast.41, f32[32,8,128]{2,1,0:T(8,128)} %get-tuple-element.32), kind=kLoop, calls=%fused_computation.14 | loop fusion | flops 12288 | bytes 147456 | tf_op jit(solution)/shard_map/add | solution.py:152
  23.1 0.0 copy-done.3
  23.1 0.2 scatter-add.6
  23.3 3.4 %collective-permute-done.3 = f32[96,128]{1,0:T(8,128)S(1)} collective-permute-done((f32[96,128]{1,0:T(8,128)}, f32[96,128]{1,0:T(8,128)S(1)}, u32[]{:S(2)}, u32[]{:S(2)}) %collective-permute-start.3) | collective-permute-done | bytes 49184 | tf_op jit(solution)/shard_map/ppermute | solution.py:149
  26.8 0.2 scatter-add.9
  27.0 0.6 %copy-done = f32[32,8,128]{2,1,0:T(8,128)S(1)} copy-done((f32[32,8,128]{2,1,0:T(8,128)S(1)}, f32[32,8,128]{2,1,0:T(8,128)}, u32[]{:S(2)}) %copy-start) | copy-done | bytes 131096
  27.6 0.7 %multiply_multiply_fusion = f32[32,8,128]{2,1,0:T(8,128)} fusion(f32[32,8,128]{2,1,0:T(8,128)S(1)} %copy-done, f32[32,8,128]{2,1,0:T(8,128)S(1)} %scatter-add.9), kind=kLoop, calls=%fused_computation.7 | loop fusion | flops 65536 | bytes 393216 | tf_op jit(solution)/shard_map/div | solution.py:153
  (7 shorter events, 0.1 us)
Async XLA Ops:
  0.0 6.8 %copy-start.1 = (f32[8,15,7,7]{1,0,3,2:T(8,128)S(1)}, f32[8,15,7,7]{1,0,3,2:T(8,128)}, u32[]{:S(2)}) copy-start(f32[8,15,7,7]{1,0,3,2:T(8,128)} %param.10) | copy-start | bytes 70564
  1.0 9.0 %collective-permute-start = (bf16[96,128]{1,0:T(8,128)(2,1)S(1)}, bf16[96,128]{1,0:T(8,128)(2,1)S(1)}, u32[]{:S(2)}, u32[]{:S(2)}) collective-permute-start(bf16[96,128]{1,0:T(8,128)(2,1)S(1)} %bitcast.42), channel_id=1, source_target_pairs={{0,1},{1,2},{2,3},{3,4},{4,5},{5,6},{6,7},{7,8},{8,9},{9,10},{10,1... | collective-permute-start | bytes 73736 | tf_op jit(solution)/shard_map/ppermute | solution.py:129
  4.7 6.0 %collective-permute-start.1 = (bf16[96,128]{1,0:T(8,128)(2,1)S(1)}, bf16[96,128]{1,0:T(8,128)(2,1)S(1)}, u32[]{:S(2)}, u32[]{:S(2)}) collective-permute-start(bf16[96,128]{1,0:T(8,128)(2,1)S(1)} %bitcast.43), channel_id=1, source_target_pairs={{1,0},{2,1},{3,2},{4,3},{5,4},{6,5},{7,6},{8,7},{9,8},{10,9},{11,1... | collective-permute-start | bytes 73736 | tf_op jit(solution)/shard_map/ppermute | solution.py:130
  6.8 2.3 %copy-start.2 = (bf16[8,32,8,128]{3,2,1,0:T(8,128)(2,1)S(1)}, bf16[8,32,8,128]{3,2,1,0:T(8,128)(2,1)}, u32[]{:S(2)}) copy-start(bf16[8,32,8,128]{3,2,1,0:T(8,128)(2,1)} %param.8) | copy-start | bytes 1572868
  10.0 0.7 %copy-start.4 = (bf16[96,128]{1,0:T(8,128)(2,1)}, bf16[96,128]{1,0:T(8,128)(2,1)S(1)}, u32[]{:S(2)}) copy-start(bf16[96,128]{1,0:T(8,128)(2,1)S(1)} %collective-permute-done.refs_1_) | copy-start | bytes 73732
  10.8 0.6 %copy-start.5 = (bf16[96,128]{1,0:T(8,128)(2,1)}, bf16[96,128]{1,0:T(8,128)(2,1)S(1)}, u32[]{:S(2)}) copy-start(bf16[96,128]{1,0:T(8,128)(2,1)S(1)} %collective-permute-done.1.refs_2_) | copy-start | bytes 73732
  16.3 6.8 %copy-start.3 = (f32[32,8,128]{2,1,0:T(8,128)S(1)}, f32[32,8,128]{2,1,0:T(8,128)}, u32[]{:S(2)}) copy-start(f32[32,8,128]{2,1,0:T(8,128)} %get-tuple-element.32) | copy-start | bytes 393220
  16.3 5.9 %collective-permute-start.2 = (f32[96,128]{1,0:T(8,128)}, f32[96,128]{1,0:T(8,128)S(1)}, u32[]{:S(2)}, u32[]{:S(2)}) collective-permute-start(f32[96,128]{1,0:T(8,128)} %get-tuple-element.33), channel_id=1, source_target_pairs={{0,1},{1,2},{2,3},{3,4},{4,5},{5,6},{6,7},{7,8},{8,9},{9,10},{10,1... | collective-permute-start | bytes 147464 | tf_op jit(solution)/shard_map/ppermute | solution.py:148
  20.2 6.5 %collective-permute-start.3 = (f32[96,128]{1,0:T(8,128)}, f32[96,128]{1,0:T(8,128)S(1)}, u32[]{:S(2)}, u32[]{:S(2)}) collective-permute-start(f32[96,128]{1,0:T(8,128)} %get-tuple-element.34), channel_id=1, source_target_pairs={{1,0},{2,1},{3,2},{4,3},{5,4},{6,5},{7,6},{8,7},{9,8},{10,9},{11,1... | collective-permute-start | bytes 147464 | tf_op jit(solution)/shard_map/ppermute | solution.py:149
  26.7 0.9 %copy-start = (f32[32,8,128]{2,1,0:T(8,128)S(1)}, f32[32,8,128]{2,1,0:T(8,128)}, u32[]{:S(2)}) copy-start(f32[32,8,128]{2,1,0:T(8,128)} %refs_0_.1) | copy-start | bytes 393220

commit v8 on v5

--- a/solution.py
+++ b/solution.py
@@ -155,7 +155,8 @@
             pltpu.VMEM((reach_y, reach_x * planes, views * planes), jnp.bfloat16),
             pltpu.VMEM((views * planes, n_mid), jnp.bfloat16),
         ],
-    )(start, before, after, blur_b, corr_b, meas2, background)
+    )(*[pltpu.with_memory_space_constraint(x, pltpu.VMEM) for x in (start, before, after, blur_b, corr_b, meas2)],
+      background)
     return est
 
 

time: 20.9 us -> 19.4 us (0.928)
  waiting for transfers between devices: 3.08 us -> 5.08 us
  local copies, waits for them, and re-layouts: 4.09 us -> 2.53 us
  matrix products: 2.06 us -> 0.84 us
  Pallas kernels: 5.06 us -> 4.37 us
    ppermute x1, waiting for transfers between devices: 3.07 us -> 5.08 us  [local(): after = lax.ppermute(first, 'gy', [(i + 1, i) for i in range(peers - 1)])]
    unnamed x11 -> x7, local copies, waits for them, and re-layouts: 2.46 us -> 0.97 us
    pallas_call x1, Pallas kernels: 5.06 us -> 4.37 us  [local(): pl.pallas_call(lambda *refs: rl_kernel(*refs, cols=cols, reach_y=reach_y,...]
    dot_general x1, matrix products: 1.12 us -> 0.5 us  [build_bases(): jnp.einsum('vabc,val->bcl', kernel, onehot, precision=lax.Precision.HIGHEST)]
    dot_general x1, matrix products: 0.94 us -> 0.34 us  [build_bases(): jnp.einsum('vabc,acl->bvl', kernel, onehot, precision=lax.Precision.HIGHEST)]
  transfers between devices with their start and end apart: 2 -> 2, of which waited for: 1 -> 1; matrix products, arithmetic and copies ran while one was open for 17% -> 7% of each run, Pallas kernels for 0% -> 0%
where the time goes in v8:
time: 19.4 us; the launch traced here: 19.2 us
  starting transfers between devices  5.76 us (30%)
  waiting for transfers between devices  5.08 us (26%)
  Pallas kernels  4.37 us (23%)
  local copies, waits for them, and re-layouts  2.53 us (13%)
  matrix products  0.84 us (4%)
  other arithmetic  0.47 us (2%)
    ppermute x1, waiting for transfers between devices, local(): after = lax.ppermute(first, 'gy', [(i + 1, i) for i in range(peers - 1)])  5.08 us
    pallas_call x1, Pallas kernels, local(): pl.pallas_call(lambda *refs: rl_kernel(*refs, cols=cols, reach_y=reach_y,...  4.37 us
    ppermute x1, starting transfers between devices, local(): before = lax.ppermute(last, 'gy', [(i, i + 1) for i in range(peers - 1)])  3.71 us
    ppermute x1, starting transfers between devices, local(): after = lax.ppermute(first, 'gy', [(i + 1, i) for i in range(peers - 1)])  2.05 us
    transpose x3, local copies, waits for them, and re-layouts, meas_rows(): m = jnp.transpose(measured[:, :, lo:hi, :], (2, 0, 1, 3)).reshape(-1, cols)  1.51 us
    unnamed x7, local copies, waits for them, and re-layouts  0.97 us
    dot_general x1, matrix products, build_bases(): jnp.einsum('vabc,val->bcl', kernel, onehot, precision=lax.Precision.HIGHEST)  0.5 us
  transfers between devices with their start and end apart: 2, of which 1 were waited for; matrix products, arithmetic and copies ran while one was open for 7% of the time, Pallas kernels for 0%

profile of v8, /device:TPU:5, one launch (start us, length us, event | category | flops | bytes accessed | tf_op | source)
XLA Modules:
  0.0 19.2 jit_solution(3876147772547833229)
XLA Ops:
  0.0 1.5 %slice_bitcast_fusion = (bf16[3,8,32,128]{3,0,2,1:T(4,128)(2,1)S(1)}, bf16[3,8,32,128]{3,0,2,1:T(4,128)(2,1)S(1)}) fusion(bf16[8,32,8,128]{3,2,1,0:T(8,128)(2,1)} %param.4), kind=kLoop, calls=%fused_computation.6 | loop fusion | bytes 786432 | tf_op jit(solution)/shard_map/transpose | solution.py:137
  1.5 0.0 copy-start
  1.5 0.9 %copy-done = f32[32,8,128]{2,1,0:T(8,128)S(1)} copy-done((f32[32,8,128]{2,1,0:T(8,128)S(1)}, f32[32,8,128]{2,1,0:T(8,128)}, u32[]{:S(2)}) %copy-start) | copy-done | bytes 131096
  2.5 3.7 %collective-permute-start = (bf16[960,128]{1,0:T(8,128)(2,1)S(1)}, bf16[960,128]{1,0:T(8,128)(2,1)S(1)}, u32[]{:S(2)}, u32[]{:S(2)}) collective-permute-start(bf16[960,128]{1,0:T(8,128)(2,1)S(1)} %pad_maximum_fusion), channel_id=1, source_target_pairs={{0,1},{1,2},{2,3},{3,4},{4,5},{5,6},{6,7},{7,8},{8,9},{9,10},{10,1... | collective-permute-start | bytes 737288 | tf_op jit(solution)/shard_map/ppermute | solution.py:143
  6.2 0.0 copy-start.2
  6.3 0.0 copy-start.1
  6.3 2.1 %collective-permute-start.1 = (bf16[960,128]{1,0:T(8,128)(2,1)S(1)}, bf16[960,128]{1,0:T(8,128)(2,1)S(1)}, u32[]{:S(2)}, u32[]{:S(2)}) collective-permute-start(bf16[960,128]{1,0:T(8,128)(2,1)S(1)} %pad_maximum_fusion.1), channel_id=1, source_target_pairs={{1,0},{2,1},{3,2},{4,3},{5,4},{6,5},{7,6},{8,7},{9,8},{10,9},{11,1... | collective-permute-start | bytes 737288 | tf_op jit(solution)/shard_map/ppermute | solution.py:144
  8.4 0.0 copy-done.2
  8.4 0.2 reduce_sum.9
  8.5 0.1 broadcast_divide_fusion
  8.6 0.1 add_select_fusion.1
  8.7 0.3 %fusion.2.refs_3_ = bf16[7,8,256]{2,1,0:T(8,128)(2,1)S(1)} fusion(f32[8,15,7,7]{1,0,3,2:T(8,128)S(1)} %broadcast_divide_fusion, s32[15,7]{0,1:T(8,128)S(1)} %add_select_fusion.1), kind=kOutput, calls=%fused_computation.4 | convolution fusion | flops 18104576 | bytes 52612 | tf_op jit(solution)/shard_map/vabc,acl->bvl/dot_general | solution.py:18
  9.1 0.1 add_select_fusion
  9.1 0.0 copy-done.1
  9.1 0.1 copy.16
  9.2 0.5 %fusion.1.refs_4_ = bf16[7,7,256]{2,1,0:T(8,128)(2,1)S(1)} fusion(f32[8,15,7,7]{1,0,3,2:T(8,128)S(1)} %broadcast_divide_fusion, s32[8,15]{1,0:T(8,128)S(1)} %add_select_fusion), kind=kOutput, calls=%fused_computation.3 | convolution fusion | flops 18106624 | bytes 49088 | tf_op jit(solution)/shard_map/vabc,val->bcl/dot_general | solution.py:22
  9.7 0.0 collective-permute-done.refs_1_
  9.8 5.1 %collective-permute-done.1.refs_2_ = bf16[960,128]{1,0:T(8,128)(2,1)S(1)} collective-permute-done((bf16[960,128]{1,0:T(8,128)(2,1)S(1)}, bf16[960,128]{1,0:T(8,128)(2,1)S(1)}, u32[]{:S(2)}, u32[]{:S(2)}) %collective-permute-start.1) | collective-permute-done | bytes 245792 | tf_op jit(solution)/shard_map/ppermute | solution.py:144
  14.8 4.4 %shard_map.46 = f32[32,8,128]{2,1,0:T(8,128)} custom-call(f32[32,8,128]{2,1,0:T(8,128)S(1)} %copy-done, bf16[960,128]{1,0:T(8,128)(2,1)S(1)} %collective-permute-done.refs_1_, bf16[960,128]{1,0:T(8,128)(2,1)S(1)} %collective-permute-done.1.refs_2_, bf16[7,8,256]{2,1,0:T(8,128)(2,1)S(1)} %fusion.2.refs_3_, bf16[7,7,256]{2,1,0:T(8,128)(2,1)S(1)} %fusion.1.refs_4_, ...), custom_call_target="tpu_custom_call" | custom-call | tf_op jit(solution)/shard_map/pallas_call | solution.py:147
  (10 shorter events, 0.2 us)
Async XLA Ops:
  1.5 0.9 %copy-start = (f32[32,8,128]{2,1,0:T(8,128)S(1)}, f32[32,8,128]{2,1,0:T(8,128)}, u32[]{:S(2)}) copy-start(f32[32,8,128]{2,1,0:T(8,128)} %refs_0_.1) | copy-start | bytes 393220
  2.5 7.3 %collective-permute-start = (bf16[960,128]{1,0:T(8,128)(2,1)S(1)}, bf16[960,128]{1,0:T(8,128)(2,1)S(1)}, u32[]{:S(2)}, u32[]{:S(2)}) collective-permute-start(bf16[960,128]{1,0:T(8,128)(2,1)S(1)} %pad_maximum_fusion), channel_id=1, source_target_pairs={{0,1},{1,2},{2,3},{3,4},{4,5},{5,6},{6,7},{7,8},{8,9},{9,10},{10,1... | collective-permute-start | bytes 737288 | tf_op jit(solution)/shard_map/ppermute | solution.py:143
  6.2 2.1 %copy-start.2 = (f32[8,15,7,7]{1,0,3,2:T(8,128)S(1)}, f32[8,15,7,7]{1,0,3,2:T(8,128)}, u32[]{:S(2)}) copy-start(f32[8,15,7,7]{1,0,3,2:T(8,128)} %param.6) | copy-start | bytes 70564
  6.3 2.9 %copy-start.1 = (bf16[8,32,8,128]{3,2,1,0:T(8,128)(2,1)S(1)}, bf16[8,32,8,128]{3,2,1,0:T(8,128)(2,1)}, u32[]{:S(2)}) copy-start(bf16[8,32,8,128]{3,2,1,0:T(8,128)(2,1)} %param.4) | copy-start | bytes 1572868
  6.3 8.5 %collective-permute-start.1 = (bf16[960,128]{1,0:T(8,128)(2,1)S(1)}, bf16[960,128]{1,0:T(8,128)(2,1)S(1)}, u32[]{:S(2)}, u32[]{:S(2)}) collective-permute-start(bf16[960,128]{1,0:T(8,128)(2,1)S(1)} %pad_maximum_fusion.1), channel_id=1, source_target_pairs={{1,0},{2,1},{3,2},{4,3},{5,4},{6,5},{7,6},{8,7},{9,8},{10,9},{11,1... | collective-permute-start | bytes 737288 | tf_op jit(solution)/shard_map/ppermute | solution.py:144

commit v9 on v8

--- a/solution.py
+++ b/solution.py
@@ -126,15 +126,14 @@
     vmem = pl.BlockSpec(memory_space=pltpu.VMEM)
     smem = pl.BlockSpec(memory_space=pltpu.SMEM)
 
-    rounded = start.astype(jnp.bfloat16)
     meas2 = measured.reshape(views * planes, n_out)
 
     def slab(lo, hi):
-        r = jnp.transpose(rounded[:, lo:hi, :], (1, 0, 2)).reshape(-1, cols)
+        r = jnp.concatenate([start[:, i, :].astype(jnp.bfloat16) for i in range(lo, hi)], axis=0)
         return r
 
     def meas_rows(lo, hi):
-        m = jnp.transpose(measured[:, :, lo:hi, :], (2, 0, 1, 3)).reshape(-1, cols)
+        m = jnp.concatenate([measured[:, :, r, :].reshape(-1, cols) for r in range(lo, hi)], axis=0)
         return m
 
     last = jnp.concatenate([slab(rows - 2 * half, rows), meas_rows(rows - half, rows)], axis=0)

time: 19.4 us -> 20.1 us (1.036)
  the two profiles are of different devices: /device:TPU:5 before, /device:TPU:16 now
where the time goes in v9:
time: 20.1 us; the launch traced here: 19.9 us
  waiting for transfers between devices  5.08 us (25%)
  starting transfers between devices  4.81 us (24%)
  Pallas kernels  4.37 us (22%)
  local copies, waits for them, and re-layouts  4.22 us (21%)
  matrix products  0.83 us (4%)
  other arithmetic  0.42 us (2%)
    ppermute x1, waiting for transfers between devices, local(): before = lax.ppermute(last, 'gy', [(i, i + 1) for i in range(peers - 1)])  4.95 us
    pallas_call x1, Pallas kernels, local(): pl.pallas_call(lambda *refs: rl_kernel(*refs, cols=cols, reach_y=reach_y,...  4.37 us
    slice x1, local copies, waits for them, and re-layouts, meas_rows(): measured[:, :, r, :].reshape(-1, cols)  2.97 us
    ppermute x1, starting transfers between devices, local(): after = lax.ppermute(first, 'gy', [(i + 1, i) for i in range(peers - 1)])  2.75 us
    ppermute x1, starting transfers between devices, local(): before = lax.ppermute(last, 'gy', [(i, i + 1) for i in range(peers - 1)])  2.05 us
    unnamed x23, local copies, waits for them, and re-layouts  1.22 us
    dot_general x1, matrix products, build_bases(): jnp.einsum('vabc,val->bcl', kernel, onehot, precision=lax.Precision.HIGHEST)  0.49 us
  transfers between devices with their start and end apart: 2, of which 2 were waited for; matrix products, arithmetic and copies ran while one was open for 7% of the time, Pallas kernels for 0%

profile of v9, /device:TPU:16, one launch (start us, length us, event | category | flops | bytes accessed | tf_op | source)
XLA Modules:
  0.0 19.9 jit_solution(7140000807219679776)
XLA Ops:
  0.0 0.9 %copy.28 = bf16[32,8,128]{2,0,1:T(8,128)(2,1)S(1)} copy(f32[32,8,128]{2,1,0:T(8,128)} %refs_0_.1) | data formatting | bytes 196608 | tf_op args[1]
  0.9 3.0 %fusion.15 = (bf16[8,32,1,128]{3,2,1,0:T(2,128)(2,1)S(1)}, bf16[8,32,1,128]{3,2,1,0:T(2,128)(2,1)S(1)}, bf16[8,32,1,128]{3,2,1,0:T(2,128)(2,1)S(1)}, bf16[8,32,1...) fusion(bf16[8,32,8,128]{3,2,1,0:T(8,128)(2,1)} %param.4), kind=kLoop, calls=%fused_computation.54 | loop fusion | bytes 786432 | tf_op jit(solution)/shard_map/slice | solution.py:136
  4.1 2.8 %collective-permute-start.1 = (bf16[960,128]{1,0:T(8,128)(2,1)S(1)}, bf16[960,128]{1,0:T(8,128)(2,1)S(1)}, u32[]{:S(2)}, u32[]{:S(2)}) collective-permute-start(bf16[960,128]{1,0:T(8,128)(2,1)S(1)} %constant_dynamic-update-slice_fusion.9), channel_id=1, source_target_pairs={{1,0},{2,1},{3,2},{4,3},{5,4},{6,5},{7,6},{8,7},{9,8},{10,9},{11,1... | collective-permute-start | bytes 737288 | tf_op jit(solution)/shard_map/ppermute | solution.py:143
  6.9 0.0 copy-start.2
  7.0 0.0 copy-start.1
  7.0 2.1 %collective-permute-start = (bf16[960,128]{1,0:T(8,128)(2,1)S(1)}, bf16[960,128]{1,0:T(8,128)(2,1)S(1)}, u32[]{:S(2)}, u32[]{:S(2)}) collective-permute-start(bf16[960,128]{1,0:T(8,128)(2,1)S(1)} %constant_dynamic-update-slice_fusion), channel_id=1, source_target_pairs={{0,1},{1,2},{2,3},{3,4},{4,5},{5,6},{6,7},{7,8},{8,9},{9,10},{10,1... | collective-permute-start | bytes 737288 | tf_op jit(solution)/shard_map/ppermute | solution.py:142
  9.1 0.0 copy-done.2
  9.1 0.2 reduce_sum.9
  9.3 0.1 broadcast_divide_fusion
  9.4 0.1 add_select_fusion.1
  9.4 0.3 %fusion.2.refs_3_ = bf16[7,8,256]{2,1,0:T(8,128)(2,1)S(1)} fusion(f32[8,15,7,7]{1,0,3,2:T(8,128)S(1)} %broadcast_divide_fusion, s32[15,7]{0,1:T(8,128)S(1)} %add_select_fusion.1), kind=kOutput, calls=%fused_computation.4 | convolution fusion | flops 18104576 | bytes 52612 | tf_op jit(solution)/shard_map/vabc,acl->bvl/dot_general | solution.py:18
  9.8 0.1 add_select_fusion
  9.9 0.0 copy-done.1
  9.9 0.1 copy.29
  10.0 0.0 copy-start
  10.0 0.5 %fusion.1.refs_4_ = bf16[7,7,256]{2,1,0:T(8,128)(2,1)S(1)} fusion(f32[8,15,7,7]{1,0,3,2:T(8,128)S(1)} %broadcast_divide_fusion, s32[8,15]{1,0:T(8,128)S(1)} %add_select_fusion), kind=kOutput, calls=%fused_computation.3 | convolution fusion | flops 18106624 | bytes 49088 | tf_op jit(solution)/shard_map/vabc,val->bcl/dot_general | solution.py:22
  10.5 0.1 collective-permute-done.1.refs_2_
  10.6 5.0 %collective-permute-done.refs_1_ = bf16[960,128]{1,0:T(8,128)(2,1)S(1)} collective-permute-done((bf16[960,128]{1,0:T(8,128)(2,1)S(1)}, bf16[960,128]{1,0:T(8,128)(2,1)S(1)}, u32[]{:S(2)}, u32[]{:S(2)}) %collective-permute-start) | collective-permute-done | bytes 245792 | tf_op jit(solution)/shard_map/ppermute | solution.py:142
  15.6 0.0 copy-done
  15.6 4.4 %shard_map.46 = f32[32,8,128]{2,1,0:T(8,128)} custom-call(f32[32,8,128]{2,1,0:T(8,128)S(1)} %copy-done, bf16[960,128]{1,0:T(8,128)(2,1)S(1)} %collective-permute-done.refs_1_, bf16[960,128]{1,0:T(8,128)(2,1)S(1)} %collective-permute-done.1.refs_2_, bf16[7,8,256]{2,1,0:T(8,128)(2,1)S(1)} %fusion.2.refs_3_, bf16[7,7,256]{2,1,0:T(8,128)(2,1)S(1)} %fusion.1.refs_4_, ...), custom_call_target="tpu_custom_call" | custom-call | tf_op jit(solution)/shard_map/pallas_call | solution.py:146
  (19 shorter events, 0.2 us)
Async XLA Ops:
  4.1 6.5 %collective-permute-start.1 = (bf16[960,128]{1,0:T(8,128)(2,1)S(1)}, bf16[960,128]{1,0:T(8,128)(2,1)S(1)}, u32[]{:S(2)}, u32[]{:S(2)}) collective-permute-start(bf16[960,128]{1,0:T(8,128)(2,1)S(1)} %constant_dynamic-update-slice_fusion.9), channel_id=1, source_target_pairs={{1,0},{2,1},{3,2},{4,3},{5,4},{6,5},{7,6},{8,7},{9,8},{10,9},{11,1... | collective-permute-start | bytes 737288 | tf_op jit(solution)/shard_map/ppermute | solution.py:143
  6.9 2.2 %copy-start.2 = (f32[8,15,7,7]{1,0,3,2:T(8,128)S(1)}, f32[8,15,7,7]{1,0,3,2:T(8,128)}, u32[]{:S(2)}) copy-start(f32[8,15,7,7]{1,0,3,2:T(8,128)} %param.6) | copy-start | bytes 70564
  7.0 2.9 %copy-start.1 = (bf16[8,32,8,128]{3,2,1,0:T(8,128)(2,1)S(1)}, bf16[8,32,8,128]{3,2,1,0:T(8,128)(2,1)}, u32[]{:S(2)}) copy-start(bf16[8,32,8,128]{3,2,1,0:T(8,128)(2,1)} %param.4) | copy-start | bytes 1572868
  7.0 8.5 %collective-permute-start = (bf16[960,128]{1,0:T(8,128)(2,1)S(1)}, bf16[960,128]{1,0:T(8,128)(2,1)S(1)}, u32[]{:S(2)}, u32[]{:S(2)}) collective-permute-start(bf16[960,128]{1,0:T(8,128)(2,1)S(1)} %constant_dynamic-update-slice_fusion), channel_id=1, source_target_pairs={{0,1},{1,2},{2,3},{3,4},{4,5},{5,6},{6,7},{7,8},{8,9},{9,10},{10,1... | collective-permute-start | bytes 737288 | tf_op jit(solution)/shard_map/ppermute | solution.py:142
  10.0 5.6 %copy-start = (f32[32,8,128]{2,1,0:T(8,128)S(1)}, f32[32,8,128]{2,1,0:T(8,128)}, u32[]{:S(2)}) copy-start(f32[32,8,128]{2,1,0:T(8,128)} %refs_0_.1) | copy-start | bytes 393220

commit v10 on v8

--- a/solution.py
+++ b/solution.py
@@ -42,14 +42,9 @@
     return jnp.where(keep, rolled, jnp.zeros_like(rolled))
 
 
-def rl_kernel(start_ref, before_ref, after_ref, bbase_ref, cbase_ref, meas_ref, bg_ref, out_ref,
-              xs_ref, wb_ref, wc_ref, rext_ref, *, cols, reach_y, reach_x, half, half_z):
-    planes = start_ref.shape[0]
-    n_out = start_ref.shape[1] * cols
-    views = bbase_ref.shape[1]
-    hw = half * cols
-    n_mid = n_out + 2 * hw
-    width = reach_x * planes
+def weights_kernel(bbase_ref, cbase_ref, wb_ref, wc_ref, *, planes, half_z, width):
+    reach_y, views = bbase_ref.shape[0], bbase_ref.shape[1]
+    reach_x = cbase_ref.shape[1]
     for b in range(reach_y):
         for v in range(views):
             row = bbase_ref[b, v:v + 1, :].astype(jnp.float32)
@@ -57,6 +52,16 @@
         for c in range(reach_x):
             row = cbase_ref[b, c:c + 1, :].astype(jnp.float32)
             wc_ref[b, c * planes:(c + 1) * planes, :] = toeplitz_block(row, planes, half_z, views * planes)
+
+
+def rl_kernel(start_ref, before_ref, after_ref, wb_ref, wc_ref, meas_ref, bg_ref, out_ref,
+              xs_ref, rext_ref, *, cols, reach_y, reach_x, half, half_z):
+    planes = start_ref.shape[0]
+    n_out = start_ref.shape[1] * cols
+    views = meas_ref.shape[0] // planes
+    hw = half * cols
+    n_mid = n_out + 2 * hw
+    width = reach_x * planes
     rows = start_ref.shape[1]
     vp = views * planes
     m0 = 2 * half * planes
@@ -144,6 +149,15 @@
     after = lax.ppermute(first, "gy", [(i + 1, i) for i in range(peers - 1)])
 
     n_mid = n_out + 2 * hw
+    wb, wc = pl.pallas_call(
+        lambda *refs: weights_kernel(*refs, planes=planes, half_z=half_z, width=reach_x * planes),
+        out_shape=(
+            jax.ShapeDtypeStruct((reach_y, views * planes, lanes), jnp.bfloat16),
+            jax.ShapeDtypeStruct((reach_y, reach_x * planes, views * planes), jnp.bfloat16),
+        ),
+        in_specs=[vmem] * 2,
+        out_specs=(vmem, vmem),
+    )(*[pltpu.with_memory_space_constraint(x, pltpu.VMEM) for x in (blur_b, corr_b)])
     est = pl.pallas_call(
         lambda *refs: rl_kernel(*refs, cols=cols, reach_y=reach_y, reach_x=reach_x, half=half, half_z=half_z),
         out_shape=jax.ShapeDtypeStruct((planes, rows, cols), jnp.float32),
@@ -151,11 +165,9 @@
         out_specs=vmem,
         scratch_shapes=[
             pltpu.VMEM((lanes, n_out + 4 * hw), jnp.bfloat16),
-            pltpu.VMEM((reach_y, views * planes, lanes), jnp.bfloat16),
-            pltpu.VMEM((reach_y, reach_x * planes, views * planes), jnp.bfloat16),
             pltpu.VMEM((views * planes, n_mid), jnp.bfloat16),
         ],
-    )(*[pltpu.with_memory_space_constraint(x, pltpu.VMEM) for x in (start, before, after, blur_b, corr_b, meas2)],
+    )(*[pltpu.with_memory_space_constraint(x, pltpu.VMEM) for x in (start, before, after, wb, wc, meas2)],
       background)
     return est
 

time: 19.4 us -> 20.5 us (1.057)
  waiting for transfers between devices: 5.08 us -> 3.36 us
  Pallas kernels: 4.37 us -> 5.97 us
  other arithmetic: 0.47 us -> 1.43 us
  local copies, waits for them, and re-layouts: 2.53 us -> 2.79 us
    pallas_call x0 -> x1, Pallas kernels: none -> 1.73 us  [local(): pl.pallas_call(lambda *refs: weights_kernel(*refs, planes=planes, half_z=...]
    ppermute x1, waiting for transfers between devices: 5.08 us -> 3.35 us  [local(): after = lax.ppermute(first, 'gy', [(i + 1, i) for i in range(peers - 1)])]
    unnamed x7 -> x11, local copies, waits for them, and re-layouts: 0.97 us -> 2.51 us
    transpose x3, local copies, waits for them, and re-layouts: 1.51 us -> 0.23 us  [meas_rows(): m = jnp.transpose(measured[:, :, lo:hi, :], (2, 0, 1, 3)).reshape(-1, cols)]
    convert_element_type x1, other arithmetic: 0.01 us -> 0.97 us  [local(): rounded = start.astype(jnp.bfloat16)]
  transfers between devices with their start and end apart: 2 -> 2, of which waited for: 1 -> 1; matrix products, arithmetic and copies ran while one was open for 7% -> 7% of each run, Pallas kernels for 0% -> 9%
where the time goes in v10:
time: 20.5 us; the launch traced here: 20.3 us
  Pallas kernels  5.97 us (29%)
  starting transfers between devices  5.76 us (28%)
  waiting for transfers between devices  3.36 us (16%)
  local copies, waits for them, and re-layouts  2.79 us (14%)
  other arithmetic  1.43 us (7%)
  matrix products  0.84 us (4%)
    pallas_call x1, Pallas kernels, local(): pl.pallas_call(lambda *refs: rl_kernel(*refs, cols=cols, reach_y=reach_y,...  4.24 us
    ppermute x1, starting transfers between devices, local(): before = lax.ppermute(last, 'gy', [(i, i + 1) for i in range(peers - 1)])  3.71 us
    ppermute x1, waiting for transfers between devices, local(): after = lax.ppermute(first, 'gy', [(i + 1, i) for i in range(peers - 1)])  3.35 us
    unnamed x11, local copies, waits for them, and re-layouts  2.51 us
    ppermute x1, starting transfers between devices, local(): after = lax.ppermute(first, 'gy', [(i + 1, i) for i in range(peers - 1)])  2.05 us
    pallas_call x1, Pallas kernels, local(): pl.pallas_call(lambda *refs: weights_kernel(*refs, planes=planes, half_z=...  1.73 us
    convert_element_type x1, other arithmetic, local(): rounded = start.astype(jnp.bfloat16)  0.97 us
    dot_general x1, matrix products, build_bases(): jnp.einsum('vabc,val->bcl', kernel, onehot, precision=lax.Precision.HIGHEST)  0.5 us
  transfers between devices with their start and end apart: 2, of which 1 were waited for; matrix products, arithmetic and copies ran while one was open for 7% of the time, Pallas kernels for 9%

profile of v10, /device:TPU:5, one launch (start us, length us, event | category | flops | bytes accessed | tf_op | source)
XLA Modules:
  0.0 20.3 jit_solution(16308104338818915421)
XLA Ops:
  0.0 0.0 copy-start.3
  0.0 1.0 %convert_element_type.13 = bf16[32,8,128]{2,1,0:T(8,128)(2,1)S(1)} convert(f32[32,8,128]{2,1,0:T(8,128)} %refs_0_.1) | non-fusion elementwise | flops 32768 | bytes 196608 | tf_op jit(solution)/shard_map/convert_element_type | solution.py:134
  1.0 0.1 copy-done.3
  1.1 0.2 slice_bitcast_fusion
  1.3 3.7 %collective-permute-start = (bf16[960,128]{1,0:T(8,128)(2,1)S(1)}, bf16[960,128]{1,0:T(8,128)(2,1)S(1)}, u32[]{:S(2)}, u32[]{:S(2)}) collective-permute-start(bf16[960,128]{1,0:T(8,128)(2,1)S(1)} %pad_maximum_fusion), channel_id=1, source_target_pairs={{0,1},{1,2},{2,3},{3,4},{4,5},{5,6},{6,7},{7,8},{8,9},{9,10},{10,1... | collective-permute-start | bytes 737288 | tf_op jit(solution)/shard_map/ppermute | solution.py:148
  5.1 0.0 copy-start.4
  5.2 2.1 %collective-permute-start.1 = (bf16[960,128]{1,0:T(8,128)(2,1)S(1)}, bf16[960,128]{1,0:T(8,128)(2,1)S(1)}, u32[]{:S(2)}, u32[]{:S(2)}) collective-permute-start(bf16[960,128]{1,0:T(8,128)(2,1)S(1)} %pad_maximum_fusion.1), channel_id=1, source_target_pairs={{1,0},{2,1},{3,2},{4,3},{5,4},{6,5},{7,6},{8,7},{9,8},{10,9},{11,1... | collective-permute-start | bytes 737288 | tf_op jit(solution)/shard_map/ppermute | solution.py:149
  7.2 0.1 add_select_fusion.1
  7.3 0.0 copy-done.4
  7.3 0.2 reduce_sum.9
  7.5 0.1 broadcast_divide_fusion
  7.6 0.3 %fusion.2.refs_0_ = bf16[7,8,256]{2,1,0:T(8,128)(2,1)S(1)} fusion(f32[8,15,7,7]{1,0,3,2:T(8,128)S(1)} %broadcast_divide_fusion, s32[15,7]{0,1:T(8,128)S(1)} %add_select_fusion.1), kind=kOutput, calls=%fused_computation.4 | convolution fusion | flops 18104576 | bytes 52612 | tf_op jit(solution)/shard_map/vabc,acl->bvl/dot_general | solution.py:18
  7.9 0.1 add_select_fusion
  8.0 0.1 copy.16
  8.1 0.0 copy-start.2
  8.1 0.5 %fusion.1.refs_1_ = bf16[7,7,256]{2,1,0:T(8,128)(2,1)S(1)} fusion(f32[8,15,7,7]{1,0,3,2:T(8,128)S(1)} %broadcast_divide_fusion, s32[8,15]{1,0:T(8,128)S(1)} %add_select_fusion), kind=kOutput, calls=%fused_computation.3 | convolution fusion | flops 18106624 | bytes 49088 | tf_op jit(solution)/shard_map/vabc,val->bcl/dot_general | solution.py:22
  8.6 1.7 %shard_map.46 = (bf16[7,256,256]{2,1,0:T(8,128)(2,1)}, bf16[7,224,256]{2,1,0:T(8,128)(2,1)}) custom-call(bf16[7,8,256]{2,1,0:T(8,128)(2,1)S(1)} %fusion.2.refs_0_, bf16[7,7,256]{2,1,0:T(8,128)(2,1)S(1)} %fusion.1.refs_1_), custom_call_target="tpu_custom_call" | custom-call | tf_op jit(solution)/shard_map/pallas_call | solution.py:152
  10.3 0.0 collective-permute-done.refs_1_
  10.3 3.4 %collective-permute-done.1.refs_2_ = bf16[960,128]{1,0:T(8,128)(2,1)S(1)} collective-permute-done((bf16[960,128]{1,0:T(8,128)(2,1)S(1)}, bf16[960,128]{1,0:T(8,128)(2,1)S(1)}, u32[]{:S(2)}, u32[]{:S(2)}) %collective-permute-start.1) | collective-permute-done | bytes 245792 | tf_op jit(solution)/shard_map/ppermute | solution.py:149
  13.7 0.0 copy-done.2
  13.7 0.0 copy-start
  13.7 1.2 %copy-done = bf16[7,256,256]{2,1,0:T(8,128)(2,1)S(1)} copy-done((bf16[7,256,256]{2,1,0:T(8,128)(2,1)S(1)}, bf16[7,256,256]{2,1,0:T(8,128)(2,1)}, u32[]{:S(2)}) %copy-start) | copy-done | bytes 917528
  14.9 0.0 copy-start.1
  14.9 1.1 %copy-done.1 = bf16[7,224,256]{2,1,0:T(8,128)(2,1)S(1)} copy-done((bf16[7,224,256]{2,1,0:T(8,128)(2,1)S(1)}, bf16[7,224,256]{2,1,0:T(8,128)(2,1)}, u32[]{:S(2)}) %copy-start.1) | copy-done | bytes 802840
  16.0 4.2 %shard_map.47 = f32[32,8,128]{2,1,0:T(8,128)} custom-call(f32[32,8,128]{2,1,0:T(8,128)S(1)} %copy-done.2, bf16[960,128]{1,0:T(8,128)(2,1)S(1)} %collective-permute-done.refs_1_, bf16[960,128]{1,0:T(8,128)(2,1)S(1)} %collective-permute-done.1.refs_2_, bf16[7,256,256]{2,1,0:T(8,128)(2,1)S(1)} %copy-done, bf16[7,224,256]{2,1,0:T(8,128)(2,1)S(1)} %copy-done.1, ...), custom_call_target="tpu_custom_call" | custom-call | tf_op jit(solution)/shard_map/pallas_call | solution.py:161
  (9 shorter events, 0.2 us)
Async XLA Ops:
  0.0 1.1 %copy-start.3 = (bf16[8,32,8,128]{3,2,1,0:T(8,128)(2,1)S(1)}, bf16[8,32,8,128]{3,2,1,0:T(8,128)(2,1)}, u32[]{:S(2)}) copy-start(bf16[8,32,8,128]{3,2,1,0:T(8,128)(2,1)} %param.4) | copy-start | bytes 1572868
  1.3 9.0 %collective-permute-start = (bf16[960,128]{1,0:T(8,128)(2,1)S(1)}, bf16[960,128]{1,0:T(8,128)(2,1)S(1)}, u32[]{:S(2)}, u32[]{:S(2)}) collective-permute-start(bf16[960,128]{1,0:T(8,128)(2,1)S(1)} %pad_maximum_fusion), channel_id=1, source_target_pairs={{0,1},{1,2},{2,3},{3,4},{4,5},{5,6},{6,7},{7,8},{8,9},{9,10},{10,1... | collective-permute-start | bytes 737288 | tf_op jit(solution)/shard_map/ppermute | solution.py:148
  5.1 2.2 %copy-start.4 = (f32[8,15,7,7]{1,0,3,2:T(8,128)S(1)}, f32[8,15,7,7]{1,0,3,2:T(8,128)}, u32[]{:S(2)}) copy-start(f32[8,15,7,7]{1,0,3,2:T(8,128)} %param.6) | copy-start | bytes 70564
  5.2 8.5 %collective-permute-start.1 = (bf16[960,128]{1,0:T(8,128)(2,1)S(1)}, bf16[960,128]{1,0:T(8,128)(2,1)S(1)}, u32[]{:S(2)}, u32[]{:S(2)}) collective-permute-start(bf16[960,128]{1,0:T(8,128)(2,1)S(1)} %pad_maximum_fusion.1), channel_id=1, source_target_pairs={{1,0},{2,1},{3,2},{4,3},{5,4},{6,5},{7,6},{8,7},{9,8},{10,9},{11,1... | collective-permute-start | bytes 737288 | tf_op jit(solution)/shard_map/ppermute | solution.py:149
  8.1 5.6 %copy-start.2 = (f32[32,8,128]{2,1,0:T(8,128)S(1)}, f32[32,8,128]{2,1,0:T(8,128)}, u32[]{:S(2)}) copy-start(f32[32,8,128]{2,1,0:T(8,128)} %refs_0_.1) | copy-start | bytes 393220
  13.7 1.2 %copy-start = (bf16[7,256,256]{2,1,0:T(8,128)(2,1)S(1)}, bf16[7,256,256]{2,1,0:T(8,128)(2,1)}, u32[]{:S(2)}) copy-start(bf16[7,256,256]{2,1,0:T(8,128)(2,1)} %get-tuple-element.7.refs_3_) | copy-start | bytes 2752516
  14.9 1.1 %copy-start.1 = (bf16[7,224,256]{2,1,0:T(8,128)(2,1)S(1)}, bf16[7,224,256]{2,1,0:T(8,128)(2,1)}, u32[]{:S(2)}) copy-start(bf16[7,224,256]{2,1,0:T(8,128)(2,1)} %get-tuple-element.8.refs_4_) | copy-start | bytes 2408452

commit v11 on v10

--- a/solution.py
+++ b/solution.py
@@ -54,8 +54,12 @@
             wc_ref[b, c * planes:(c + 1) * planes, :] = toeplitz_block(row, planes, half_z, views * planes)
 
 
-def rl_kernel(start_ref, before_ref, after_ref, wb_ref, wc_ref, meas_ref, bg_ref, out_ref,
-              xs_ref, rext_ref, *, cols, reach_y, reach_x, half, half_z):
+def rl_kernel(start_ref, before_ref, after_ref, wb_hbm, wc_hbm, meas_ref, bg_ref, out_ref,
+              xs_ref, rext_ref, wb_ref, wc_ref, sems, *, cols, reach_y, reach_x, half, half_z):
+    copy_b = pltpu.make_async_copy(wb_hbm, wb_ref, sems.at[0])
+    copy_c = pltpu.make_async_copy(wc_hbm, wc_ref, sems.at[1])
+    copy_b.start()
+    copy_c.start()
     planes = start_ref.shape[0]
     n_out = start_ref.shape[1] * cols
     views = meas_ref.shape[0] // planes
@@ -88,6 +92,7 @@
         for c in range(reach_x):
             xs_ref[c * planes:(c + 1) * planes, e * cols:(e + 1) * cols] = (
                 lane_shift(slab, c - reach_x // 2, cols).astype(jnp.bfloat16))
+    copy_b.wait()
     step = 2 * cols
     for k in range(n_mid // step):
         acc = None
@@ -102,6 +107,7 @@
                 rs = slice(v * planes, (v + 1) * planes)
                 ratio = meas[rs].astype(jnp.float32) / (acc[rs, i * cols:(i + 1) * cols] + bg_ref[v])
                 rext_ref[rs, m * cols:(m + 1) * cols] = ratio.astype(jnp.bfloat16)
+    copy_c.wait()
     for k in range(n_out // step):
         acc = None
         for b in range(reach_y):
@@ -161,13 +167,17 @@
     est = pl.pallas_call(
         lambda *refs: rl_kernel(*refs, cols=cols, reach_y=reach_y, reach_x=reach_x, half=half, half_z=half_z),
         out_shape=jax.ShapeDtypeStruct((planes, rows, cols), jnp.float32),
-        in_specs=[vmem] * 6 + [smem],
+        in_specs=[vmem] * 3 + [pl.BlockSpec(memory_space=pl.ANY)] * 2 + [vmem, smem],
         out_specs=vmem,
         scratch_shapes=[
             pltpu.VMEM((lanes, n_out + 4 * hw), jnp.bfloat16),
             pltpu.VMEM((views * planes, n_mid), jnp.bfloat16),
+            pltpu.VMEM(wb.shape, jnp.bfloat16),
+            pltpu.VMEM(wc.shape, jnp.bfloat16),
+            pltpu.SemaphoreType.DMA((2,)),
         ],
-    )(*[pltpu.with_memory_space_constraint(x, pltpu.VMEM) for x in (start, before, after, wb, wc, meas2)],
+    )(*[pltpu.with_memory_space_constraint(x, pltpu.VMEM) for x in (start, before, after)], wb, wc,
+      pltpu.with_memory_space_constraint(meas2, pltpu.VMEM),
       background)
     return est
 

time: 20.5 us -> 20.2 us (0.985)
  local copies, waits for them, and re-layouts: 2.79 us -> 0.53 us
  Pallas kernels: 5.97 us -> 7.92 us
    unnamed x11 -> x7, local copies, waits for them, and re-layouts: 2.51 us -> 0.19 us
    pallas_call x1, Pallas kernels: 4.24 us -> 6.21 us  [local(): pl.pallas_call(lambda *refs: rl_kernel(*refs, cols=cols, reach_y=reach_y,...]
where the time goes in v11:
time: 20.2 us; the launch traced here: 20 us
  Pallas kernels  7.92 us (39%)
  starting transfers between devices  5.76 us (29%)
  waiting for transfers between devices  3.37 us (17%)
  other arithmetic  1.43 us (7%)
  matrix products  0.84 us (4%)
  local copies, waits for them, and re-layouts  0.53 us (3%)
    pallas_call x1, Pallas kernels, local(): pl.pallas_call(lambda *refs: rl_kernel(*refs, cols=cols, reach_y=reach_y,...  6.21 us
    ppermute x1, starting transfers between devices, local(): before = lax.ppermute(last, 'gy', [(i, i + 1) for i in range(peers - 1)])  3.71 us
    ppermute x1, waiting for transfers between devices, local(): after = lax.ppermute(first, 'gy', [(i + 1, i) for i in range(peers - 1)])  3.37 us
    ppermute x1, starting transfers between devices, local(): after = lax.ppermute(first, 'gy', [(i + 1, i) for i in range(peers - 1)])  2.05 us
    pallas_call x1, Pallas kernels, local(): pl.pallas_call(lambda *refs: weights_kernel(*refs, planes=planes, half_z=...  1.71 us
    convert_element_type x1, other arithmetic, local(): rounded = start.astype(jnp.bfloat16)  0.97 us
    dot_general x1, matrix products, build_bases(): jnp.einsum('vabc,val->bcl', kernel, onehot, precision=lax.Precision.HIGHEST)  0.5 us
  transfers between devices with their start and end apart: 2, of which 1 were waited for; matrix products, arithmetic and copies ran while one was open for 7% of the time, Pallas kernels for 9%

profile of v11, /device:TPU:5, one launch (start us, length us, event | category | flops | bytes accessed | tf_op | source)
XLA Modules:
  0.0 20.0 jit_solution(1880939668144807600)
XLA Ops:
  0.0 0.0 copy-start.1
  0.0 1.0 %convert_element_type.13 = bf16[32,8,128]{2,1,0:T(8,128)(2,1)S(1)} convert(f32[32,8,128]{2,1,0:T(8,128)} %refs_0_.1) | non-fusion elementwise | flops 32768 | bytes 196608 | tf_op jit(solution)/shard_map/convert_element_type | solution.py:140
  1.0 0.1 copy-done.1
  1.1 0.2 %slice_bitcast_fusion = (bf16[3,8,32,128]{3,0,2,1:T(4,128)(2,1)S(1)}, bf16[3,8,32,128]{3,0,2,1:T(4,128)(2,1)S(1)}) fusion(bf16[8,32,8,128]{3,2,1,0:T(8,128)(2,1)S(1)} %copy-done.1), kind=kLoop, calls=%fused_computation.6 | loop fusion | bytes 786432 | tf_op jit(solution)/shard_map/transpose | solution.py:148
  1.4 3.7 %collective-permute-start = (bf16[960,128]{1,0:T(8,128)(2,1)S(1)}, bf16[960,128]{1,0:T(8,128)(2,1)S(1)}, u32[]{:S(2)}, u32[]{:S(2)}) collective-permute-start(bf16[960,128]{1,0:T(8,128)(2,1)S(1)} %pad_maximum_fusion), channel_id=1, source_target_pairs={{0,1},{1,2},{2,3},{3,4},{4,5},{5,6},{6,7},{7,8},{8,9},{9,10},{10,1... | collective-permute-start | bytes 737288 | tf_op jit(solution)/shard_map/ppermute | solution.py:154
  5.2 0.0 copy-start.2
  5.2 2.1 %collective-permute-start.1 = (bf16[960,128]{1,0:T(8,128)(2,1)S(1)}, bf16[960,128]{1,0:T(8,128)(2,1)S(1)}, u32[]{:S(2)}, u32[]{:S(2)}) collective-permute-start(bf16[960,128]{1,0:T(8,128)(2,1)S(1)} %pad_maximum_fusion.1), channel_id=1, source_target_pairs={{1,0},{2,1},{3,2},{4,3},{5,4},{6,5},{7,6},{8,7},{9,8},{10,9},{11,1... | collective-permute-start | bytes 737288 | tf_op jit(solution)/shard_map/ppermute | solution.py:155
  7.3 0.1 add_select_fusion.1
  7.4 0.0 copy-done.2
  7.4 0.2 reduce_sum.9
  7.6 0.1 broadcast_divide_fusion
  7.6 0.3 %fusion.2.refs_0_ = bf16[7,8,256]{2,1,0:T(8,128)(2,1)S(1)} fusion(f32[8,15,7,7]{1,0,3,2:T(8,128)S(1)} %broadcast_divide_fusion, s32[15,7]{0,1:T(8,128)S(1)} %add_select_fusion.1), kind=kOutput, calls=%fused_computation.4 | convolution fusion | flops 18104576 | bytes 52612 | tf_op jit(solution)/shard_map/vabc,acl->bvl/dot_general | solution.py:18
  8.0 0.1 add_select_fusion
  8.1 0.1 copy.16
  8.2 0.0 copy-start
  8.2 0.5 %fusion.1.refs_1_ = bf16[7,7,256]{2,1,0:T(8,128)(2,1)S(1)} fusion(f32[8,15,7,7]{1,0,3,2:T(8,128)S(1)} %broadcast_divide_fusion, s32[8,15]{1,0:T(8,128)S(1)} %add_select_fusion), kind=kOutput, calls=%fused_computation.3 | convolution fusion | flops 18106624 | bytes 49088 | tf_op jit(solution)/shard_map/vabc,val->bcl/dot_general | solution.py:22
  8.7 1.7 %shard_map.46 = (bf16[7,256,256]{2,1,0:T(8,128)(2,1)}, bf16[7,224,256]{2,1,0:T(8,128)(2,1)}) custom-call(bf16[7,8,256]{2,1,0:T(8,128)(2,1)S(1)} %fusion.2.refs_0_, bf16[7,7,256]{2,1,0:T(8,128)(2,1)S(1)} %fusion.1.refs_1_), custom_call_target="tpu_custom_call" | custom-call | tf_op jit(solution)/shard_map/pallas_call | solution.py:158
  10.4 0.0 collective-permute-done.refs_1_
  10.4 3.4 %collective-permute-done.1.refs_2_ = bf16[960,128]{1,0:T(8,128)(2,1)S(1)} collective-permute-done((bf16[960,128]{1,0:T(8,128)(2,1)S(1)}, bf16[960,128]{1,0:T(8,128)(2,1)S(1)}, u32[]{:S(2)}, u32[]{:S(2)}) %collective-permute-start.1) | collective-permute-done | bytes 245792 | tf_op jit(solution)/shard_map/ppermute | solution.py:155
  13.8 0.0 copy-done
  13.8 6.2 %shard_map.47 = f32[32,8,128]{2,1,0:T(8,128)} custom-call(f32[32,8,128]{2,1,0:T(8,128)S(1)} %copy-done, bf16[960,128]{1,0:T(8,128)(2,1)S(1)} %collective-permute-done.refs_1_, bf16[960,128]{1,0:T(8,128)(2,1)S(1)} %collective-permute-done.1.refs_2_, bf16[7,256,256]{2,1,0:T(8,128)(2,1)} %get-tuple-element.7.refs_3_, ...), custom_call_target="tpu_custom_call" | custom-call | tf_op jit(solution)/shard_map/pallas_call | solution.py:167
  (9 shorter events, 0.2 us)
Async XLA Ops:
  0.0 1.1 %copy-start.1 = (bf16[8,32,8,128]{3,2,1,0:T(8,128)(2,1)S(1)}, bf16[8,32,8,128]{3,2,1,0:T(8,128)(2,1)}, u32[]{:S(2)}) copy-start(bf16[8,32,8,128]{3,2,1,0:T(8,128)(2,1)} %param.4) | copy-start | bytes 1572868
  1.4 9.0 %collective-permute-start = (bf16[960,128]{1,0:T(8,128)(2,1)S(1)}, bf16[960,128]{1,0:T(8,128)(2,1)S(1)}, u32[]{:S(2)}, u32[]{:S(2)}) collective-permute-start(bf16[960,128]{1,0:T(8,128)(2,1)S(1)} %pad_maximum_fusion), channel_id=1, source_target_pairs={{0,1},{1,2},{2,3},{3,4},{4,5},{5,6},{6,7},{7,8},{8,9},{9,10},{10,1... | collective-permute-start | bytes 737288 | tf_op jit(solution)/shard_map/ppermute | solution.py:154
  5.2 2.2 %copy-start.2 = (f32[8,15,7,7]{1,0,3,2:T(8,128)S(1)}, f32[8,15,7,7]{1,0,3,2:T(8,128)}, u32[]{:S(2)}) copy-start(f32[8,15,7,7]{1,0,3,2:T(8,128)} %param.6) | copy-start | bytes 70564
  5.2 8.5 %collective-permute-start.1 = (bf16[960,128]{1,0:T(8,128)(2,1)S(1)}, bf16[960,128]{1,0:T(8,128)(2,1)S(1)}, u32[]{:S(2)}, u32[]{:S(2)}) collective-permute-start(bf16[960,128]{1,0:T(8,128)(2,1)S(1)} %pad_maximum_fusion.1), channel_id=1, source_target_pairs={{1,0},{2,1},{3,2},{4,3},{5,4},{6,5},{7,6},{8,7},{9,8},{10,9},{11,1... | collective-permute-start | bytes 737288 | tf_op jit(solution)/shard_map/ppermute | solution.py:155
  8.2 5.6 %copy-start = (f32[32,8,128]{2,1,0:T(8,128)S(1)}, f32[32,8,128]{2,1,0:T(8,128)}, u32[]{:S(2)}) copy-start(f32[32,8,128]{2,1,0:T(8,128)} %refs_0_.1) | copy-start | bytes 393220

commit v12 on v8

--- a/solution.py
+++ b/solution.py
@@ -31,7 +31,7 @@
     l = lax.broadcasted_iota(jnp.int32, (planes, lanes), 1)
     d = l % planes - q
     keep = (d <= half_z) & (d >= -half_z) & (l < width)
-    return jnp.where(keep, blk, 0.0).astype(jnp.bfloat16)
+    return jnp.where(keep, blk, jnp.zeros_like(blk))
 
 
 def lane_shift(x, shift, cols):
@@ -52,10 +52,10 @@
     width = reach_x * planes
     for b in range(reach_y):
         for v in range(views):
-            row = bbase_ref[b, v:v + 1, :].astype(jnp.float32)
+            row = bbase_ref[b, v:v + 1, :]
             wb_ref[b, v * planes:(v + 1) * planes, :] = toeplitz_block(row, planes, half_z, width)
         for c in range(reach_x):
-            row = cbase_ref[b, c:c + 1, :].astype(jnp.float32)
+            row = cbase_ref[b, c:c + 1, :]
             wc_ref[b, c * planes:(c + 1) * planes, :] = toeplitz_block(row, planes, half_z, views * planes)
     rows = start_ref.shape[1]
     vp = views * planes
@@ -63,11 +63,11 @@
 
     def rounded_slab(e):
         if e < 2 * half:
-            return before_ref[e * planes:(e + 1) * planes, :].astype(jnp.float32)
+            return before_ref[e * planes:(e + 1) * planes, :]
         if e >= 2 * half + rows:
             j = e - 2 * half - rows
-            return after_ref[j * planes:(j + 1) * planes, :].astype(jnp.float32)
-        return start_ref[:, e - 2 * half, :].astype(jnp.bfloat16).astype(jnp.float32)
+            return after_ref[j * planes:(j + 1) * planes, :]
+        return start_ref[:, e - 2 * half, :].astype(jnp.bfloat16)
 
     def measured_slab(m):
         if m < half:
@@ -81,8 +81,7 @@
     for e in range(rows + 4 * half):
         slab = rounded_slab(e)
         for c in range(reach_x):
-            xs_ref[c * planes:(c + 1) * planes, e * cols:(e + 1) * cols] = (
-                lane_shift(slab, c - reach_x // 2, cols).astype(jnp.bfloat16))
+            xs_ref[c * planes:(c + 1) * planes, e * cols:(e + 1) * cols] = lane_shift(slab, c - reach_x // 2, cols)
     step = 2 * cols
     for k in range(n_mid // step):
         acc = None

time: 19.4 us -> 19.4 us (level)
  no operation moved by 1% of the time
where the time goes in v12:
time: 19.4 us; the launch traced here: 19.2 us
  starting transfers between devices  5.76 us (30%)
  waiting for transfers between devices  5.08 us (26%)
  Pallas kernels  4.33 us (22%)
  local copies, waits for them, and re-layouts  2.53 us (13%)
  matrix products  0.84 us (4%)
  other arithmetic  0.47 us (2%)
    ppermute x1, waiting for transfers between devices, local(): after = lax.ppermute(first, 'gy', [(i + 1, i) for i in range(peers - 1)])  5.08 us
    pallas_call x1, Pallas kernels, local(): pl.pallas_call(lambda *refs: rl_kernel(*refs, cols=cols, reach_y=reach_y,...  4.33 us
    ppermute x1, starting transfers between devices, local(): before = lax.ppermute(last, 'gy', [(i, i + 1) for i in range(peers - 1)])  3.71 us
    ppermute x1, starting transfers between devices, local(): after = lax.ppermute(first, 'gy', [(i + 1, i) for i in range(peers - 1)])  2.05 us
    transpose x3, local copies, waits for them, and re-layouts, meas_rows(): m = jnp.transpose(measured[:, :, lo:hi, :], (2, 0, 1, 3)).reshape(-1, cols)  1.51 us
    unnamed x7, local copies, waits for them, and re-layouts  0.97 us
    dot_general x1, matrix products, build_bases(): jnp.einsum('vabc,val->bcl', kernel, onehot, precision=lax.Precision.HIGHEST)  0.5 us
  transfers between devices with their start and end apart: 2, of which 1 were waited for; matrix products, arithmetic and copies ran while one was open for 7% of the time, Pallas kernels for 0%

profile of v12, /device:TPU:5, one launch (start us, length us, event | category | flops | bytes accessed | tf_op | source)
XLA Modules:
  0.0 19.2 jit_solution(2944246779142804953)
XLA Ops:
  0.0 1.5 %slice_bitcast_fusion = (bf16[3,8,32,128]{3,0,2,1:T(4,128)(2,1)S(1)}, bf16[3,8,32,128]{3,0,2,1:T(4,128)(2,1)S(1)}) fusion(bf16[8,32,8,128]{3,2,1,0:T(8,128)(2,1)} %param.4), kind=kLoop, calls=%fused_computation.6 | loop fusion | bytes 786432 | tf_op jit(solution)/shard_map/transpose | solution.py:136
  1.5 0.0 copy-start
  1.5 0.9 %copy-done = f32[32,8,128]{2,1,0:T(8,128)S(1)} copy-done((f32[32,8,128]{2,1,0:T(8,128)S(1)}, f32[32,8,128]{2,1,0:T(8,128)}, u32[]{:S(2)}) %copy-start) | copy-done | bytes 131096
  2.5 3.7 %collective-permute-start = (bf16[960,128]{1,0:T(8,128)(2,1)S(1)}, bf16[960,128]{1,0:T(8,128)(2,1)S(1)}, u32[]{:S(2)}, u32[]{:S(2)}) collective-permute-start(bf16[960,128]{1,0:T(8,128)(2,1)S(1)} %pad_maximum_fusion), channel_id=1, source_target_pairs={{0,1},{1,2},{2,3},{3,4},{4,5},{5,6},{6,7},{7,8},{8,9},{9,10},{10,1... | collective-permute-start | bytes 737288 | tf_op jit(solution)/shard_map/ppermute | solution.py:142
  6.2 0.0 copy-start.2
  6.3 0.0 copy-start.1
  6.3 2.1 %collective-permute-start.1 = (bf16[960,128]{1,0:T(8,128)(2,1)S(1)}, bf16[960,128]{1,0:T(8,128)(2,1)S(1)}, u32[]{:S(2)}, u32[]{:S(2)}) collective-permute-start(bf16[960,128]{1,0:T(8,128)(2,1)S(1)} %pad_maximum_fusion.1), channel_id=1, source_target_pairs={{1,0},{2,1},{3,2},{4,3},{5,4},{6,5},{7,6},{8,7},{9,8},{10,9},{11,1... | collective-permute-start | bytes 737288 | tf_op jit(solution)/shard_map/ppermute | solution.py:143
  8.4 0.0 copy-done.2
  8.4 0.2 reduce_sum.9
  8.5 0.1 broadcast_divide_fusion
  8.6 0.1 add_select_fusion.1
  8.7 0.3 %fusion.2.refs_3_ = bf16[7,8,256]{2,1,0:T(8,128)(2,1)S(1)} fusion(f32[8,15,7,7]{1,0,3,2:T(8,128)S(1)} %broadcast_divide_fusion, s32[15,7]{0,1:T(8,128)S(1)} %add_select_fusion.1), kind=kOutput, calls=%fused_computation.4 | convolution fusion | flops 18104576 | bytes 52612 | tf_op jit(solution)/shard_map/vabc,acl->bvl/dot_general | solution.py:18
  9.1 0.1 add_select_fusion
  9.1 0.0 copy-done.1
  9.1 0.1 copy.16
  9.2 0.5 %fusion.1.refs_4_ = bf16[7,7,256]{2,1,0:T(8,128)(2,1)S(1)} fusion(f32[8,15,7,7]{1,0,3,2:T(8,128)S(1)} %broadcast_divide_fusion, s32[8,15]{1,0:T(8,128)S(1)} %add_select_fusion), kind=kOutput, calls=%fused_computation.3 | convolution fusion | flops 18106624 | bytes 49088 | tf_op jit(solution)/shard_map/vabc,val->bcl/dot_general | solution.py:22
  9.7 0.0 collective-permute-done.refs_1_
  9.8 5.1 %collective-permute-done.1.refs_2_ = bf16[960,128]{1,0:T(8,128)(2,1)S(1)} collective-permute-done((bf16[960,128]{1,0:T(8,128)(2,1)S(1)}, bf16[960,128]{1,0:T(8,128)(2,1)S(1)}, u32[]{:S(2)}, u32[]{:S(2)}) %collective-permute-start.1) | collective-permute-done | bytes 245792 | tf_op jit(solution)/shard_map/ppermute | solution.py:143
  14.8 4.3 %shard_map.46 = f32[32,8,128]{2,1,0:T(8,128)} custom-call(f32[32,8,128]{2,1,0:T(8,128)S(1)} %copy-done, bf16[960,128]{1,0:T(8,128)(2,1)S(1)} %collective-permute-done.refs_1_, bf16[960,128]{1,0:T(8,128)(2,1)S(1)} %collective-permute-done.1.refs_2_, bf16[7,8,256]{2,1,0:T(8,128)(2,1)S(1)} %fusion.2.refs_3_, bf16[7,7,256]{2,1,0:T(8,128)(2,1)S(1)} %fusion.1.refs_4_, ...), custom_call_target="tpu_custom_call" | custom-call | tf_op jit(solution)/shard_map/pallas_call | solution.py:146
  (10 shorter events, 0.2 us)
Async XLA Ops:
  1.5 0.9 %copy-start = (f32[32,8,128]{2,1,0:T(8,128)S(1)}, f32[32,8,128]{2,1,0:T(8,128)}, u32[]{:S(2)}) copy-start(f32[32,8,128]{2,1,0:T(8,128)} %refs_0_.1) | copy-start | bytes 393220
  2.5 7.3 %collective-permute-start = (bf16[960,128]{1,0:T(8,128)(2,1)S(1)}, bf16[960,128]{1,0:T(8,128)(2,1)S(1)}, u32[]{:S(2)}, u32[]{:S(2)}) collective-permute-start(bf16[960,128]{1,0:T(8,128)(2,1)S(1)} %pad_maximum_fusion), channel_id=1, source_target_pairs={{0,1},{1,2},{2,3},{3,4},{4,5},{5,6},{6,7},{7,8},{8,9},{9,10},{10,1... | collective-permute-start | bytes 737288 | tf_op jit(solution)/shard_map/ppermute | solution.py:142
  6.2 2.1 %copy-start.2 = (f32[8,15,7,7]{1,0,3,2:T(8,128)S(1)}, f32[8,15,7,7]{1,0,3,2:T(8,128)}, u32[]{:S(2)}) copy-start(f32[8,15,7,7]{1,0,3,2:T(8,128)} %param.6) | copy-start | bytes 70564
  6.3 2.9 %copy-start.1 = (bf16[8,32,8,128]{3,2,1,0:T(8,128)(2,1)S(1)}, bf16[8,32,8,128]{3,2,1,0:T(8,128)(2,1)}, u32[]{:S(2)}) copy-start(bf16[8,32,8,128]{3,2,1,0:T(8,128)(2,1)} %param.4) | copy-start | bytes 1572868
  6.3 8.5 %collective-permute-start.1 = (bf16[960,128]{1,0:T(8,128)(2,1)S(1)}, bf16[960,128]{1,0:T(8,128)(2,1)S(1)}, u32[]{:S(2)}, u32[]{:S(2)}) collective-permute-start(bf16[960,128]{1,0:T(8,128)(2,1)S(1)} %pad_maximum_fusion.1), channel_id=1, source_target_pairs={{1,0},{2,1},{3,2},{4,3},{5,4},{6,5},{7,6},{8,7},{9,8},{10,9},{11,1... | collective-permute-start | bytes 737288 | tf_op jit(solution)/shard_map/ppermute | solution.py:143
